TPU v7x, 128 devices: a whole 4x4x4 slice. The times are simulated.
128 devices in a mesh: gx: 8 (over y_hi, z), gy: 16 (over x, y_lo, core).
Axes of the slice: x: 4, y: 4 (y_hi: 2, y_lo: 2; y = y_hi * 2 + y_lo), z: 4, core: 2. Of those that a mesh axis runs over, the one named last changes fastest.
Arguments:
- observed: float32 [2, 8192, 8192], P(None, 'gx', 'gy'), may hold values from -6 to 6
- noise_var: float32 [8192, 8192], P('gx', 'gy'), may hold values from 0.05 to 0.5
- row_kernel: float32 [4096, 4096], P('gx'), may hold values from -1 to 1.2, as said below
- col_kernel: float32 [4096, 4096], P('gy'), may hold values from -1 to 1.2, as said below
Outputs:
- gram_times: float32 [2, 8192, 8192], P(None, 'gx', 'gy')
Inputs may be any that keep to these rules, and one draw needn't show every extreme that they name: row_kernel is symmetric. col_kernel is symmetric.
All inputs are finite; a program needn't handle non-finite values.
Results may differ from a plain program's by a relative error of at most 0.000065.
Values sent between devices are 32-bit elements; how exact they have to be, the bound alone decides.
No kernel may reach another device: no remote copies, remote signals or barrier semaphores. Data moves between devices by JAX's collectives and lax.ppermute only.
A program may use at most 128 MiB of HBM per device.

v0:
```python
import jax
import jax.numpy as jnp
from jax import lax
from jax.sharding import Mesh, PartitionSpec as P


def axis_count(axis):
    return lax.psum(1, axis)


def with_halo(cells, sides, width):
    for axis, dim in sides:
        count = axis_count(axis)
        ends = count - 1
        head = lax.slice_in_dim(cells, 0, width, axis=dim)
        tail = lax.slice_in_dim(cells, cells.shape[dim] - width, cells.shape[dim], axis=dim)
        cells = jnp.concatenate(
            [
                lax.ppermute(tail, axis, [(i, (i + 1) % count) for i in range(ends)]),
                cells,
                lax.ppermute(head, axis, [((i + 1) % count, i) for i in range(ends)]),
            ],
            axis=dim,
        )
    return cells


def edges(cells, axis, dim, width):
    count = axis_count(axis)
    ends = count - 1
    head = lax.slice_in_dim(cells, 0, width, axis=dim)
    tail = lax.slice_in_dim(cells, cells.shape[dim] - width, cells.shape[dim], axis=dim)
    before = lax.ppermute(tail, axis, [(i, i + 1) for i in range(ends)])
    after = lax.ppermute(head, axis, [(i + 1, i) for i in range(ends)])
    return before, after


def keys_weight(dist):
    span = jnp.abs(dist)
    inner = (1.5 * span - 2.5) * span * span + 1.0
    outer = ((-0.5 * span + 2.5) * span - 4.0) * span + 2.0
    return jnp.where(span < 1.0, inner, jnp.where(span < 2.0, outer, 0.0))


def tap_table(rows, cols, coarse_on_rows, pad):
    r = lax.broadcasted_iota(jnp.float32, (rows, cols), 0)
    c = lax.broadcasted_iota(jnp.float32, (rows, cols), 1)
    if coarse_on_rows:
        coarse, fine = r, c
    else:
        coarse, fine = c, r
    if pad == 4:
        dist = coarse - ((fine - 4.0) * 0.5 + 0.25)
    else:
        dist = coarse - 2.0 - (fine * 0.5 + 0.25)
    return keys_weight(dist).astype(jnp.bfloat16)


def split3(x):
    hi = lax.reduce_precision(x, exponent_bits=8, mantissa_bits=7)
    rest = x - hi
    mid = lax.reduce_precision(rest, exponent_bits=8, mantissa_bits=7)
    lo = rest - mid
    return hi.astype(jnp.bfloat16), mid.astype(jnp.bfloat16), lo.astype(jnp.bfloat16)


def exact_dot(eq, x, table, data_first):
    ins, out = eq.split("->")
    first, second = ins.split(",")
    parts = jnp.stack(split3(x))
    if data_first:
        terms = jnp.einsum(f"s{first},{second}->s{out}", parts, table, preferred_element_type=jnp.float32)
    else:
        terms = jnp.einsum(f"{first},s{second}->s{out}", table, parts, preferred_element_type=jnp.float32)
    return terms[0] + terms[1] + terms[2]


def row_windows(kernel, count, block, width):
    padded = jnp.pad(kernel, ((0, width - kernel.shape[0]), (2, width - block - 2)))
    return jnp.concatenate([padded[:, block * w : block * w + width] for w in range(count)], axis=1)


def body(observed, noise_var, row_kernel, col_kernel):
    highest = lax.Precision.HIGH
    rows_axis = ("yh", "z")
    cols_axis = ("x", "yl", "core")
    tile_rows = row_kernel.shape[0]
    tile_cols = col_kernel.shape[0]
    ext_rows = tile_rows + 8
    row_count = axis_count(rows_axis)
    swap = [(0, 1), (1, 0)]
    side = lax.axis_index("yl")
    span = 4 * tile_cols
    quarters = range(col_kernel.shape[1] // span)
    low = jnp.concatenate([col_kernel[:, q * span : q * span + span // 2] for q in quarters], axis=1)
    high = jnp.concatenate([col_kernel[:, q * span + span // 2 : (q + 1) * span] for q in quarters], axis=1)
    near_cols = jnp.where(side == 0, low, high)
    far_cols = jnp.where(side == 0, high, low)
    partner_cols = lax.ppermute(far_cols, "yl", swap)
    row_rows = with_halo(row_kernel, ((rows_axis, 0),), 2)
    row_big = row_windows(row_rows, row_count, tile_rows, ext_rows)
    before, after = edges(observed, cols_axis, 2, 4)
    col_adj = tap_table(2 * tile_cols + 8, tile_cols, False, 4)
    row_adj = tap_table(ext_rows, 2 * tile_rows, True, 2)
    colsum = (
        exact_dot("rpq,qj->rpj", observed, col_adj[4:-4], True)
        + exact_dot("rpq,qj->rpj", before, col_adj[:4], True)
        + exact_dot("rpq,qj->rpj", after, col_adj[-4:], True)
    )
    inducing = exact_dot("ip,rpj->rij", colsum, row_adj, False)
    half = lax.all_gather(inducing, ("x", "core"), axis=2, tiled=True)
    near = jnp.einsum("rik,jk->rij", half, near_cols, precision=highest)
    for_partner = jnp.einsum("rik,jk->rij", half, partner_cols, precision=highest)
    mixed = near + lax.ppermute(for_partner, "yl", swap)
    product = jnp.einsum(
        "ik,rkj->rij", row_big, lax.all_gather(mixed, rows_axis, axis=1, tiled=True), precision=highest
    )
    coarse_ext = with_halo(product, ((cols_axis, 2),), 2)
    row_fwd = tap_table(2 * tile_rows, ext_rows, False, 2)
    col_fwd = tap_table(tile_cols + 4, 2 * tile_cols, True, 2)
    rowpass = exact_dot("pi,rij->rpj", coarse_ext, row_fwd, False)
    result = exact_dot("rpj,jq->rpq", rowpass, col_fwd, True)
    return result + noise_var[None] * observed


def solution(mesh):
    rows_n, cols_n = mesh.devices.shape
    z = min(4, rows_n)
    shape = (rows_n // z, z, cols_n // 4, 2, 2)
    fine = Mesh(mesh.devices.reshape(shape), ("yh", "z", "x", "yl", "core"))
    rows = ("yh", "z")
    cols = ("x", "yl", "core")
    return jax.shard_map(
        body,
        mesh=fine,
        in_specs=(P(None, rows, cols), P(rows, cols), P(rows, None), P(cols, None)),
        out_specs=P(None, rows, cols),
        check_vma=False,
    )
```

profile of v0, /device:TPU:1, one launch (start us, length us, event | category | flops | bytes accessed | tf_op | source)
XLA Modules:
  0.0 274.7 jit_solution(1124713238582573614)
XLA Ops:
  6.5 0.0 all-gather.6.cloned.1.call-start
  6.5 1.9 fusion.161
  8.4 0.3 copy.22
  8.8 4.6 %collective-permute-start = (f32[2,1024,4]{1,2,0:T(4,128)S(1)}, f32[2,1024,4]{1,2,0:T(4,128)S(1)}, u32[]{:S(2)}, u32[]{:S(2)}) collective-permute-start(f32[2,1024,4]{1,2,0:T(4,128)S(1)} %copy.22), channel_id=1, source_target_pairs={{0,1},{1,2},{2,3},{3,4},{4,5},{5,6},{6,7},{7,8},{8,9},{9,10},{10,1... | collective-permute-start | bytes 98312 | tf_op jit(solution)/shard_map/ppermute | solution.py:33
  13.4 0.3 copy.23
  13.7 1.9 collective-permute-start.1
  15.6 3.2 %fusion.47 = (bf16[1,2,1024,512]{3,2,1,0:T(8,128)(2,1)S(1)}, bf16[1,2,1024,512]{3,2,1,0:T(8,128)(2,1)S(1)}, bf16[1,2,1024,512]{3,2,1,0:T(8,128)(2,1)S(1)}) fusion(f32[2,1024,512]{2,1,0:T(8,128)} %param.4), kind=kLoop, calls=%fused_computation.77 | loop fusion | flops 7340032 | bytes 10485760 | tf_op jit(solution)/shard_map/stack | solution.py:70
  18.9 0.4 fusion.91
  19.2 1.8 fusion.8
  21.1 0.0 collective-permute-done
  21.1 1.0 fusion.106
  22.2 0.0 collective-permute-done.1
  22.2 1.0 fusion.112
  23.2 1.3 reduce-precision_convert_fusion.5
  24.5 0.4 reduce-precision_convert_fusion.4
  24.9 2.3 fusion.54
  27.2 1.2 slice_add_fusion.10
  28.4 0.0 all-gather.6.cloned.1.call-update
  28.4 0.0 all-gather.4.cloned.1.call-start
  28.5 2.6 fusion.160
  31.1 0.0 copy-start.2
  31.1 0.0 copy-start.4
  31.1 0.3 fusion.58
  31.4 0.5 copy-done.2
  31.9 0.1 copy-done.4
  32.1 1.1 collective-permute-start.2
  33.2 46.1 %collective-permute-done.2 = f32[256,2048]{1,0:T(8,128)} collective-permute-done((f32[256,2048]{1,0:T(8,128)S(1)}, f32[256,2048]{1,0:T(8,128)}, u32[]{:S(2)}, u32[]{:S(2)}) %collective-permute-start.2) | collective-permute-done | bytes 2097184 | tf_op jit(solution)/shard_map/ppermute | solution.py:99
  79.3 3.0 %all-gather.6.cloned.1.call-done = f32[1,2,520,2048]{3,2,1,0:T(8,128)} async-done(((f32[1,2,520,256]{3,2,1,0:T(8,128)}), f32[1,2,520,2048]{3,2,1,0:T(8,128)}) %all-gather.6.cloned.1.call-update) | async-done | bytes 8519696 | tf_op jit(solution)/shard_map/all_gather | solution.py:111
  82.4 6.9 %fusion.4 = f32[2,520,256]{2,1,0:T(8,128)S(1)} fusion(f32[1,2,520,2048]{3,2,1,0:T(8,128)} %all-gather.6.cloned.1.call-done, f32[256,2048]{1,0:T(8,128)} %collective-permute-done.2), kind=kOutput, calls=%fused_computation.9 | convolution fusion | flops 3271557120 | bytes 11681792 | tf_op jit(solution)/shard_map/rik,jk->rij/dot_general | solution.py:113
  89.3 1.3 collective-permute-start.3
  90.6 0.0 copy-done
  90.6 0.0 copy-done.5
  90.6 3.5 %fusion.6 = f32[2,520,256]{2,1,0:T(8,128)S(1)} fusion(f32[1,2,520,2048]{3,2,1,0:T(8,128)S(1)} %copy-done, f32[256,512]{1,0:T(8,128)S(1)} %copy-done.3, f32[256,512]{1,0:T(8,128)S(1)} %copy-done.5, f32[256,512]{1,0:T(8,128)S(1)} %get-tuple-element.20, f32[256,512]{1,0:T(8,128)S(1)} %get-tuple-element.21, f32[256,512]{1,0:T(8,128)S(1)} %get-tuple-element.22, ...), kind=kOutput, calls=%fused_computation.11 | convolution fusion | flops 3275227136 | bytes 13778945 | tf_op jit(solution)/shard_map/rik,jk->rij/dot_general | solution.py:112
  94.2 20.1 %collective-permute-done.3 = f32[2,520,256]{2,1,0:T(8,128)S(1)} collective-permute-done((f32[2,520,256]{2,1,0:T(8,128)S(1)}, f32[2,520,256]{2,1,0:T(8,128)S(1)}, u32[]{:S(2)}, u32[]{:S(2)}) %collective-permute-start.3) | collective-permute-done | bytes 1064992 | tf_op jit(solution)/shard_map/ppermute | solution.py:114
  114.2 1.1 add.203
  115.4 0.0 all-gather.4.cloned.1.call-update
  115.4 1.0 fusion.159
  116.4 3.2 %collective-permute-start.4 = (f32[2,4096]{1,0:T(2,128)S(1)}, f32[2,4096]{1,0:T(2,128)S(1)}, u32[]{:S(2)}, u32[]{:S(2)}) collective-permute-start(f32[2,4096]{1,0:T(2,128)S(1)} %get-tuple-element.17), channel_id=1, source_target_pairs={{0,16},{16,32},{32,48},{48,64},{64,80},{80,96},{96,112},{1,17},{17... | collective-permute-start | bytes 98312 | tf_op jit(solution)/shard_map/ppermute | solution.py:19
  119.6 1.5 collective-permute-start.5
  121.1 0.0 collective-permute-done.4
  121.2 3.1 %collective-permute-done.5 = f32[2,4096]{1,0:T(2,128)S(1)} collective-permute-done((f32[2,4096]{1,0:T(2,128)S(1)}, f32[2,4096]{1,0:T(2,128)S(1)}, u32[]{:S(2)}, u32[]{:S(2)}) %collective-permute-start.5) | collective-permute-done | bytes 32800 | tf_op jit(solution)/shard_map/ppermute | solution.py:21
  124.3 11.0 %select_maximum_fusion = f32[520,4104]{1,0:T(8,128)S(1)} fusion(f32[2,4096]{1,0:T(2,128)S(1)} %collective-permute-done.5, f32[512,4096]{1,0:T(8,128)} %param.6, f32[2,4096]{1,0:T(2,128)S(1)} %collective-permute-done.4), kind=kLoop, calls=%fused_computation.2 | loop fusion | flops 27743040 | bytes 16990464 | tf_op jit(solution)/shard_map/concatenate | solution.py:17
  135.2 3.4 %fusion.158 = (f32[520,520]{1,0:T(8,128)S(1)}, f32[520,520]{1,0:T(8,128)S(1)}, f32[520,520]{1,0:T(8,128)}, f32[520,520]{1,0:T(8,128)}, f32[520,520]{1,0:T(8,128)...) fusion(f32[520,4104]{1,0:T(8,128)S(1)} %select_maximum_fusion), kind=kLoop, calls=%fused_computation.213 | loop fusion | bytes 17305600 | tf_op jit(solution)/shard_map/slice | solution.py:80
  138.7 11.6 %concatenate.48 = f32[520,4160]{1,0:T(8,128)} concatenate(f32[520,520]{1,0:T(8,128)} %get-tuple-element.16, f32[520,520]{1,0:T(8,128)} %get-tuple-element.15, f32[520,520]{1,0:T(8,128)} %get-tuple-element.14, f32[520,520]{1,0:T(8,128)} %get-tuple-element.13, f32[520,520]{1,0:T(8,128)} %get-tuple-element.12, f32[520,520]{1,0:T(8,128)} %get-tuple-element.11, ...), dimensions={1} | concatenate | bytes 17305600 | tf_op jit(solution)/shard_map/concatenate | solution.py:80
  150.3 73.9 %all-gather.4.cloned.1.call-done = f32[2,4160,256]{2,1,0:T(8,128)} async-done(((f32[2,520,256]{2,1,0:T(8,128)}), f32[2,4160,256]{2,1,0:T(8,128)}) %all-gather.4.cloned.1.call-update) | async-done | bytes 8519696 | tf_op jit(solution)/shard_map/all_gather | solution.py:116
  224.2 12.2 %fusion.1 = f32[2,256,520]{1,2,0:T(8,128)S(1)} fusion(f32[2,4160,256]{2,1,0:T(8,128)} %all-gather.4.cloned.1.call-done, f32[520,4160]{1,0:T(8,128)} %concatenate.48), kind=kOutput, calls=%fused_computation.6 | convolution fusion | flops 6645350400 | bytes 18237440 | tf_op jit(solution)/shard_map/ik,rkj->rij/dot_general | solution.py:115
  236.4 0.2 fusion.162
  236.6 0.2 copy.10
  236.9 3.2 %collective-permute-start.6 = (f32[2,520,2]{1,2,0:T(2,128)S(1)}, f32[2,520,2]{1,2,0:T(2,128)S(1)}, u32[]{:S(2)}, u32[]{:S(2)}) collective-permute-start(f32[2,520,2]{1,2,0:T(2,128)S(1)} %copy.10), channel_id=1, source_target_pairs={{0,1},{1,2},{2,3},{3,4},{4,5},{5,6},{6,7},{7,8},{8,9},{9,10},{10,1... | collective-permute-start | bytes 24968 | tf_op jit(solution)/shard_map/ppermute | solution.py:19
  240.1 0.2 copy.12
  240.3 2.2 collective-permute-start.7
  242.5 0.0 collective-permute-done.6
  242.5 0.2 copy.11
  242.7 2.5 collective-permute-done.7
  245.3 0.2 copy.13
  245.5 0.7 reduce-precision_convert_fusion.7
  246.2 3.8 %convolution_bitcast_fusion = f32[3,2,1024,260]{2,3,1,0:T(8,128)S(1)} fusion(bf16[1,2,520,260]{3,2,1,0:T(8,128)(2,1)S(1)} %get-tuple-element.36, bf16[1,2,520,260]{3,2,1,0:T(8,128)(2,1)S(1)} %get-tuple-element.35, bf16[1,2,520,260]{3,2,1,0:T(8,128)(2,1)S(1)} %get-tuple-element.34, f32[1024]{0:T(1024)S(1)} %multiply_add_fusion, f32[520]{0:T(1024)S(1)} %iota_add_fusion), kind=kOutput, calls=%fused_computation.50 | convolution fusion | flops 1672544640 | bytes 8018336 | tf_op jit(solution)/shard_map/pi,srij->srpj/dot_general | solution.py:74
  250.0 1.0 reduce-precision_convert_fusion.3
  251.1 0.5 reduce-precision_convert_fusion.2
  251.5 0.0 copy-start.1
  251.6 0.0 copy-start.6
  251.6 7.3 %fusion.17 = f32[3,2,1024,512]{3,2,1,0:T(8,128)} fusion(bf16[1,2,1024,260]{2,3,1,0:T(8,128)(2,1)S(1)} %get-tuple-element.33, bf16[1,2,1024,260]{2,3,1,0:T(8,128)(2,1)S(1)} %get-tuple-element.32, bf16[1,2,1024,260]{2,3,1,0:T(8,128)(2,1)S(1)} %get-tuple-element.5, f32[512]{0:T(512)S(1)} %multiply_add_fusion.2, f32[260]{0:T(512)S(1)} %iota_add_fusion.1), kind=kOutput, calls=%fused_computation.28 | convolution fusion | flops 1641369600 | bytes 15780880 | tf_op jit(solution)/shard_map/srpj,jq->srpq/dot_general | solution.py:72
  258.8 0.0 copy-done.1
  258.8 9.0 %fusion.16 = f32[2,1024,512]{2,1,0:T(8,128)} fusion(f32[3,2,1024,512]{3,2,1,0:T(8,128)} %fusion.17, f32[2,1024,512]{2,1,0:T(8,128)S(1)} %copy-done.1, f32[1024,512]{1,0:T(8,128)S(1)} %copy-done.6), kind=kLoop, calls=%fused_computation.26 | loop fusion | flops 4194304 | bytes 23068672 | tf_op jit(solution)/shard_map/add | solution.py:123
  (12 shorter events, 0.1 us)
Async XLA Ops:
  6.5 75.8 %all-gather.6.cloned.1.call-start = ((), (), s32[]{:S(2)}) async-start(), calls=%async_computation.1 | async-start | bytes 9584640 | tf_op jit(solution)/shard_map/all_gather | solution.py:111
  8.8 12.3 %collective-permute-start = (f32[2,1024,4]{1,2,0:T(4,128)S(1)}, f32[2,1024,4]{1,2,0:T(4,128)S(1)}, u32[]{:S(2)}, u32[]{:S(2)}) collective-permute-start(f32[2,1024,4]{1,2,0:T(4,128)S(1)} %copy.22), channel_id=1, source_target_pairs={{0,1},{1,2},{2,3},{3,4},{4,5},{5,6},{6,7},{7,8},{8,9},{9,10},{10,1... | collective-permute-start | bytes 98312 | tf_op jit(solution)/shard_map/ppermute | solution.py:33
  13.7 8.5 %collective-permute-start.1 = (f32[2,1024,4]{1,2,0:T(4,128)S(1)}, f32[2,1024,4]{1,2,0:T(4,128)S(1)}, u32[]{:S(2)}, u32[]{:S(2)}) collective-permute-start(f32[2,1024,4]{1,2,0:T(4,128)S(1)} %copy.23), channel_id=1, source_target_pairs={{1,0},{2,1},{3,2},{4,3},{5,4},{6,5},{7,6},{8,7},{9,8},{10,9},{11,1... | collective-permute-start | bytes 98312 | tf_op jit(solution)/shard_map/ppermute | solution.py:34
  28.4 195.8 %all-gather.4.cloned.1.call-start = ((), (), s32[]{:S(2)}) async-start(), calls=%async_computation | async-start | bytes 9584640 | tf_op jit(solution)/shard_map/all_gather | solution.py:116
  31.1 0.8 copy-start.2
  31.1 1.0 copy-start.4
  32.1 47.2 %collective-permute-start.2 = (f32[256,2048]{1,0:T(8,128)S(1)}, f32[256,2048]{1,0:T(8,128)}, u32[]{:S(2)}, u32[]{:S(2)}) collective-permute-start(f32[256,2048]{1,0:T(8,128)S(1)} %fusion.58), channel_id=1, source_target_pairs={{0,2},{2,0},{1,3},{3,1},{4,6},{6,4},{5,7},{7,5},{8,10},{10,8},{9,1... | collective-permute-start | bytes 6291464 | tf_op jit(solution)/shard_map/ppermute | solution.py:99
  82.4 8.3 %copy-start = (f32[1,2,520,2048]{3,2,1,0:T(8,128)S(1)}, f32[1,2,520,2048]{3,2,1,0:T(8,128)}, u32[]{:S(2)}) copy-start(f32[1,2,520,2048]{3,2,1,0:T(8,128)} %all-gather.6.cloned.1.call-done) | copy-start | bytes 25559044
  82.4 8.3 %copy-start.3 = (f32[256,512]{1,0:T(8,128)S(1)}, f32[256,512]{1,0:T(8,128)}, u32[]{:S(2)}) copy-start(f32[256,512]{1,0:T(8,128)} %copy-done.2) | copy-start | bytes 1572868
  82.4 8.3 %copy-start.5 = (f32[256,512]{1,0:T(8,128)S(1)}, f32[256,512]{1,0:T(8,128)}, u32[]{:S(2)}) copy-start(f32[256,512]{1,0:T(8,128)} %copy-done.4) | copy-start | bytes 1572868
  89.3 24.9 %collective-permute-start.3 = (f32[2,520,256]{2,1,0:T(8,128)S(1)}, f32[2,520,256]{2,1,0:T(8,128)S(1)}, u32[]{:S(2)}, u32[]{:S(2)}) collective-permute-start(f32[2,520,256]{2,1,0:T(8,128)S(1)} %fusion.4), channel_id=1, source_target_pairs={{0,2},{2,0},{1,3},{3,1},{4,6},{6,4},{5,7},{7,5},{8,10},{10,8},{9,1... | collective-permute-start | bytes 3194888 | tf_op jit(solution)/shard_map/ppermute | solution.py:114
  116.4 4.8 %collective-permute-start.4 = (f32[2,4096]{1,0:T(2,128)S(1)}, f32[2,4096]{1,0:T(2,128)S(1)}, u32[]{:S(2)}, u32[]{:S(2)}) collective-permute-start(f32[2,4096]{1,0:T(2,128)S(1)} %get-tuple-element.17), channel_id=1, source_target_pairs={{0,16},{16,32},{32,48},{48,64},{64,80},{80,96},{96,112},{1,17},{17... | collective-permute-start | bytes 98312 | tf_op jit(solution)/shard_map/ppermute | solution.py:19
  119.6 4.7 %collective-permute-start.5 = (f32[2,4096]{1,0:T(2,128)S(1)}, f32[2,4096]{1,0:T(2,128)S(1)}, u32[]{:S(2)}, u32[]{:S(2)}) collective-permute-start(f32[2,4096]{1,0:T(2,128)S(1)} %get-tuple-element.18), channel_id=1, source_target_pairs={{16,0},{32,16},{48,32},{64,48},{80,64},{96,80},{112,96},{17,1},{33... | collective-permute-start | bytes 98312 | tf_op jit(solution)/shard_map/ppermute | solution.py:21
  236.9 5.6 %collective-permute-start.6 = (f32[2,520,2]{1,2,0:T(2,128)S(1)}, f32[2,520,2]{1,2,0:T(2,128)S(1)}, u32[]{:S(2)}, u32[]{:S(2)}) collective-permute-start(f32[2,520,2]{1,2,0:T(2,128)S(1)} %copy.10), channel_id=1, source_target_pairs={{0,1},{1,2},{2,3},{3,4},{4,5},{5,6},{6,7},{7,8},{8,9},{9,10},{10,1... | collective-permute-start | bytes 24968 | tf_op jit(solution)/shard_map/ppermute | solution.py:19
  240.3 5.0 %collective-permute-start.7 = (f32[2,520,2]{1,2,0:T(2,128)S(1)}, f32[2,520,2]{1,2,0:T(2,128)S(1)}, u32[]{:S(2)}, u32[]{:S(2)}) collective-permute-start(f32[2,520,2]{1,2,0:T(2,128)S(1)} %copy.12), channel_id=1, source_target_pairs={{1,0},{2,1},{3,2},{4,3},{5,4},{6,5},{7,6},{8,7},{9,8},{10,9},{11,1... | collective-permute-start | bytes 24968 | tf_op jit(solution)/shard_map/ppermute | solution.py:21
  251.5 7.3 %copy-start.1 = (f32[2,1024,512]{2,1,0:T(8,128)S(1)}, f32[2,1024,512]{2,1,0:T(8,128)}, u32[]{:S(2)}) copy-start(f32[2,1024,512]{2,1,0:T(8,128)} %param.4) | copy-start | bytes 12582916
  251.6 7.3 %copy-start.6 = (f32[1024,512]{1,0:T(8,128)S(1)}, f32[1024,512]{1,0:T(8,128)}, u32[]{:S(2)}) copy-start(f32[1024,512]{1,0:T(8,128)} %param.5) | copy-start | bytes 6291460
Sparse Core Ops, SparseCore 0:
  28.6 53.7 all-gather.5
  115.5 108.6 all-gather.3
where the time goes:
time: 276 us; the launch traced here: 275 us
  waiting for transfers between devices  149 us (54%)
  matrix products  39.9 us (14%)
  other arithmetic  30.2 us (11%)
  local copies, waits for them, and re-layouts  23 us (8%)
  starting transfers between devices  19.1 us (7%)
  between operations  13.7 us (5%)
    all_gather x1, waiting for transfers between devices, body(): lax.all_gather(mixed, rows_axis, axis=1, tiled=True)  73.9 us
    ppermute x1, waiting for transfers between devices, body(): partner_cols = lax.ppermute(far_cols, 'yl', swap)  46.1 us
    ppermute x1, waiting for transfers between devices, body(): mixed = near + lax.ppermute(for_partner, 'yl', swap)  20.1 us
    dot_general x1, matrix products, body(): jnp.einsum('ik,rkj->rij', row_big, lax.all_gather(mixed, rows_axis, axis=...  12.2 us
    concatenate x1, local copies, waits for them, and re-layouts, row_windows(): jnp.concatenate([padded[:, block * w:block * w + width] for w in range(co...  11.6 us
    dot_general x4, matrix products, exact_dot(): jnp.einsum(f's{first},{second}->s{out}', parts, table, preferred_element_...  11.1 us
    concatenate x1, other arithmetic, with_halo(): jnp.concatenate([lax.ppermute(tail, axis, [(i, (i + 1) % count) for i in...  11 us
    add x1, other arithmetic, body(): return result + noise_var[None] * observed  9.05 us
  transfers between devices with their start and end apart: 10, of which 6 were waited for; matrix products, arithmetic and copies ran while one was open for 15% of the time, Pallas kernels for 0%

commit v1 on v0

--- a/solution.py
+++ b/solution.py
@@ -75,9 +75,9 @@
     return terms[0] + terms[1] + terms[2]
 
 
-def row_windows(kernel, count, block, width):
+def row_windows(kernel, order, block, width):
     padded = jnp.pad(kernel, ((0, width - kernel.shape[0]), (2, width - block - 2)))
-    return jnp.concatenate([padded[:, block * w : block * w + width] for w in range(count)], axis=1)
+    return jnp.concatenate([padded[:, block * w : block * w + width] for w in order], axis=1)
 
 
 def body(observed, noise_var, row_kernel, col_kernel):
@@ -98,7 +98,10 @@
     far_cols = jnp.where(side == 0, high, low)
     partner_cols = lax.ppermute(far_cols, "yl", swap)
     row_rows = with_halo(row_kernel, ((rows_axis, 0),), 2)
-    row_big = row_windows(row_rows, row_count, tile_rows, ext_rows)
+    halves_n = axis_count("yh")
+    depth = axis_count("z")
+    order = [h * depth + d for d in range(depth) for h in range(halves_n)]
+    row_big = row_windows(row_rows, order, tile_rows, ext_rows)
     before, after = edges(observed, cols_axis, 2, 4)
     col_adj = tap_table(2 * tile_cols + 8, tile_cols, False, 4)
     row_adj = tap_table(ext_rows, 2 * tile_rows, True, 2)
@@ -113,7 +116,7 @@
     for_partner = jnp.einsum("rik,jk->rij", half, partner_cols, precision=highest)
     mixed = near + lax.ppermute(for_partner, "yl", swap)
     product = jnp.einsum(
-        "ik,rkj->rij", row_big, lax.all_gather(mixed, rows_axis, axis=1, tiled=True), precision=highest
+        "ik,rkj->rij", row_big, lax.all_gather(mixed, ("z", "yh"), axis=1, tiled=True), precision=highest
     )
     coarse_ext = with_halo(product, ((cols_axis, 2),), 2)
     row_fwd = tap_table(2 * tile_rows, ext_rows, False, 2)

time: 276 us -> 276 us (level)
  no operation moved by 1% of the time
where the time goes in v1:
time: 276 us; the launch traced here: 275 us
  waiting for transfers between devices  149 us (54%)
  matrix products  39.9 us (14%)
  other arithmetic  30.2 us (11%)
  local copies, waits for them, and re-layouts  23 us (8%)
  starting transfers between devices  19.1 us (7%)
  between operations  13.7 us (5%)
    all_gather x1, waiting for transfers between devices, body(): lax.all_gather(mixed, ('z', 'yh'), axis=1, tiled=True)  73.9 us
    ppermute x1, waiting for transfers between devices, body(): partner_cols = lax.ppermute(far_cols, 'yl', swap)  46.1 us
    ppermute x1, waiting for transfers between devices, body(): mixed = near + lax.ppermute(for_partner, 'yl', swap)  20.1 us
    dot_general x1, matrix products, body(): jnp.einsum('ik,rkj->rij', row_big, lax.all_gather(mixed, ('z', 'yh'), axi...  12.2 us
    concatenate x1, local copies, waits for them, and re-layouts, row_windows(): jnp.concatenate([padded[:, block * w:block * w + width] for w in order],...  11.6 us
    dot_general x4, matrix products, exact_dot(): jnp.einsum(f's{first},{second}->s{out}', parts, table, preferred_element_...  11.2 us
    concatenate x1, other arithmetic, with_halo(): jnp.concatenate([lax.ppermute(tail, axis, [(i, (i + 1) % count) for i in...  11 us
    add x1, other arithmetic, body(): return result + noise_var[None] * observed  9.05 us
  transfers between devices with their start and end apart: 10, of which 6 were waited for; matrix products, arithmetic and copies ran while one was open for 15% of the time, Pallas kernels for 0%

profile of v1, /device:TPU:1, one launch (start us, length us, event | category | flops | bytes accessed | tf_op | source)
XLA Modules:
  0.0 274.7 jit_solution(1158796201203381123)
XLA Ops:
  6.5 0.0 all-gather.6.cloned.1.call-start
  6.5 1.9 fusion.161
  8.4 0.3 copy.22
  8.8 4.6 %collective-permute-start = (f32[2,1024,4]{1,2,0:T(4,128)S(1)}, f32[2,1024,4]{1,2,0:T(4,128)S(1)}, u32[]{:S(2)}, u32[]{:S(2)}) collective-permute-start(f32[2,1024,4]{1,2,0:T(4,128)S(1)} %copy.22), channel_id=1, source_target_pairs={{0,1},{1,2},{2,3},{3,4},{4,5},{5,6},{6,7},{7,8},{8,9},{9,10},{10,1... | collective-permute-start | bytes 98312 | tf_op jit(solution)/shard_map/ppermute | solution.py:33
  13.4 0.3 copy.23
  13.7 1.9 collective-permute-start.1
  15.6 3.2 %fusion.47 = (bf16[1,2,1024,512]{3,2,1,0:T(8,128)(2,1)S(1)}, bf16[1,2,1024,512]{3,2,1,0:T(8,128)(2,1)S(1)}, bf16[1,2,1024,512]{3,2,1,0:T(8,128)(2,1)S(1)}) fusion(f32[2,1024,512]{2,1,0:T(8,128)} %param.4), kind=kLoop, calls=%fused_computation.77 | loop fusion | flops 7340032 | bytes 10485760 | tf_op jit(solution)/shard_map/stack | solution.py:70
  18.9 0.4 fusion.91
  19.2 1.8 fusion.8
  21.1 0.0 collective-permute-done
  21.1 1.0 fusion.106
  22.2 0.0 collective-permute-done.1
  22.2 1.0 fusion.112
  23.2 1.3 reduce-precision_convert_fusion.5
  24.5 0.4 reduce-precision_convert_fusion.4
  24.9 2.3 fusion.54
  27.2 1.2 slice_add_fusion.10
  28.4 0.0 all-gather.6.cloned.1.call-update
  28.4 0.0 all-gather.4.cloned.1.call-start
  28.5 2.6 fusion.160
  31.1 0.0 copy-start.2
  31.1 0.0 copy-start.4
  31.1 0.3 fusion.58
  31.4 0.5 copy-done.2
  31.9 0.1 copy-done.4
  32.1 1.1 collective-permute-start.2
  33.2 46.1 %collective-permute-done.2 = f32[256,2048]{1,0:T(8,128)} collective-permute-done((f32[256,2048]{1,0:T(8,128)S(1)}, f32[256,2048]{1,0:T(8,128)}, u32[]{:S(2)}, u32[]{:S(2)}) %collective-permute-start.2) | collective-permute-done | bytes 2097184 | tf_op jit(solution)/shard_map/ppermute | solution.py:99
  79.3 3.0 %all-gather.6.cloned.1.call-done = f32[1,2,520,2048]{3,2,1,0:T(8,128)} async-done(((f32[1,2,520,256]{3,2,1,0:T(8,128)}), f32[1,2,520,2048]{3,2,1,0:T(8,128)}) %all-gather.6.cloned.1.call-update) | async-done | bytes 8519696 | tf_op jit(solution)/shard_map/all_gather | solution.py:114
  82.4 6.9 %fusion.4 = f32[2,520,256]{2,1,0:T(8,128)S(1)} fusion(f32[1,2,520,2048]{3,2,1,0:T(8,128)} %all-gather.6.cloned.1.call-done, f32[256,2048]{1,0:T(8,128)} %collective-permute-done.2), kind=kOutput, calls=%fused_computation.9 | convolution fusion | flops 3271557120 | bytes 11681792 | tf_op jit(solution)/shard_map/rik,jk->rij/dot_general | solution.py:116
  89.3 1.3 collective-permute-start.3
  90.6 0.0 copy-done
  90.6 0.0 copy-done.3
  90.6 0.0 copy-done.5
  90.6 3.5 %fusion.6 = f32[2,520,256]{2,1,0:T(8,128)S(1)} fusion(f32[1,2,520,2048]{3,2,1,0:T(8,128)S(1)} %copy-done, f32[256,512]{1,0:T(8,128)S(1)} %copy-done.3, f32[256,512]{1,0:T(8,128)S(1)} %copy-done.5, f32[256,512]{1,0:T(8,128)S(1)} %get-tuple-element.20, f32[256,512]{1,0:T(8,128)S(1)} %get-tuple-element.21, f32[256,512]{1,0:T(8,128)S(1)} %get-tuple-element.22, ...), kind=kOutput, calls=%fused_computation.11 | convolution fusion | flops 3275227136 | bytes 13778945 | tf_op jit(solution)/shard_map/rik,jk->rij/dot_general | solution.py:115
  94.2 20.1 %collective-permute-done.3 = f32[2,520,256]{2,1,0:T(8,128)S(1)} collective-permute-done((f32[2,520,256]{2,1,0:T(8,128)S(1)}, f32[2,520,256]{2,1,0:T(8,128)S(1)}, u32[]{:S(2)}, u32[]{:S(2)}) %collective-permute-start.3) | collective-permute-done | bytes 1064992 | tf_op jit(solution)/shard_map/ppermute | solution.py:117
  114.2 1.1 add.203
  115.4 0.0 all-gather.4.cloned.1.call-update
  115.4 1.0 fusion.159
  116.4 3.2 %collective-permute-start.4 = (f32[2,4096]{1,0:T(2,128)S(1)}, f32[2,4096]{1,0:T(2,128)S(1)}, u32[]{:S(2)}, u32[]{:S(2)}) collective-permute-start(f32[2,4096]{1,0:T(2,128)S(1)} %get-tuple-element.17), channel_id=1, source_target_pairs={{0,16},{16,32},{32,48},{48,64},{64,80},{80,96},{96,112},{1,17},{17... | collective-permute-start | bytes 98312 | tf_op jit(solution)/shard_map/ppermute | solution.py:19
  119.6 1.5 collective-permute-start.5
  121.1 0.0 collective-permute-done.4
  121.2 3.1 %collective-permute-done.5 = f32[2,4096]{1,0:T(2,128)S(1)} collective-permute-done((f32[2,4096]{1,0:T(2,128)S(1)}, f32[2,4096]{1,0:T(2,128)S(1)}, u32[]{:S(2)}, u32[]{:S(2)}) %collective-permute-start.5) | collective-permute-done | bytes 32800 | tf_op jit(solution)/shard_map/ppermute | solution.py:21
  124.3 11.0 %select_maximum_fusion = f32[520,4104]{1,0:T(8,128)S(1)} fusion(f32[2,4096]{1,0:T(2,128)S(1)} %collective-permute-done.5, f32[512,4096]{1,0:T(8,128)} %param.6, f32[2,4096]{1,0:T(2,128)S(1)} %collective-permute-done.4), kind=kLoop, calls=%fused_computation.2 | loop fusion | flops 27743040 | bytes 16990464 | tf_op jit(solution)/shard_map/concatenate | solution.py:17
  135.2 3.4 %fusion.158 = (f32[520,520]{1,0:T(8,128)S(1)}, f32[520,520]{1,0:T(8,128)S(1)}, f32[520,520]{1,0:T(8,128)}, f32[520,520]{1,0:T(8,128)}, f32[520,520]{1,0:T(8,128)...) fusion(f32[520,4104]{1,0:T(8,128)S(1)} %select_maximum_fusion), kind=kLoop, calls=%fused_computation.213 | loop fusion | bytes 17305600 | tf_op jit(solution)/shard_map/slice | solution.py:80
  138.7 11.6 %concatenate.48 = f32[520,4160]{1,0:T(8,128)} concatenate(f32[520,520]{1,0:T(8,128)} %get-tuple-element.16, f32[520,520]{1,0:T(8,128)} %get-tuple-element.15, f32[520,520]{1,0:T(8,128)} %get-tuple-element.14, f32[520,520]{1,0:T(8,128)} %get-tuple-element.13, f32[520,520]{1,0:T(8,128)} %get-tuple-element.12, f32[520,520]{1,0:T(8,128)} %get-tuple-element.11, ...), dimensions={1} | concatenate | bytes 17305600 | tf_op jit(solution)/shard_map/concatenate | solution.py:80
  150.3 73.9 %all-gather.4.cloned.1.call-done = f32[2,4160,256]{2,1,0:T(8,128)} async-done(((f32[2,520,256]{2,1,0:T(8,128)}), f32[2,4160,256]{2,1,0:T(8,128)}) %all-gather.4.cloned.1.call-update) | async-done | bytes 8519696 | tf_op jit(solution)/shard_map/all_gather | solution.py:119
  224.2 12.2 %fusion.1 = f32[2,256,520]{1,2,0:T(8,128)S(1)} fusion(f32[2,4160,256]{2,1,0:T(8,128)} %all-gather.4.cloned.1.call-done, f32[520,4160]{1,0:T(8,128)} %concatenate.48), kind=kOutput, calls=%fused_computation.6 | convolution fusion | flops 6645350400 | bytes 18237440 | tf_op jit(solution)/shard_map/ik,rkj->rij/dot_general | solution.py:118
  236.4 0.2 fusion.162
  236.6 0.2 copy.10
  236.9 3.2 %collective-permute-start.6 = (f32[2,520,2]{1,2,0:T(2,128)S(1)}, f32[2,520,2]{1,2,0:T(2,128)S(1)}, u32[]{:S(2)}, u32[]{:S(2)}) collective-permute-start(f32[2,520,2]{1,2,0:T(2,128)S(1)} %copy.10), channel_id=1, source_target_pairs={{0,1},{1,2},{2,3},{3,4},{4,5},{5,6},{6,7},{7,8},{8,9},{9,10},{10,1... | collective-permute-start | bytes 24968 | tf_op jit(solution)/shard_map/ppermute | solution.py:19
  240.1 0.2 copy.12
  240.3 2.2 collective-permute-start.7
  242.5 0.0 collective-permute-done.6
  242.5 0.2 copy.11
  242.7 2.5 collective-permute-done.7
  245.3 0.2 copy.13
  245.5 0.7 reduce-precision_convert_fusion.7
  246.2 3.8 %convolution_bitcast_fusion = f32[3,2,1024,260]{2,3,1,0:T(8,128)S(1)} fusion(bf16[1,2,520,260]{3,2,1,0:T(8,128)(2,1)S(1)} %get-tuple-element.36, bf16[1,2,520,260]{3,2,1,0:T(8,128)(2,1)S(1)} %get-tuple-element.35, bf16[1,2,520,260]{3,2,1,0:T(8,128)(2,1)S(1)} %get-tuple-element.34, f32[1024]{0:T(1024)S(1)} %multiply_add_fusion, f32[520]{0:T(1024)S(1)} %iota_add_fusion), kind=kOutput, calls=%fused_computation.50 | convolution fusion | flops 1672544640 | bytes 8018336 | tf_op jit(solution)/shard_map/pi,srij->srpj/dot_general | solution.py:74
  250.0 1.0 reduce-precision_convert_fusion.3
  251.0 0.5 reduce-precision_convert_fusion.2
  251.5 0.0 copy-start.1
  251.6 0.0 copy-start.6
  251.6 7.3 %fusion.17 = f32[3,2,1024,512]{3,2,1,0:T(8,128)} fusion(bf16[1,2,1024,260]{2,3,1,0:T(8,128)(2,1)S(1)} %get-tuple-element.33, bf16[1,2,1024,260]{2,3,1,0:T(8,128)(2,1)S(1)} %get-tuple-element.32, bf16[1,2,1024,260]{2,3,1,0:T(8,128)(2,1)S(1)} %get-tuple-element.5, f32[512]{0:T(512)S(1)} %multiply_add_fusion.2, f32[260]{0:T(512)S(1)} %iota_add_fusion.1), kind=kOutput, calls=%fused_computation.28 | convolution fusion | flops 1641369600 | bytes 15780880 | tf_op jit(solution)/shard_map/srpj,jq->srpq/dot_general | solution.py:72
  258.8 9.0 %fusion.16 = f32[2,1024,512]{2,1,0:T(8,128)} fusion(f32[3,2,1024,512]{3,2,1,0:T(8,128)} %fusion.17, f32[2,1024,512]{2,1,0:T(8,128)S(1)} %copy-done.1, f32[1024,512]{1,0:T(8,128)S(1)} %copy-done.6), kind=kLoop, calls=%fused_computation.26 | loop fusion | flops 4194304 | bytes 23068672 | tf_op jit(solution)/shard_map/add | solution.py:126
  (12 shorter events, 0.1 us)
Async XLA Ops:
  6.5 75.8 %all-gather.6.cloned.1.call-start = ((), (), s32[]{:S(2)}) async-start(), calls=%async_computation.1 | async-start | bytes 9584640 | tf_op jit(solution)/shard_map/all_gather | solution.py:114
  8.8 12.3 %collective-permute-start = (f32[2,1024,4]{1,2,0:T(4,128)S(1)}, f32[2,1024,4]{1,2,0:T(4,128)S(1)}, u32[]{:S(2)}, u32[]{:S(2)}) collective-permute-start(f32[2,1024,4]{1,2,0:T(4,128)S(1)} %copy.22), channel_id=1, source_target_pairs={{0,1},{1,2},{2,3},{3,4},{4,5},{5,6},{6,7},{7,8},{8,9},{9,10},{10,1... | collective-permute-start | bytes 98312 | tf_op jit(solution)/shard_map/ppermute | solution.py:33
  13.7 8.5 %collective-permute-start.1 = (f32[2,1024,4]{1,2,0:T(4,128)S(1)}, f32[2,1024,4]{1,2,0:T(4,128)S(1)}, u32[]{:S(2)}, u32[]{:S(2)}) collective-permute-start(f32[2,1024,4]{1,2,0:T(4,128)S(1)} %copy.23), channel_id=1, source_target_pairs={{1,0},{2,1},{3,2},{4,3},{5,4},{6,5},{7,6},{8,7},{9,8},{10,9},{11,1... | collective-permute-start | bytes 98312 | tf_op jit(solution)/shard_map/ppermute | solution.py:34
  28.4 195.8 %all-gather.4.cloned.1.call-start = ((), (), s32[]{:S(2)}) async-start(), calls=%async_computation | async-start | bytes 9584640 | tf_op jit(solution)/shard_map/all_gather | solution.py:119
  31.1 0.8 copy-start.2
  31.1 1.0 copy-start.4
  32.1 47.2 %collective-permute-start.2 = (f32[256,2048]{1,0:T(8,128)S(1)}, f32[256,2048]{1,0:T(8,128)}, u32[]{:S(2)}, u32[]{:S(2)}) collective-permute-start(f32[256,2048]{1,0:T(8,128)S(1)} %fusion.58), channel_id=1, source_target_pairs={{0,2},{2,0},{1,3},{3,1},{4,6},{6,4},{5,7},{7,5},{8,10},{10,8},{9,1... | collective-permute-start | bytes 6291464 | tf_op jit(solution)/shard_map/ppermute | solution.py:99
  82.4 8.3 %copy-start = (f32[1,2,520,2048]{3,2,1,0:T(8,128)S(1)}, f32[1,2,520,2048]{3,2,1,0:T(8,128)}, u32[]{:S(2)}) copy-start(f32[1,2,520,2048]{3,2,1,0:T(8,128)} %all-gather.6.cloned.1.call-done) | copy-start | bytes 25559044
  82.4 8.3 %copy-start.3 = (f32[256,512]{1,0:T(8,128)S(1)}, f32[256,512]{1,0:T(8,128)}, u32[]{:S(2)}) copy-start(f32[256,512]{1,0:T(8,128)} %copy-done.2) | copy-start | bytes 1572868
  82.4 8.3 %copy-start.5 = (f32[256,512]{1,0:T(8,128)S(1)}, f32[256,512]{1,0:T(8,128)}, u32[]{:S(2)}) copy-start(f32[256,512]{1,0:T(8,128)} %copy-done.4) | copy-start | bytes 1572868
  89.3 24.9 %collective-permute-start.3 = (f32[2,520,256]{2,1,0:T(8,128)S(1)}, f32[2,520,256]{2,1,0:T(8,128)S(1)}, u32[]{:S(2)}, u32[]{:S(2)}) collective-permute-start(f32[2,520,256]{2,1,0:T(8,128)S(1)} %fusion.4), channel_id=1, source_target_pairs={{0,2},{2,0},{1,3},{3,1},{4,6},{6,4},{5,7},{7,5},{8,10},{10,8},{9,1... | collective-permute-start | bytes 3194888 | tf_op jit(solution)/shard_map/ppermute | solution.py:117
  116.4 4.8 %collective-permute-start.4 = (f32[2,4096]{1,0:T(2,128)S(1)}, f32[2,4096]{1,0:T(2,128)S(1)}, u32[]{:S(2)}, u32[]{:S(2)}) collective-permute-start(f32[2,4096]{1,0:T(2,128)S(1)} %get-tuple-element.17), channel_id=1, source_target_pairs={{0,16},{16,32},{32,48},{48,64},{64,80},{80,96},{96,112},{1,17},{17... | collective-permute-start | bytes 98312 | tf_op jit(solution)/shard_map/ppermute | solution.py:19
  119.6 4.7 %collective-permute-start.5 = (f32[2,4096]{1,0:T(2,128)S(1)}, f32[2,4096]{1,0:T(2,128)S(1)}, u32[]{:S(2)}, u32[]{:S(2)}) collective-permute-start(f32[2,4096]{1,0:T(2,128)S(1)} %get-tuple-element.18), channel_id=1, source_target_pairs={{16,0},{32,16},{48,32},{64,48},{80,64},{96,80},{112,96},{17,1},{33... | collective-permute-start | bytes 98312 | tf_op jit(solution)/shard_map/ppermute | solution.py:21
  236.9 5.6 %collective-permute-start.6 = (f32[2,520,2]{1,2,0:T(2,128)S(1)}, f32[2,520,2]{1,2,0:T(2,128)S(1)}, u32[]{:S(2)}, u32[]{:S(2)}) collective-permute-start(f32[2,520,2]{1,2,0:T(2,128)S(1)} %copy.10), channel_id=1, source_target_pairs={{0,1},{1,2},{2,3},{3,4},{4,5},{5,6},{6,7},{7,8},{8,9},{9,10},{10,1... | collective-permute-start | bytes 24968 | tf_op jit(solution)/shard_map/ppermute | solution.py:19
  240.3 5.0 %collective-permute-start.7 = (f32[2,520,2]{1,2,0:T(2,128)S(1)}, f32[2,520,2]{1,2,0:T(2,128)S(1)}, u32[]{:S(2)}, u32[]{:S(2)}) collective-permute-start(f32[2,520,2]{1,2,0:T(2,128)S(1)} %copy.12), channel_id=1, source_target_pairs={{1,0},{2,1},{3,2},{4,3},{5,4},{6,5},{7,6},{8,7},{9,8},{10,9},{11,1... | collective-permute-start | bytes 24968 | tf_op jit(solution)/shard_map/ppermute | solution.py:21
  251.5 7.3 %copy-start.1 = (f32[2,1024,512]{2,1,0:T(8,128)S(1)}, f32[2,1024,512]{2,1,0:T(8,128)}, u32[]{:S(2)}) copy-start(f32[2,1024,512]{2,1,0:T(8,128)} %param.4) | copy-start | bytes 12582916
  251.6 7.3 %copy-start.6 = (f32[1024,512]{1,0:T(8,128)S(1)}, f32[1024,512]{1,0:T(8,128)}, u32[]{:S(2)}) copy-start(f32[1024,512]{1,0:T(8,128)} %param.5) | copy-start | bytes 6291460
Sparse Core Ops, SparseCore 0:
  28.6 53.7 all-gather.5
  115.5 108.6 all-gather.3

commit v2 on v1

--- a/solution.py
+++ b/solution.py
@@ -65,14 +65,13 @@
 
 
 def exact_dot(eq, x, table, data_first):
-    ins, out = eq.split("->")
+    ins, _ = eq.split("->")
     first, second = ins.split(",")
-    parts = jnp.stack(split3(x))
     if data_first:
-        terms = jnp.einsum(f"s{first},{second}->s{out}", parts, table, preferred_element_type=jnp.float32)
-    else:
-        terms = jnp.einsum(f"{first},s{second}->s{out}", table, parts, preferred_element_type=jnp.float32)
-    return terms[0] + terms[1] + terms[2]
+        parts = jnp.concatenate(split3(x), axis=first.index(second[0]))
+        return jnp.einsum(eq, parts, jnp.concatenate([table] * 3, axis=0), preferred_element_type=jnp.float32)
+    parts = jnp.concatenate(split3(x), axis=second.index(first[1]))
+    return jnp.einsum(eq, jnp.concatenate([table] * 3, axis=1), parts, preferred_element_type=jnp.float32)
 
 
 def row_windows(kernel, order, block, width):

time: 276 us -> 260 us (0.942)
  other arithmetic: 30.2 us -> 20.6 us
  matrix products: 39.9 us -> 35.2 us
    add x2 -> x0, other arithmetic: 10.2 us -> none  [the longest x1 9.05 us: body(): return result + noise_var[None] * observed]
    dot_general x6, matrix products: 17.2 us -> 12.5 us  [the longest x4 7.21 us: exact_dot(): jnp.einsum(eq, parts, jnp.concatenate([table] * 3, axis=0), preferred_ele...]
    convert_element_type x1 -> x4, other arithmetic: 0.37 us -> 4.28 us  [tap_table(): return keys_weight(dist).astype(jnp.bfloat16)]
    another operation x3 -> x0, other arithmetic: 3.25 us -> none  [exact_dot(): parts = jnp.stack(split3(x))]
  transfers between devices with their start and end apart: 10 -> 10, of which waited for: 6 -> 6; matrix products, arithmetic and copies ran while one was open for 15% -> 16% of each run, Pallas kernels for 0% -> 0%
where the time goes in v2:
time: 260 us; the launch traced here: 259 us
  waiting for transfers between devices  147 us (57%)
  matrix products  35.2 us (14%)
  local copies, waits for them, and re-layouts  23.9 us (9%)
  other arithmetic  20.6 us (8%)
  starting transfers between devices  19 us (7%)
  between operations  13.7 us (5%)
    all_gather x1, waiting for transfers between devices, body(): lax.all_gather(mixed, ('z', 'yh'), axis=1, tiled=True)  73.9 us
    ppermute x1, waiting for transfers between devices, body(): partner_cols = lax.ppermute(far_cols, 'yl', swap)  46.1 us
    ppermute x1, waiting for transfers between devices, body(): mixed = near + lax.ppermute(for_partner, 'yl', swap)  20.1 us
    dot_general x1, matrix products, body(): jnp.einsum('ik,rkj->rij', row_big, lax.all_gather(mixed, ('z', 'yh'), axi...  12.2 us
    concatenate x1, local copies, waits for them, and re-layouts, row_windows(): jnp.concatenate([padded[:, block * w:block * w + width] for w in order],...  11.6 us
    concatenate x1, other arithmetic, with_halo(): jnp.concatenate([lax.ppermute(tail, axis, [(i, (i + 1) % count) for i in...  11 us
    dot_general x4, matrix products, exact_dot(): jnp.einsum(eq, parts, jnp.concatenate([table] * 3, axis=0), preferred_ele...  7.21 us
    dot_general x1, matrix products, body(): jnp.einsum('rik,jk->rij', half, partner_cols, precision=highest)  6.93 us
  transfers between devices with their start and end apart: 10, of which 6 were waited for; matrix products, arithmetic and copies ran while one was open for 16% of the time, Pallas kernels for 0%

profile of v2, /device:TPU:1, one launch (start us, length us, event | category | flops | bytes accessed | tf_op | source)
XLA Modules:
  0.0 258.9 jit_solution(11175421567967225632)
XLA Ops:
  6.5 0.0 all-gather.3.cloned.1.call-start
  6.5 1.9 fusion.117
  8.4 0.3 copy.16
  8.8 4.6 %collective-permute-start = (f32[2,1024,4]{1,2,0:T(4,128)S(1)}, f32[2,1024,4]{1,2,0:T(4,128)S(1)}, u32[]{:S(2)}, u32[]{:S(2)}) collective-permute-start(f32[2,1024,4]{1,2,0:T(4,128)S(1)} %copy.16), channel_id=1, source_target_pairs={{0,1},{1,2},{2,3},{3,4},{4,5},{5,6},{6,7},{7,8},{8,9},{9,10},{10,1... | collective-permute-start | bytes 98312 | tf_op jit(solution)/shard_map/ppermute | solution.py:33
  13.4 0.3 copy.17
  13.7 1.9 collective-permute-start.1
  15.6 3.2 %reduce-precision_convert_fusion.1 = (bf16[2,1024,512]{2,1,0:T(8,128)(2,1)S(1)}, bf16[2,1024,512]{2,1,0:T(8,128)(2,1)S(1)}, bf16[2,1024,512]{2,1,0:T(8,128)(2,1)S(1)}) fusion(f32[2,1024,512]{2,1,0:T(8,128)} %param.4), kind=kLoop, calls=%fused_computation.18 | loop fusion | flops 7340032 | bytes 10485760 | tf_op jit(solution)/shard_map/convert_element_type | solution.py:64
  18.9 0.4 fusion.82
  19.2 1.3 fusion.40
  20.5 0.1 slice.112
  20.6 0.0 collective-permute-done
  20.6 0.5 fusion.85
  21.1 0.0 collective-permute-done.1
  21.2 0.5 fusion.91
  21.6 2.3 reduce-precision_convert_fusion.5
  23.9 2.8 %fusion.59 = f32[2,520,256]{2,1,0:T(8,128)} fusion(bf16[520,1024]{1,0:T(8,128)(2,1)S(1)} %fusion.40, bf16[2,1024,256]{2,1,0:T(8,128)(2,1)S(1)} %get-tuple-element.35, bf16[2,1024,256]{2,1,0:T(8,128)(2,1)S(1)} %get-tuple-element.36, bf16[2,1024,256]{2,1,0:T(8,128)(2,1)S(1)} %get-tuple-element.34), kind=kOutput, calls=%fused_computation.87 | convolution fusion | flops 1654800384 | bytes 5275648 | tf_op jit(solution)/shard_map/ip,rpj->rij/dot_general | solution.py:74
  26.7 0.0 all-gather.3.cloned.1.call-update
  26.7 0.0 all-gather.5.cloned.1.call-start
  26.8 2.6 %fusion.116 = (f32[256,512]{1,0:T(8,128)S(1)}, f32[256,512]{1,0:T(8,128)S(1)}, f32[256,512]{1,0:T(8,128)S(1)}, f32[256,512]{1,0:T(8,128)S(1)}, f32[256,512]{1,0:...) fusion(f32[256,4096]{1,0:T(8,128)} %param.7), kind=kLoop, calls=%fused_computation.161 | loop fusion | bytes 8388608 | tf_op jit(solution)/shard_map/slice | solution.py:94
  29.4 0.0 copy-start.2
  29.4 0.0 copy-start.4
  29.4 0.3 fusion.65
  29.7 0.5 copy-done.2
  30.2 0.1 copy-done.4
  30.4 1.1 collective-permute-start.2
  31.5 46.1 %collective-permute-done.2 = f32[256,2048]{1,0:T(8,128)} collective-permute-done((f32[256,2048]{1,0:T(8,128)S(1)}, f32[256,2048]{1,0:T(8,128)}, u32[]{:S(2)}, u32[]{:S(2)}) %collective-permute-start.2) | collective-permute-done | bytes 2097184 | tf_op jit(solution)/shard_map/ppermute | solution.py:98
  77.6 3.0 %all-gather.3.cloned.1.call-done = f32[2,520,2048]{2,1,0:T(8,128)} async-done(((f32[2,520,256]{2,1,0:T(8,128)}), f32[2,520,2048]{2,1,0:T(8,128)}) %all-gather.3.cloned.1.call-update) | async-done | bytes 8519696 | tf_op jit(solution)/shard_map/all_gather | solution.py:113
  80.7 6.9 %fusion.49 = f32[2,520,256]{2,1,0:T(8,128)S(1)} fusion(f32[2,520,2048]{2,1,0:T(8,128)} %all-gather.3.cloned.1.call-done, f32[256,2048]{1,0:T(8,128)} %collective-permute-done.2), kind=kOutput, calls=%fused_computation.79 | convolution fusion | flops 3271557120 | bytes 11681792 | tf_op jit(solution)/shard_map/rik,jk->rij/dot_general | solution.py:115
  87.6 1.5 collective-permute-start.3
  89.1 0.0 copy-done
  89.1 0.0 copy-done.3
  89.1 0.0 copy-done.5
  89.1 3.5 %fusion.51 = f32[2,520,256]{2,1,0:T(8,128)S(1)} fusion(f32[2,520,2048]{2,1,0:T(8,128)S(1)} %copy-done, f32[256,512]{1,0:T(8,128)S(1)} %copy-done.3, f32[256,512]{1,0:T(8,128)S(1)} %copy-done.5, f32[256,512]{1,0:T(8,128)S(1)} %get-tuple-element.16, f32[256,512]{1,0:T(8,128)S(1)} %get-tuple-element.17, f32[256,512]{1,0:T(8,128)S(1)} %get-tuple-element.18, ...), kind=kOutput, calls=%fused_computation.81 | convolution fusion | flops 3275227136 | bytes 13778945 | tf_op jit(solution)/shard_map/rik,jk->rij/dot_general | solution.py:114
  92.6 20.1 %collective-permute-done.3 = f32[2,520,256]{2,1,0:T(8,128)S(1)} collective-permute-done((f32[2,520,256]{2,1,0:T(8,128)S(1)}, f32[2,520,256]{2,1,0:T(8,128)S(1)}, u32[]{:S(2)}, u32[]{:S(2)}) %collective-permute-start.3) | collective-permute-done | bytes 1064992 | tf_op jit(solution)/shard_map/ppermute | solution.py:116
  112.7 1.1 add.216
  113.8 0.0 all-gather.5.cloned.1.call-update
  113.8 1.0 fusion.115
  114.8 3.2 %collective-permute-start.4 = (f32[2,4096]{1,0:T(2,128)S(1)}, f32[2,4096]{1,0:T(2,128)S(1)}, u32[]{:S(2)}, u32[]{:S(2)}) collective-permute-start(f32[2,4096]{1,0:T(2,128)S(1)} %get-tuple-element.13), channel_id=1, source_target_pairs={{0,16},{16,32},{32,48},{48,64},{64,80},{80,96},{96,112},{1,17},{17... | collective-permute-start | bytes 98312 | tf_op jit(solution)/shard_map/ppermute | solution.py:19
  118.1 1.3 collective-permute-start.5
  119.4 2.3 fusion.43
  121.7 0.0 collective-permute-done.4
  121.7 1.1 collective-permute-done.5
  122.7 11.0 %select_maximum_fusion = f32[520,4104]{1,0:T(8,128)S(1)} fusion(f32[2,4096]{1,0:T(2,128)S(1)} %collective-permute-done.5, f32[512,4096]{1,0:T(8,128)} %param.6, f32[2,4096]{1,0:T(2,128)S(1)} %collective-permute-done.4), kind=kLoop, calls=%fused_computation.2 | loop fusion | flops 27743040 | bytes 16990464 | tf_op jit(solution)/shard_map/concatenate | solution.py:17
  133.7 3.4 %fusion.114 = (f32[520,520]{1,0:T(8,128)S(1)}, f32[520,520]{1,0:T(8,128)S(1)}, f32[520,520]{1,0:T(8,128)}, f32[520,520]{1,0:T(8,128)}, f32[520,520]{1,0:T(8,128)...) fusion(f32[520,4104]{1,0:T(8,128)S(1)} %select_maximum_fusion), kind=kLoop, calls=%fused_computation.159 | loop fusion | bytes 17305600 | tf_op jit(solution)/shard_map/slice | solution.py:79
  137.1 11.6 %concatenate.62 = f32[520,4160]{1,0:T(8,128)} concatenate(f32[520,520]{1,0:T(8,128)} %get-tuple-element.12, f32[520,520]{1,0:T(8,128)} %get-tuple-element.11, f32[520,520]{1,0:T(8,128)} %get-tuple-element.10, f32[520,520]{1,0:T(8,128)} %get-tuple-element.9, f32[520,520]{1,0:T(8,128)} %get-tuple-element.8, f32[520,520]{1,0:T(8,128)} %get-tuple-element.7, ...), dimensions={1} | concatenate | bytes 17305600 | tf_op jit(solution)/shard_map/concatenate | solution.py:79
  148.7 73.9 %all-gather.5.cloned.1.call-done = f32[2,4160,256]{2,1,0:T(8,128)} async-done(((f32[2,520,256]{2,1,0:T(8,128)}), f32[2,4160,256]{2,1,0:T(8,128)}) %all-gather.5.cloned.1.call-update) | async-done | bytes 8519696 | tf_op jit(solution)/shard_map/all_gather | solution.py:118
  222.7 12.2 %fusion.62 = f32[2,520,256]{2,1,0:T(8,128)S(1)} fusion(f32[2,4160,256]{2,1,0:T(8,128)} %all-gather.5.cloned.1.call-done, f32[520,4160]{1,0:T(8,128)} %concatenate.62), kind=kOutput, calls=%fused_computation.88 | convolution fusion | flops 6645350400 | bytes 18237440 | tf_op jit(solution)/shard_map/ik,rkj->rij/dot_general | solution.py:117
  234.9 0.2 fusion.118
  235.1 0.2 copy.10
  235.3 3.2 %collective-permute-start.6 = (f32[2,520,2]{1,2,0:T(2,128)S(1)}, f32[2,520,2]{1,2,0:T(2,128)S(1)}, u32[]{:S(2)}, u32[]{:S(2)}) collective-permute-start(f32[2,520,2]{1,2,0:T(2,128)S(1)} %copy.10), channel_id=1, source_target_pairs={{0,1},{1,2},{2,3},{3,4},{4,5},{5,6},{6,7},{7,8},{8,9},{9,10},{10,1... | collective-permute-start | bytes 24968 | tf_op jit(solution)/shard_map/ppermute | solution.py:19
  238.5 0.2 copy.11
  238.7 2.1 collective-permute-start.7
  240.9 0.4 fusion.77
  241.3 0.0 collective-permute-done.6
  241.3 0.2 copy.12
  241.5 2.2 collective-permute-done.7
  243.7 0.2 copy.13
  244.0 0.0 copy-start.6
  244.0 0.7 reduce-precision_convert_fusion.7
  244.7 0.5 copy-done.6
  245.2 2.5 reduce-precision_convert_fusion.3
  247.7 0.0 copy-done.1
  247.7 0.3 copy-done.7
  248.1 4.0 %multiply_add_fusion = f32[2,1024,512]{2,1,0:T(8,128)} fusion(f32[2,1024,512]{2,1,0:T(8,128)S(1)} %copy-done.1, f32[1024,512]{1,0:T(8,128)S(1)} %copy-done.7, bf16[2,1024,260]{1,2,0:T(8,128)(2,1)S(1)} %get-tuple-element.29, bf16[2,1024,260]{1,2,0:T(8,128)(2,1)S(1)} %get-tuple-element.30, bf16[2,1024,260]{1,2,0:T(8,128)(2,1)S(1)} %get-tuple-element.28, ...), kind=kOutput, calls=%fused_computation.20 | convolution fusion | flops 1649856512 | bytes 13946880 | tf_op jit(solution)/shard_map/rpj,jq->rpq/dot_general | solution.py:72
  (13 shorter events, 0.1 us)
Async XLA Ops:
  6.5 74.1 %all-gather.3.cloned.1.call-start = ((), (), s32[]{:S(2)}) async-start(), calls=%async_computation | async-start | bytes 9584640 | tf_op jit(solution)/shard_map/all_gather | solution.py:113
  8.8 11.8 %collective-permute-start = (f32[2,1024,4]{1,2,0:T(4,128)S(1)}, f32[2,1024,4]{1,2,0:T(4,128)S(1)}, u32[]{:S(2)}, u32[]{:S(2)}) collective-permute-start(f32[2,1024,4]{1,2,0:T(4,128)S(1)} %copy.16), channel_id=1, source_target_pairs={{0,1},{1,2},{2,3},{3,4},{4,5},{5,6},{6,7},{7,8},{8,9},{9,10},{10,1... | collective-permute-start | bytes 98312 | tf_op jit(solution)/shard_map/ppermute | solution.py:33
  13.7 7.4 %collective-permute-start.1 = (f32[2,1024,4]{1,2,0:T(4,128)S(1)}, f32[2,1024,4]{1,2,0:T(4,128)S(1)}, u32[]{:S(2)}, u32[]{:S(2)}) collective-permute-start(f32[2,1024,4]{1,2,0:T(4,128)S(1)} %copy.17), channel_id=1, source_target_pairs={{1,0},{2,1},{3,2},{4,3},{5,4},{6,5},{7,6},{8,7},{9,8},{10,9},{11,1... | collective-permute-start | bytes 98312 | tf_op jit(solution)/shard_map/ppermute | solution.py:34
  26.7 196.0 %all-gather.5.cloned.1.call-start = ((), (), s32[]{:S(2)}) async-start(), calls=%async_computation.1 | async-start | bytes 9584640 | tf_op jit(solution)/shard_map/all_gather | solution.py:118
  29.4 0.8 copy-start.2
  29.4 1.0 copy-start.4
  30.4 47.2 %collective-permute-start.2 = (f32[256,2048]{1,0:T(8,128)S(1)}, f32[256,2048]{1,0:T(8,128)}, u32[]{:S(2)}, u32[]{:S(2)}) collective-permute-start(f32[256,2048]{1,0:T(8,128)S(1)} %fusion.65), channel_id=1, source_target_pairs={{0,2},{2,0},{1,3},{3,1},{4,6},{6,4},{5,7},{7,5},{8,10},{10,8},{9,1... | collective-permute-start | bytes 6291464 | tf_op jit(solution)/shard_map/ppermute | solution.py:98
  80.6 8.4 %copy-start = (f32[2,520,2048]{2,1,0:T(8,128)S(1)}, f32[2,520,2048]{2,1,0:T(8,128)}, u32[]{:S(2)}) copy-start(f32[2,520,2048]{2,1,0:T(8,128)} %all-gather.3.cloned.1.call-done) | copy-start | bytes 25559044
  80.6 8.4 %copy-start.3 = (f32[256,512]{1,0:T(8,128)S(1)}, f32[256,512]{1,0:T(8,128)}, u32[]{:S(2)}) copy-start(f32[256,512]{1,0:T(8,128)} %copy-done.2) | copy-start | bytes 1572868
  80.6 8.4 %copy-start.5 = (f32[256,512]{1,0:T(8,128)S(1)}, f32[256,512]{1,0:T(8,128)}, u32[]{:S(2)}) copy-start(f32[256,512]{1,0:T(8,128)} %copy-done.4) | copy-start | bytes 1572868
  87.6 25.1 %collective-permute-start.3 = (f32[2,520,256]{2,1,0:T(8,128)S(1)}, f32[2,520,256]{2,1,0:T(8,128)S(1)}, u32[]{:S(2)}, u32[]{:S(2)}) collective-permute-start(f32[2,520,256]{2,1,0:T(8,128)S(1)} %fusion.49), channel_id=1, source_target_pairs={{0,2},{2,0},{1,3},{3,1},{4,6},{6,4},{5,7},{7,5},{8,10},{10,8},{9,1... | collective-permute-start | bytes 3194888 | tf_op jit(solution)/shard_map/ppermute | solution.py:116
  114.8 6.8 %collective-permute-start.4 = (f32[2,4096]{1,0:T(2,128)S(1)}, f32[2,4096]{1,0:T(2,128)S(1)}, u32[]{:S(2)}, u32[]{:S(2)}) collective-permute-start(f32[2,4096]{1,0:T(2,128)S(1)} %get-tuple-element.13), channel_id=1, source_target_pairs={{0,16},{16,32},{32,48},{48,64},{64,80},{80,96},{96,112},{1,17},{17... | collective-permute-start | bytes 98312 | tf_op jit(solution)/shard_map/ppermute | solution.py:19
  118.1 4.7 %collective-permute-start.5 = (f32[2,4096]{1,0:T(2,128)S(1)}, f32[2,4096]{1,0:T(2,128)S(1)}, u32[]{:S(2)}, u32[]{:S(2)}) collective-permute-start(f32[2,4096]{1,0:T(2,128)S(1)} %get-tuple-element.14), channel_id=1, source_target_pairs={{16,0},{32,16},{48,32},{64,48},{80,64},{96,80},{112,96},{17,1},{33... | collective-permute-start | bytes 98312 | tf_op jit(solution)/shard_map/ppermute | solution.py:21
  235.3 5.9 %collective-permute-start.6 = (f32[2,520,2]{1,2,0:T(2,128)S(1)}, f32[2,520,2]{1,2,0:T(2,128)S(1)}, u32[]{:S(2)}, u32[]{:S(2)}) collective-permute-start(f32[2,520,2]{1,2,0:T(2,128)S(1)} %copy.10), channel_id=1, source_target_pairs={{0,1},{1,2},{2,3},{3,4},{4,5},{5,6},{6,7},{7,8},{8,9},{9,10},{10,1... | collective-permute-start | bytes 24968 | tf_op jit(solution)/shard_map/ppermute | solution.py:19
  238.7 5.0 %collective-permute-start.7 = (f32[2,520,2]{1,2,0:T(2,128)S(1)}, f32[2,520,2]{1,2,0:T(2,128)S(1)}, u32[]{:S(2)}, u32[]{:S(2)}) collective-permute-start(f32[2,520,2]{1,2,0:T(2,128)S(1)} %copy.11), channel_id=1, source_target_pairs={{1,0},{2,1},{3,2},{4,3},{5,4},{6,5},{7,6},{8,7},{9,8},{10,9},{11,1... | collective-permute-start | bytes 24968 | tf_op jit(solution)/shard_map/ppermute | solution.py:21
  244.0 1.2 copy-start.6
  245.2 2.5 copy-start.1
  245.2 2.9 %copy-start.7 = (f32[1024,512]{1,0:T(8,128)S(1)}, f32[1024,512]{1,0:T(8,128)}, u32[]{:S(2)}) copy-start(f32[1024,512]{1,0:T(8,128)} %param.5) | copy-start | bytes 6291460
Sparse Core Ops, SparseCore 0:
  26.8 53.7 all-gather.2
  114.0 108.6 all-gather.4

commit v3 on v2

--- a/solution.py
+++ b/solution.py
@@ -102,6 +102,7 @@
     order = [h * depth + d for d in range(depth) for h in range(halves_n)]
     row_big = row_windows(row_rows, order, tile_rows, ext_rows)
     before, after = edges(observed, cols_axis, 2, 4)
+    noisy = lax.optimization_barrier(noise_var[None] * observed)
     col_adj = tap_table(2 * tile_cols + 8, tile_cols, False, 4)
     row_adj = tap_table(ext_rows, 2 * tile_rows, True, 2)
     colsum = (
@@ -122,7 +123,7 @@
     col_fwd = tap_table(tile_cols + 4, 2 * tile_cols, True, 2)
     rowpass = exact_dot("pi,rij->rpj", coarse_ext, row_fwd, False)
     result = exact_dot("rpj,jq->rpq", rowpass, col_fwd, True)
-    return result + noise_var[None] * observed
+    return result + noisy
 
 
 def solution(mesh):

time: 260 us -> 263 us (1.012)
  other arithmetic: 20.6 us -> 23.8 us
    convert_element_type x4, other arithmetic: 3.94 us -> 7.1 us  [split3(): hi.astype(jnp.bfloat16)]
  transfers between devices with their start and end apart: 10 -> 10, of which waited for: 6 -> 6; matrix products, arithmetic and copies ran while one was open for 16% -> 17% of each run, Pallas kernels for 0% -> 0%
where the time goes in v3:
time: 263 us; the launch traced here: 262 us
  waiting for transfers between devices  146 us (56%)
  matrix products  35.1 us (13%)
  other arithmetic  23.8 us (9%)
  local copies, waits for them, and re-layouts  23.6 us (9%)
  starting transfers between devices  19 us (7%)
  between operations  13.7 us (5%)
    all_gather x1, waiting for transfers between devices, body(): lax.all_gather(mixed, ('z', 'yh'), axis=1, tiled=True)  73.9 us
    ppermute x1, waiting for transfers between devices, body(): partner_cols = lax.ppermute(far_cols, 'yl', swap)  46.1 us
    ppermute x1, waiting for transfers between devices, body(): mixed = near + lax.ppermute(for_partner, 'yl', swap)  20.1 us
    dot_general x1, matrix products, body(): jnp.einsum('ik,rkj->rij', row_big, lax.all_gather(mixed, ('z', 'yh'), axi...  12.2 us
    concatenate x1, local copies, waits for them, and re-layouts, row_windows(): jnp.concatenate([padded[:, block * w:block * w + width] for w in order],...  11.6 us
    concatenate x1, other arithmetic, with_halo(): jnp.concatenate([lax.ppermute(tail, axis, [(i, (i + 1) % count) for i in...  11 us
    dot_general x4, matrix products, exact_dot(): jnp.einsum(eq, parts, jnp.concatenate([table] * 3, axis=0), preferred_ele...  7.12 us
    convert_element_type x4, other arithmetic, split3(): hi.astype(jnp.bfloat16)  7.1 us
  transfers between devices with their start and end apart: 10, of which 6 were waited for; matrix products, arithmetic and copies ran while one was open for 17% of the time, Pallas kernels for 0%

profile of v3, /device:TPU:1, one launch (start us, length us, event | category | flops | bytes accessed | tf_op | source)
XLA Modules:
  0.0 261.6 jit_solution(6647238779713989489)
XLA Ops:
  6.5 0.0 all-gather.3.cloned.1.call-start
  6.5 1.9 fusion.118
  8.4 0.3 copy.16
  8.8 4.6 %collective-permute-start = (f32[2,1024,4]{1,2,0:T(4,128)S(1)}, f32[2,1024,4]{1,2,0:T(4,128)S(1)}, u32[]{:S(2)}, u32[]{:S(2)}) collective-permute-start(f32[2,1024,4]{1,2,0:T(4,128)S(1)} %copy.16), channel_id=1, source_target_pairs={{0,1},{1,2},{2,3},{3,4},{4,5},{5,6},{6,7},{7,8},{8,9},{9,10},{10,1... | collective-permute-start | bytes 98312 | tf_op jit(solution)/shard_map/ppermute | solution.py:33
  13.4 0.3 copy.17
  13.7 1.9 collective-permute-start.1
  15.7 0.4 fusion.83
  16.0 6.3 %reduce-precision_convert_fusion.1 = (bf16[2,1024,512]{2,1,0:T(8,128)(2,1)S(1)}, bf16[2,1024,512]{2,1,0:T(8,128)(2,1)S(1)}, bf16[2,1024,512]{2,1,0:T(8,128)(2,1)S(1)}, f32[2,1024,512]{2,1,0:T(8,128)}) fusion(f32[2,1024,512]{2,1,0:T(8,128)} %param.4, f32[1024,512]{1,0:T(8,128)} %param.5), kind=kLoop, calls=%fused_computation.18 | loop fusion | flops 8388608 | bytes 16777216 | tf_op jit(solution)/shard_map/convert_element_type | solution.py:64
  22.4 1.3 fusion.40
  23.7 0.1 slice.112
  23.7 0.0 collective-permute-done
  23.8 0.5 fusion.86
  24.3 0.0 collective-permute-done.1
  24.3 0.5 fusion.92
  24.8 2.2 reduce-precision_convert_fusion.5
  27.0 2.8 %fusion.60 = f32[2,520,256]{2,1,0:T(8,128)} fusion(bf16[520,1024]{1,0:T(8,128)(2,1)S(1)} %fusion.40, bf16[2,1024,256]{2,1,0:T(8,128)(2,1)S(1)} %get-tuple-element.36, bf16[2,1024,256]{2,1,0:T(8,128)(2,1)S(1)} %get-tuple-element.37, bf16[2,1024,256]{2,1,0:T(8,128)(2,1)S(1)} %get-tuple-element.35), kind=kOutput, calls=%fused_computation.88 | convolution fusion | flops 1654800384 | bytes 5275648 | tf_op jit(solution)/shard_map/ip,rpj->rij/dot_general | solution.py:74
  29.8 0.0 all-gather.3.cloned.1.call-update
  29.8 0.0 all-gather.5.cloned.1.call-start
  29.9 2.6 fusion.117
  32.5 0.0 copy-start.1
  32.5 0.0 copy-start.3
  32.5 0.3 fusion.66
  32.8 0.5 copy-done.1
  33.4 0.1 copy-done.3
  33.5 1.1 collective-permute-start.2
  34.6 46.1 %collective-permute-done.2 = f32[256,2048]{1,0:T(8,128)} collective-permute-done((f32[256,2048]{1,0:T(8,128)S(1)}, f32[256,2048]{1,0:T(8,128)}, u32[]{:S(2)}, u32[]{:S(2)}) %collective-permute-start.2) | collective-permute-done | bytes 2097184 | tf_op jit(solution)/shard_map/ppermute | solution.py:98
  80.8 3.0 %all-gather.3.cloned.1.call-done = f32[2,520,2048]{2,1,0:T(8,128)} async-done(((f32[2,520,256]{2,1,0:T(8,128)}), f32[2,520,2048]{2,1,0:T(8,128)}) %all-gather.3.cloned.1.call-update) | async-done | bytes 8519696 | tf_op jit(solution)/shard_map/all_gather | solution.py:114
  83.8 0.0 copy-start
  83.8 6.9 %fusion.49 = f32[2,520,256]{2,1,0:T(8,128)S(1)} fusion(f32[2,520,2048]{2,1,0:T(8,128)} %all-gather.3.cloned.1.call-done, f32[256,2048]{1,0:T(8,128)} %collective-permute-done.2), kind=kOutput, calls=%fused_computation.78 | convolution fusion | flops 3271557120 | bytes 11681792 | tf_op jit(solution)/shard_map/rik,jk->rij/dot_general | solution.py:116
  90.7 1.5 collective-permute-start.3
  92.2 0.0 copy-done
  92.2 0.0 copy-done.2
  92.2 0.0 copy-done.4
  92.2 3.5 %fusion.51 = f32[2,520,256]{2,1,0:T(8,128)S(1)} fusion(f32[2,520,2048]{2,1,0:T(8,128)S(1)} %copy-done, f32[256,512]{1,0:T(8,128)S(1)} %copy-done.2, f32[256,512]{1,0:T(8,128)S(1)} %copy-done.4, f32[256,512]{1,0:T(8,128)S(1)} %get-tuple-element.16, f32[256,512]{1,0:T(8,128)S(1)} %get-tuple-element.17, f32[256,512]{1,0:T(8,128)S(1)} %get-tuple-element.18, ...), kind=kOutput, calls=%fused_computation.80 | convolution fusion | flops 3275227136 | bytes 13778945 | tf_op jit(solution)/shard_map/rik,jk->rij/dot_general | solution.py:115
  95.7 20.1 %collective-permute-done.3 = f32[2,520,256]{2,1,0:T(8,128)S(1)} collective-permute-done((f32[2,520,256]{2,1,0:T(8,128)S(1)}, f32[2,520,256]{2,1,0:T(8,128)S(1)}, u32[]{:S(2)}, u32[]{:S(2)}) %collective-permute-start.3) | collective-permute-done | bytes 1064992 | tf_op jit(solution)/shard_map/ppermute | solution.py:117
  115.8 1.1 add.216
  116.9 0.0 all-gather.5.cloned.1.call-update
  116.9 1.0 fusion.116
  117.9 3.2 %collective-permute-start.4 = (f32[2,4096]{1,0:T(2,128)S(1)}, f32[2,4096]{1,0:T(2,128)S(1)}, u32[]{:S(2)}, u32[]{:S(2)}) collective-permute-start(f32[2,4096]{1,0:T(2,128)S(1)} %get-tuple-element.13), channel_id=1, source_target_pairs={{0,16},{16,32},{32,48},{48,64},{64,80},{80,96},{96,112},{1,17},{17... | collective-permute-start | bytes 98312 | tf_op jit(solution)/shard_map/ppermute | solution.py:19
  121.2 1.3 collective-permute-start.5
  122.5 2.3 fusion.43
  124.8 0.0 collective-permute-done.4
  124.8 1.1 collective-permute-done.5
  125.8 11.0 %select_maximum_fusion = f32[520,4104]{1,0:T(8,128)S(1)} fusion(f32[2,4096]{1,0:T(2,128)S(1)} %collective-permute-done.5, f32[512,4096]{1,0:T(8,128)} %param.6, f32[2,4096]{1,0:T(2,128)S(1)} %collective-permute-done.4), kind=kLoop, calls=%fused_computation.2 | loop fusion | flops 27743040 | bytes 16990464 | tf_op jit(solution)/shard_map/concatenate | solution.py:17
  136.8 3.4 %fusion.115 = (f32[520,520]{1,0:T(8,128)S(1)}, f32[520,520]{1,0:T(8,128)S(1)}, f32[520,520]{1,0:T(8,128)}, f32[520,520]{1,0:T(8,128)}, f32[520,520]{1,0:T(8,128)...) fusion(f32[520,4104]{1,0:T(8,128)S(1)} %select_maximum_fusion), kind=kLoop, calls=%fused_computation.160 | loop fusion | bytes 17305600 | tf_op jit(solution)/shard_map/slice | solution.py:79
  140.2 11.6 %concatenate.62 = f32[520,4160]{1,0:T(8,128)} concatenate(f32[520,520]{1,0:T(8,128)} %get-tuple-element.12, f32[520,520]{1,0:T(8,128)} %get-tuple-element.11, f32[520,520]{1,0:T(8,128)} %get-tuple-element.10, f32[520,520]{1,0:T(8,128)} %get-tuple-element.9, f32[520,520]{1,0:T(8,128)} %get-tuple-element.8, f32[520,520]{1,0:T(8,128)} %get-tuple-element.7, ...), dimensions={1} | concatenate | bytes 17305600 | tf_op jit(solution)/shard_map/concatenate | solution.py:79
  151.9 73.9 %all-gather.5.cloned.1.call-done = f32[2,4160,256]{2,1,0:T(8,128)} async-done(((f32[2,520,256]{2,1,0:T(8,128)}), f32[2,4160,256]{2,1,0:T(8,128)}) %all-gather.5.cloned.1.call-update) | async-done | bytes 8519696 | tf_op jit(solution)/shard_map/all_gather | solution.py:119
  225.8 12.2 %fusion.63 = f32[2,520,256]{2,1,0:T(8,128)S(1)} fusion(f32[2,4160,256]{2,1,0:T(8,128)} %all-gather.5.cloned.1.call-done, f32[520,4160]{1,0:T(8,128)} %concatenate.62), kind=kOutput, calls=%fused_computation.89 | convolution fusion | flops 6645350400 | bytes 18237440 | tf_op jit(solution)/shard_map/ik,rkj->rij/dot_general | solution.py:118
  238.0 0.2 fusion.119
  238.2 0.2 copy.10
  238.4 3.2 %collective-permute-start.6 = (f32[2,520,2]{1,2,0:T(2,128)S(1)}, f32[2,520,2]{1,2,0:T(2,128)S(1)}, u32[]{:S(2)}, u32[]{:S(2)}) collective-permute-start(f32[2,520,2]{1,2,0:T(2,128)S(1)} %copy.10), channel_id=1, source_target_pairs={{0,1},{1,2},{2,3},{3,4},{4,5},{5,6},{6,7},{7,8},{8,9},{9,10},{10,1... | collective-permute-start | bytes 24968 | tf_op jit(solution)/shard_map/ppermute | solution.py:19
  241.6 0.2 copy.11
  241.8 2.1 collective-permute-start.7
  244.0 0.4 fusion.78
  244.4 0.0 collective-permute-done.6
  244.4 0.2 copy.12
  244.6 2.2 collective-permute-done.7
  246.8 0.2 copy.13
  247.1 0.0 copy-start.6
  247.1 0.7 reduce-precision_convert_fusion.7
  247.8 0.5 copy-done.6
  248.3 2.5 reduce-precision_convert_fusion.3
  250.8 0.0 copy-done.5
  250.8 3.9 %fusion.54 = f32[2,1024,512]{2,1,0:T(8,128)} fusion(f32[2,1024,512]{2,1,0:T(8,128)S(1)} %copy-done.5, bf16[2,1024,260]{1,2,0:T(8,128)(2,1)S(1)} %get-tuple-element.30, bf16[2,1024,260]{1,2,0:T(8,128)(2,1)S(1)} %get-tuple-element.31, bf16[2,1024,260]{1,2,0:T(8,128)(2,1)S(1)} %get-tuple-element.29, bf16[260,512]{1,0:T(8,128)(2,1)S(1)} %fusion.78), kind=kOutput, calls=%fused_computation.85 | convolution fusion | flops 1648807936 | bytes 11849728 | tf_op jit(solution)/shard_map/rpj,jq->rpq/dot_general | solution.py:72
  (11 shorter events, 0.1 us)
Async XLA Ops:
  6.5 77.2 %all-gather.3.cloned.1.call-start = ((), (), s32[]{:S(2)}) async-start(), calls=%async_computation | async-start | bytes 9584640 | tf_op jit(solution)/shard_map/all_gather | solution.py:114
  8.8 15.0 %collective-permute-start = (f32[2,1024,4]{1,2,0:T(4,128)S(1)}, f32[2,1024,4]{1,2,0:T(4,128)S(1)}, u32[]{:S(2)}, u32[]{:S(2)}) collective-permute-start(f32[2,1024,4]{1,2,0:T(4,128)S(1)} %copy.16), channel_id=1, source_target_pairs={{0,1},{1,2},{2,3},{3,4},{4,5},{5,6},{6,7},{7,8},{8,9},{9,10},{10,1... | collective-permute-start | bytes 98312 | tf_op jit(solution)/shard_map/ppermute | solution.py:33
  13.7 10.6 %collective-permute-start.1 = (f32[2,1024,4]{1,2,0:T(4,128)S(1)}, f32[2,1024,4]{1,2,0:T(4,128)S(1)}, u32[]{:S(2)}, u32[]{:S(2)}) collective-permute-start(f32[2,1024,4]{1,2,0:T(4,128)S(1)} %copy.17), channel_id=1, source_target_pairs={{1,0},{2,1},{3,2},{4,3},{5,4},{6,5},{7,6},{8,7},{9,8},{10,9},{11,1... | collective-permute-start | bytes 98312 | tf_op jit(solution)/shard_map/ppermute | solution.py:34
  29.8 195.9 %all-gather.5.cloned.1.call-start = ((), (), s32[]{:S(2)}) async-start(), calls=%async_computation.1 | async-start | bytes 9584640 | tf_op jit(solution)/shard_map/all_gather | solution.py:119
  32.5 0.8 copy-start.1
  32.5 1.0 copy-start.3
  33.5 47.2 %collective-permute-start.2 = (f32[256,2048]{1,0:T(8,128)S(1)}, f32[256,2048]{1,0:T(8,128)}, u32[]{:S(2)}, u32[]{:S(2)}) collective-permute-start(f32[256,2048]{1,0:T(8,128)S(1)} %fusion.66), channel_id=1, source_target_pairs={{0,2},{2,0},{1,3},{3,1},{4,6},{6,4},{5,7},{7,5},{8,10},{10,8},{9,1... | collective-permute-start | bytes 6291464 | tf_op jit(solution)/shard_map/ppermute | solution.py:98
  83.8 8.4 %copy-start = (f32[2,520,2048]{2,1,0:T(8,128)S(1)}, f32[2,520,2048]{2,1,0:T(8,128)}, u32[]{:S(2)}) copy-start(f32[2,520,2048]{2,1,0:T(8,128)} %all-gather.3.cloned.1.call-done) | copy-start | bytes 25559044
  83.8 8.4 %copy-start.2 = (f32[256,512]{1,0:T(8,128)S(1)}, f32[256,512]{1,0:T(8,128)}, u32[]{:S(2)}) copy-start(f32[256,512]{1,0:T(8,128)} %copy-done.1) | copy-start | bytes 1572868
  83.8 8.4 %copy-start.4 = (f32[256,512]{1,0:T(8,128)S(1)}, f32[256,512]{1,0:T(8,128)}, u32[]{:S(2)}) copy-start(f32[256,512]{1,0:T(8,128)} %copy-done.3) | copy-start | bytes 1572868
  90.7 25.1 %collective-permute-start.3 = (f32[2,520,256]{2,1,0:T(8,128)S(1)}, f32[2,520,256]{2,1,0:T(8,128)S(1)}, u32[]{:S(2)}, u32[]{:S(2)}) collective-permute-start(f32[2,520,256]{2,1,0:T(8,128)S(1)} %fusion.49), channel_id=1, source_target_pairs={{0,2},{2,0},{1,3},{3,1},{4,6},{6,4},{5,7},{7,5},{8,10},{10,8},{9,1... | collective-permute-start | bytes 3194888 | tf_op jit(solution)/shard_map/ppermute | solution.py:117
  117.9 6.8 %collective-permute-start.4 = (f32[2,4096]{1,0:T(2,128)S(1)}, f32[2,4096]{1,0:T(2,128)S(1)}, u32[]{:S(2)}, u32[]{:S(2)}) collective-permute-start(f32[2,4096]{1,0:T(2,128)S(1)} %get-tuple-element.13), channel_id=1, source_target_pairs={{0,16},{16,32},{32,48},{48,64},{64,80},{80,96},{96,112},{1,17},{17... | collective-permute-start | bytes 98312 | tf_op jit(solution)/shard_map/ppermute | solution.py:19
  121.2 4.7 %collective-permute-start.5 = (f32[2,4096]{1,0:T(2,128)S(1)}, f32[2,4096]{1,0:T(2,128)S(1)}, u32[]{:S(2)}, u32[]{:S(2)}) collective-permute-start(f32[2,4096]{1,0:T(2,128)S(1)} %get-tuple-element.14), channel_id=1, source_target_pairs={{16,0},{32,16},{48,32},{64,48},{80,64},{96,80},{112,96},{17,1},{33... | collective-permute-start | bytes 98312 | tf_op jit(solution)/shard_map/ppermute | solution.py:21
  238.4 5.9 %collective-permute-start.6 = (f32[2,520,2]{1,2,0:T(2,128)S(1)}, f32[2,520,2]{1,2,0:T(2,128)S(1)}, u32[]{:S(2)}, u32[]{:S(2)}) collective-permute-start(f32[2,520,2]{1,2,0:T(2,128)S(1)} %copy.10), channel_id=1, source_target_pairs={{0,1},{1,2},{2,3},{3,4},{4,5},{5,6},{6,7},{7,8},{8,9},{9,10},{10,1... | collective-permute-start | bytes 24968 | tf_op jit(solution)/shard_map/ppermute | solution.py:19
  241.8 5.0 %collective-permute-start.7 = (f32[2,520,2]{1,2,0:T(2,128)S(1)}, f32[2,520,2]{1,2,0:T(2,128)S(1)}, u32[]{:S(2)}, u32[]{:S(2)}) collective-permute-start(f32[2,520,2]{1,2,0:T(2,128)S(1)} %copy.11), channel_id=1, source_target_pairs={{1,0},{2,1},{3,2},{4,3},{5,4},{6,5},{7,6},{8,7},{9,8},{10,9},{11,1... | collective-permute-start | bytes 24968 | tf_op jit(solution)/shard_map/ppermute | solution.py:21
  247.1 1.2 copy-start.6
  248.3 2.5 copy-start.5
Sparse Core Ops, SparseCore 0:
  30.0 53.7 all-gather.2
  117.1 108.6 all-gather.4

commit v4 on v2

--- a/solution.py
+++ b/solution.py
@@ -117,10 +117,12 @@
     product = jnp.einsum(
         "ik,rkj->rij", row_big, lax.all_gather(mixed, ("z", "yh"), axis=1, tiled=True), precision=highest
     )
-    coarse_ext = with_halo(product, ((cols_axis, 2),), 2)
+    before, after = edges(product, cols_axis, 2, 2)
     row_fwd = tap_table(2 * tile_rows, ext_rows, False, 2)
     col_fwd = tap_table(tile_cols + 4, 2 * tile_cols, True, 2)
-    rowpass = exact_dot("pi,rij->rpj", coarse_ext, row_fwd, False)
+    rowpass = jnp.concatenate(
+        [exact_dot("pi,rij->rpj", cells, row_fwd, False) for cells in (before, product, after)], axis=2
+    )
     result = exact_dot("rpj,jq->rpq", rowpass, col_fwd, True)
     return result + noise_var[None] * observed
 

time: 260 us -> 262 us (level)
  matrix products: 35.2 us -> 38.5 us
  waiting for transfers between devices: 147 us -> 144 us
    ppermute x1 -> x2, starting transfers between devices: 4.6 us -> 7.78 us  [edges(): before = lax.ppermute(tail, axis, [(i, i + 1) for i in range(ends)])]
    ppermute x2 -> x1, starting transfers between devices: 6.4 us -> 3.22 us  [with_halo(): lax.ppermute(tail, axis, [(i, (i + 1) % count) for i in range(ends)])]
    dot_general x2 -> x4, matrix products: 5.31 us -> 7.61 us  [exact_dot(): jnp.einsum(eq, jnp.concatenate([table] * 3, axis=1), parts, preferred_ele...]
  transfers between devices with their start and end apart: 10 -> 10, of which waited for: 6 -> 5; matrix products, arithmetic and copies ran while one was open for 16% -> 18% of each run, Pallas kernels for 0% -> 0%
where the time goes in v4:
time: 262 us; the launch traced here: 260 us
  waiting for transfers between devices  144 us (55%)
  matrix products  38.5 us (15%)
  local copies, waits for them, and re-layouts  24.5 us (9%)
  other arithmetic  20.6 us (8%)
  starting transfers between devices  19 us (7%)
  between operations  13.7 us (5%)
    all_gather x1, waiting for transfers between devices, body(): lax.all_gather(mixed, ('z', 'yh'), axis=1, tiled=True)  74 us
    ppermute x1, waiting for transfers between devices, body(): partner_cols = lax.ppermute(far_cols, 'yl', swap)  46.1 us
    ppermute x1, waiting for transfers between devices, body(): mixed = near + lax.ppermute(for_partner, 'yl', swap)  20.1 us
    dot_general x1, matrix products, body(): jnp.einsum('ik,rkj->rij', row_big, lax.all_gather(mixed, ('z', 'yh'), axi...  13.2 us
    concatenate x1, local copies, waits for them, and re-layouts, row_windows(): jnp.concatenate([padded[:, block * w:block * w + width] for w in order],...  11.6 us
    concatenate x1, other arithmetic, with_halo(): jnp.concatenate([lax.ppermute(tail, axis, [(i, (i + 1) % count) for i in...  11 us
    ppermute x2, starting transfers between devices, edges(): before = lax.ppermute(tail, axis, [(i, i + 1) for i in range(ends)])  7.78 us
    dot_general x4, matrix products, exact_dot(): jnp.einsum(eq, jnp.concatenate([table] * 3, axis=1), parts, preferred_ele...  7.61 us
  transfers between devices with their start and end apart: 10, of which 5 were waited for; matrix products, arithmetic and copies ran while one was open for 18% of the time, Pallas kernels for 0%

profile of v4, /device:TPU:1, one launch (start us, length us, event | category | flops | bytes accessed | tf_op | source)
XLA Modules:
  0.0 260.2 jit_solution(15387333040728555784)
XLA Ops:
  6.5 0.0 all-gather.3.cloned.1.call-start
  6.5 1.9 fusion.122
  8.4 0.3 copy.13
  8.8 4.6 %collective-permute-start = (f32[2,1024,4]{1,2,0:T(4,128)S(1)}, f32[2,1024,4]{1,2,0:T(4,128)S(1)}, u32[]{:S(2)}, u32[]{:S(2)}) collective-permute-start(f32[2,1024,4]{1,2,0:T(4,128)S(1)} %copy.13), channel_id=1, source_target_pairs={{0,1},{1,2},{2,3},{3,4},{4,5},{5,6},{6,7},{7,8},{8,9},{9,10},{10,1... | collective-permute-start | bytes 98312 | tf_op jit(solution)/shard_map/ppermute | solution.py:33
  13.4 0.3 copy.14
  13.7 1.9 collective-permute-start.1
  15.6 3.2 %reduce-precision_convert_fusion.1 = (bf16[2,1024,512]{2,1,0:T(8,128)(2,1)S(1)}, bf16[2,1024,512]{2,1,0:T(8,128)(2,1)S(1)}, bf16[2,1024,512]{2,1,0:T(8,128)(2,1)S(1)}) fusion(f32[2,1024,512]{2,1,0:T(8,128)} %param.4), kind=kLoop, calls=%fused_computation.18 | loop fusion | flops 7340032 | bytes 10485760 | tf_op jit(solution)/shard_map/convert_element_type | solution.py:64
  18.9 0.4 fusion.83
  19.2 1.3 fusion.33
  20.5 0.1 slice.112
  20.6 0.0 collective-permute-done
  20.6 0.5 fusion.86
  21.1 0.0 collective-permute-done.1
  21.2 0.5 fusion.92
  21.6 2.3 reduce-precision_convert_fusion.5
  23.9 2.8 %fusion.57 = f32[2,520,256]{2,1,0:T(8,128)} fusion(bf16[520,1024]{1,0:T(8,128)(2,1)S(1)} %fusion.33, bf16[2,1024,256]{2,1,0:T(8,128)(2,1)S(1)} %get-tuple-element.32, bf16[2,1024,256]{2,1,0:T(8,128)(2,1)S(1)} %get-tuple-element.33, bf16[2,1024,256]{2,1,0:T(8,128)(2,1)S(1)} %get-tuple-element.31), kind=kOutput, calls=%fused_computation.85 | convolution fusion | flops 1654800384 | bytes 5275648 | tf_op jit(solution)/shard_map/ip,rpj->rij/dot_general | solution.py:74
  26.7 0.0 all-gather.3.cloned.1.call-update
  26.7 0.0 all-gather.5.cloned.1.call-start
  26.8 2.6 %fusion.121 = (f32[256,512]{1,0:T(8,128)S(1)}, f32[256,512]{1,0:T(8,128)S(1)}, f32[256,512]{1,0:T(8,128)S(1)}, f32[256,512]{1,0:T(8,128)S(1)}, f32[256,512]{1,0:...) fusion(f32[256,4096]{1,0:T(8,128)} %param.7), kind=kLoop, calls=%fused_computation.174 | loop fusion | bytes 8388608 | tf_op jit(solution)/shard_map/slice | solution.py:94
  29.4 0.0 copy-start.2
  29.4 0.3 fusion.63
  29.7 0.5 copy-done.2
  30.2 0.1 copy-done.4
  30.4 1.1 collective-permute-start.2
  31.5 46.1 %collective-permute-done.2 = f32[256,2048]{1,0:T(8,128)} collective-permute-done((f32[256,2048]{1,0:T(8,128)S(1)}, f32[256,2048]{1,0:T(8,128)}, u32[]{:S(2)}, u32[]{:S(2)}) %collective-permute-start.2) | collective-permute-done | bytes 2097184 | tf_op jit(solution)/shard_map/ppermute | solution.py:98
  77.6 3.0 %all-gather.3.cloned.1.call-done = f32[2,520,2048]{2,1,0:T(8,128)} async-done(((f32[2,520,256]{2,1,0:T(8,128)}), f32[2,520,2048]{2,1,0:T(8,128)}) %all-gather.3.cloned.1.call-update) | async-done | bytes 8519696 | tf_op jit(solution)/shard_map/all_gather | solution.py:113
  80.7 7.0 %fusion.42 = f32[2,520,256]{2,1,0:T(8,128)S(1)} fusion(f32[2,520,2048]{2,1,0:T(8,128)} %all-gather.3.cloned.1.call-done, f32[256,2048]{1,0:T(8,128)} %collective-permute-done.2), kind=kOutput, calls=%fused_computation.69 | convolution fusion | flops 3271557120 | bytes 11681792 | tf_op jit(solution)/shard_map/rik,jk->rij/dot_general | solution.py:115
  87.6 1.5 collective-permute-start.3
  89.1 0.0 copy-done.3
  89.1 3.5 %fusion.44 = f32[2,520,256]{2,1,0:T(8,128)S(1)} fusion(f32[2,520,2048]{2,1,0:T(8,128)S(1)} %copy-done, f32[256,512]{1,0:T(8,128)S(1)} %copy-done.3, f32[256,512]{1,0:T(8,128)S(1)} %copy-done.5, f32[256,512]{1,0:T(8,128)S(1)} %get-tuple-element.16, f32[256,512]{1,0:T(8,128)S(1)} %get-tuple-element.17, f32[256,512]{1,0:T(8,128)S(1)} %get-tuple-element.18, ...), kind=kOutput, calls=%fused_computation.71 | convolution fusion | flops 3275227136 | bytes 13778945 | tf_op jit(solution)/shard_map/rik,jk->rij/dot_general | solution.py:114
  92.7 20.1 %collective-permute-done.3 = f32[2,520,256]{2,1,0:T(8,128)S(1)} collective-permute-done((f32[2,520,256]{2,1,0:T(8,128)S(1)}, f32[2,520,256]{2,1,0:T(8,128)S(1)}, u32[]{:S(2)}, u32[]{:S(2)}) %collective-permute-start.3) | collective-permute-done | bytes 1064992 | tf_op jit(solution)/shard_map/ppermute | solution.py:116
  112.7 1.1 add.216
  113.9 0.0 all-gather.5.cloned.1.call-update
  113.9 1.0 fusion.120
  114.9 3.2 %collective-permute-start.4 = (f32[2,4096]{1,0:T(2,128)S(1)}, f32[2,4096]{1,0:T(2,128)S(1)}, u32[]{:S(2)}, u32[]{:S(2)}) collective-permute-start(f32[2,4096]{1,0:T(2,128)S(1)} %get-tuple-element.13), channel_id=1, source_target_pairs={{0,16},{16,32},{32,48},{48,64},{64,80},{80,96},{96,112},{1,17},{17... | collective-permute-start | bytes 98312 | tf_op jit(solution)/shard_map/ppermute | solution.py:19
  118.1 1.3 collective-permute-start.5
  119.4 2.3 fusion.36
  121.7 0.4 fusion.78
  122.1 0.0 collective-permute-done.4
  122.1 0.7 collective-permute-done.5
  122.8 11.0 %select_maximum_fusion = f32[520,4104]{1,0:T(8,128)S(1)} fusion(f32[2,4096]{1,0:T(2,128)S(1)} %collective-permute-done.5, f32[512,4096]{1,0:T(8,128)} %param.6, f32[2,4096]{1,0:T(2,128)S(1)} %collective-permute-done.4), kind=kLoop, calls=%fused_computation.2 | loop fusion | flops 27743040 | bytes 16990464 | tf_op jit(solution)/shard_map/concatenate | solution.py:17
  133.7 3.4 %fusion.119 = (f32[520,520]{1,0:T(8,128)S(1)}, f32[520,520]{1,0:T(8,128)S(1)}, f32[520,520]{1,0:T(8,128)}, f32[520,520]{1,0:T(8,128)}, f32[520,520]{1,0:T(8,128)...) fusion(f32[520,4104]{1,0:T(8,128)S(1)} %select_maximum_fusion), kind=kLoop, calls=%fused_computation.172 | loop fusion | bytes 17305600 | tf_op jit(solution)/shard_map/slice | solution.py:79
  137.1 11.6 %concatenate.70 = f32[520,4160]{1,0:T(8,128)} concatenate(f32[520,520]{1,0:T(8,128)} %get-tuple-element.12, f32[520,520]{1,0:T(8,128)} %get-tuple-element.11, f32[520,520]{1,0:T(8,128)} %get-tuple-element.10, f32[520,520]{1,0:T(8,128)} %get-tuple-element.9, f32[520,520]{1,0:T(8,128)} %get-tuple-element.8, f32[520,520]{1,0:T(8,128)} %get-tuple-element.7, ...), dimensions={1} | concatenate | bytes 17305600 | tf_op jit(solution)/shard_map/concatenate | solution.py:79
  148.7 74.0 %all-gather.5.cloned.1.call-done = f32[2,4160,256]{2,1,0:T(8,128)} async-done(((f32[2,520,256]{2,1,0:T(8,128)}), f32[2,4160,256]{2,1,0:T(8,128)}) %all-gather.5.cloned.1.call-update) | async-done | bytes 8519696 | tf_op jit(solution)/shard_map/all_gather | solution.py:118
  222.7 13.2 %reduce-precision_convert_fusion.7 = (bf16[2,520,256]{2,1,0:T(8,128)(2,1)}, bf16[2,520,256]{2,1,0:T(8,128)(2,1)}, bf16[2,520,256]{2,1,0:T(8,128)(2,1)}, f32[2,520,256]{2,1,0:T(8,128)S(1)}) fusion(f32[2,4160,256]{2,1,0:T(8,128)} %all-gather.5.cloned.1.call-done, f32[520,4160]{1,0:T(8,128)} %concatenate.70), kind=kOutput, calls=%fused_computation.84 | convolution fusion | flops 6647214080 | bytes 19834880 | tf_op jit(solution)/shard_map/ik,rkj->rij/dot_general | solution.py:117
  235.9 0.2 fusion.123
  236.1 0.2 copy.11
  236.4 3.2 %collective-permute-start.6 = (f32[2,520,2]{1,2,0:T(2,128)S(1)}, f32[2,520,2]{1,2,0:T(2,128)S(1)}, u32[]{:S(2)}, u32[]{:S(2)}) collective-permute-start(f32[2,520,2]{1,2,0:T(2,128)S(1)} %copy.11), channel_id=1, source_target_pairs={{0,1},{1,2},{2,3},{3,4},{4,5},{5,6},{6,7},{7,8},{8,9},{9,10},{10,1... | collective-permute-start | bytes 24968 | tf_op jit(solution)/shard_map/ppermute | solution.py:33
  239.6 0.2 copy.12
  239.8 2.1 collective-permute-start.7
  241.9 0.0 copy-done.6
  241.9 3.5 %fusion.51 = f32[2,1024,256]{1,2,0:T(8,128)S(1)} fusion(bf16[1024,520]{0,1:T(8,128)(2,1)S(1)} %copy-done.6, bf16[2,520,256]{2,1,0:T(8,128)(2,1)} %get-tuple-element.37, bf16[2,520,256]{2,1,0:T(8,128)(2,1)} %get-tuple-element.38, bf16[2,520,256]{2,1,0:T(8,128)(2,1)} %get-tuple-element.36), kind=kOutput, calls=%fused_computation.75 | convolution fusion | flops 1650155520 | bytes 4759552 | tf_op jit(solution)/shard_map/pi,rij->rpj/dot_general | solution.py:74
  245.5 0.0 collective-permute-done.6
  245.5 0.1 concatenate.71
  245.6 0.6 fusion.64
  246.3 0.0 collective-permute-done.7
  246.3 0.1 concatenate.74
  246.4 0.0 copy-start.7
  246.5 0.6 fusion.65
  247.1 0.0 copy-start.1
  247.1 0.7 reduce-precision_convert_fusion.3
  247.8 0.2 copy-done.7
  248.0 1.4 copy-done.1
  249.4 3.9 %multiply_add_fusion = f32[2,1024,512]{2,1,0:T(8,128)} fusion(f32[2,1024,512]{2,1,0:T(8,128)S(1)} %copy-done.1, f32[1024,512]{1,0:T(8,128)S(1)} %copy-done.7, bf16[2,1024,260]{1,2,0:T(8,128)(2,1)S(1)} %get-tuple-element.30, bf16[2,1024,260]{1,2,0:T(8,128)(2,1)S(1)} %get-tuple-element.29, bf16[2,1024,260]{1,2,0:T(8,128)(2,1)S(1)} %get-tuple-element.28, ...), kind=kOutput, calls=%fused_computation.20 | convolution fusion | flops 1649856512 | bytes 13946880 | tf_op jit(solution)/shard_map/rpj,jq->rpq/dot_general | solution.py:72
  (17 shorter events, 0.1 us)
Async XLA Ops:
  6.5 74.1 %all-gather.3.cloned.1.call-start = ((), (), s32[]{:S(2)}) async-start(), calls=%async_computation | async-start | bytes 9584640 | tf_op jit(solution)/shard_map/all_gather | solution.py:113
  8.8 11.8 %collective-permute-start = (f32[2,1024,4]{1,2,0:T(4,128)S(1)}, f32[2,1024,4]{1,2,0:T(4,128)S(1)}, u32[]{:S(2)}, u32[]{:S(2)}) collective-permute-start(f32[2,1024,4]{1,2,0:T(4,128)S(1)} %copy.13), channel_id=1, source_target_pairs={{0,1},{1,2},{2,3},{3,4},{4,5},{5,6},{6,7},{7,8},{8,9},{9,10},{10,1... | collective-permute-start | bytes 98312 | tf_op jit(solution)/shard_map/ppermute | solution.py:33
  13.7 7.4 %collective-permute-start.1 = (f32[2,1024,4]{1,2,0:T(4,128)S(1)}, f32[2,1024,4]{1,2,0:T(4,128)S(1)}, u32[]{:S(2)}, u32[]{:S(2)}) collective-permute-start(f32[2,1024,4]{1,2,0:T(4,128)S(1)} %copy.14), channel_id=1, source_target_pairs={{1,0},{2,1},{3,2},{4,3},{5,4},{6,5},{7,6},{8,7},{9,8},{10,9},{11,1... | collective-permute-start | bytes 98312 | tf_op jit(solution)/shard_map/ppermute | solution.py:34
  26.7 196.0 %all-gather.5.cloned.1.call-start = ((), (), s32[]{:S(2)}) async-start(), calls=%async_computation.1 | async-start | bytes 9584640 | tf_op jit(solution)/shard_map/all_gather | solution.py:118
  29.4 0.8 copy-start.2
  29.4 1.0 copy-start.4
  30.4 47.2 %collective-permute-start.2 = (f32[256,2048]{1,0:T(8,128)S(1)}, f32[256,2048]{1,0:T(8,128)}, u32[]{:S(2)}, u32[]{:S(2)}) collective-permute-start(f32[256,2048]{1,0:T(8,128)S(1)} %fusion.63), channel_id=1, source_target_pairs={{0,2},{2,0},{1,3},{3,1},{4,6},{6,4},{5,7},{7,5},{8,10},{10,8},{9,1... | collective-permute-start | bytes 6291464 | tf_op jit(solution)/shard_map/ppermute | solution.py:98
  80.6 8.5 %copy-start = (f32[2,520,2048]{2,1,0:T(8,128)S(1)}, f32[2,520,2048]{2,1,0:T(8,128)}, u32[]{:S(2)}) copy-start(f32[2,520,2048]{2,1,0:T(8,128)} %all-gather.3.cloned.1.call-done) | copy-start | bytes 25559044
  80.6 8.5 %copy-start.3 = (f32[256,512]{1,0:T(8,128)S(1)}, f32[256,512]{1,0:T(8,128)}, u32[]{:S(2)}) copy-start(f32[256,512]{1,0:T(8,128)} %copy-done.2) | copy-start | bytes 1572868
  80.6 8.5 %copy-start.5 = (f32[256,512]{1,0:T(8,128)S(1)}, f32[256,512]{1,0:T(8,128)}, u32[]{:S(2)}) copy-start(f32[256,512]{1,0:T(8,128)} %copy-done.4) | copy-start | bytes 1572868
  87.6 25.1 %collective-permute-start.3 = (f32[2,520,256]{2,1,0:T(8,128)S(1)}, f32[2,520,256]{2,1,0:T(8,128)S(1)}, u32[]{:S(2)}, u32[]{:S(2)}) collective-permute-start(f32[2,520,256]{2,1,0:T(8,128)S(1)} %fusion.42), channel_id=1, source_target_pairs={{0,2},{2,0},{1,3},{3,1},{4,6},{6,4},{5,7},{7,5},{8,10},{10,8},{9,1... | collective-permute-start | bytes 3194888 | tf_op jit(solution)/shard_map/ppermute | solution.py:116
  114.9 7.2 %collective-permute-start.4 = (f32[2,4096]{1,0:T(2,128)S(1)}, f32[2,4096]{1,0:T(2,128)S(1)}, u32[]{:S(2)}, u32[]{:S(2)}) collective-permute-start(f32[2,4096]{1,0:T(2,128)S(1)} %get-tuple-element.13), channel_id=1, source_target_pairs={{0,16},{16,32},{32,48},{48,64},{64,80},{80,96},{96,112},{1,17},{17... | collective-permute-start | bytes 98312 | tf_op jit(solution)/shard_map/ppermute | solution.py:19
  118.1 4.7 %collective-permute-start.5 = (f32[2,4096]{1,0:T(2,128)S(1)}, f32[2,4096]{1,0:T(2,128)S(1)}, u32[]{:S(2)}, u32[]{:S(2)}) collective-permute-start(f32[2,4096]{1,0:T(2,128)S(1)} %get-tuple-element.14), channel_id=1, source_target_pairs={{16,0},{32,16},{48,32},{64,48},{80,64},{96,80},{112,96},{17,1},{33... | collective-permute-start | bytes 98312 | tf_op jit(solution)/shard_map/ppermute | solution.py:21
  235.9 6.0 %copy-start.6 = (bf16[1024,520]{0,1:T(8,128)(2,1)S(1)}, bf16[1024,520]{0,1:T(8,128)(2,1)}, u32[]{:S(2)}) copy-start(bf16[1024,520]{0,1:T(8,128)(2,1)} %fusion.36) | copy-start | bytes 3194884
  236.4 9.1 %collective-permute-start.6 = (f32[2,520,2]{1,2,0:T(2,128)S(1)}, f32[2,520,2]{1,2,0:T(2,128)S(1)}, u32[]{:S(2)}, u32[]{:S(2)}) collective-permute-start(f32[2,520,2]{1,2,0:T(2,128)S(1)} %copy.11), channel_id=1, source_target_pairs={{0,1},{1,2},{2,3},{3,4},{4,5},{5,6},{6,7},{7,8},{8,9},{9,10},{10,1... | collective-permute-start | bytes 24968 | tf_op jit(solution)/shard_map/ppermute | solution.py:33
  239.8 6.5 %collective-permute-start.7 = (f32[2,520,2]{1,2,0:T(2,128)S(1)}, f32[2,520,2]{1,2,0:T(2,128)S(1)}, u32[]{:S(2)}, u32[]{:S(2)}) collective-permute-start(f32[2,520,2]{1,2,0:T(2,128)S(1)} %copy.12), channel_id=1, source_target_pairs={{1,0},{2,1},{3,2},{4,3},{5,4},{6,5},{7,6},{8,7},{9,8},{10,9},{11,1... | collective-permute-start | bytes 24968 | tf_op jit(solution)/shard_map/ppermute | solution.py:34
  246.4 1.6 copy-start.7
  247.1 2.3 copy-start.1
Sparse Core Ops, SparseCore 0:
  26.8 53.7 all-gather.2
  114.0 108.6 all-gather.4

commit v5 on v2

--- a/solution.py
+++ b/solution.py
@@ -111,9 +111,11 @@
     )
     inducing = exact_dot("ip,rpj->rij", colsum, row_adj, False)
     half = lax.all_gather(inducing, ("x", "core"), axis=2, tiled=True)
+    from_partner = [
+        lax.ppermute(jnp.einsum("ik,jk->ij", one, partner_cols, precision=highest), "yl", swap) for one in half
+    ]
     near = jnp.einsum("rik,jk->rij", half, near_cols, precision=highest)
-    for_partner = jnp.einsum("rik,jk->rij", half, partner_cols, precision=highest)
-    mixed = near + lax.ppermute(for_partner, "yl", swap)
+    mixed = near + jnp.stack(from_partner)
     product = jnp.einsum(
         "ik,rkj->rij", row_big, lax.all_gather(mixed, ("z", "yh"), axis=1, tiled=True), precision=highest
     )

time: 260 us -> 261 us (level)
    dot_general x1 -> x2, matrix products: 6.93 us -> 8.31 us  [body(): jnp.einsum('ik,jk->ij', one, partner_cols, precision=highest)]
    ppermute x1 -> x2, waiting for transfers between devices: 20.1 us -> 19 us  [body(): lax.ppermute(jnp.einsum('ik,jk->ij', one, partner_cols, precision=highest...]
  transfers between devices with their start and end apart: 10 -> 11, of which waited for: 6 -> 7; matrix products, arithmetic and copies ran while one was open for 16% -> 16% of each run, Pallas kernels for 0% -> 0%
where the time goes in v5:
time: 261 us; the launch traced here: 260 us
  waiting for transfers between devices  145 us (56%)
  matrix products  37.6 us (14%)
  local copies, waits for them, and re-layouts  24.6 us (9%)
  starting transfers between devices  19.8 us (8%)
  other arithmetic  19.5 us (7%)
  between operations  13.8 us (5%)
    all_gather x1, waiting for transfers between devices, body(): lax.all_gather(mixed, ('z', 'yh'), axis=1, tiled=True)  74 us
    ppermute x1, waiting for transfers between devices, body(): partner_cols = lax.ppermute(far_cols, 'yl', swap)  46.1 us
    ppermute x2, waiting for transfers between devices, body(): lax.ppermute(jnp.einsum('ik,jk->ij', one, partner_cols, precision=highest...  19 us
    dot_general x1, matrix products, body(): jnp.einsum('ik,rkj->rij', row_big, lax.all_gather(mixed, ('z', 'yh'), axi...  12.2 us
    concatenate x1, local copies, waits for them, and re-layouts, row_windows(): jnp.concatenate([padded[:, block * w:block * w + width] for w in order],...  11.7 us
    concatenate x1, other arithmetic, with_halo(): jnp.concatenate([lax.ppermute(tail, axis, [(i, (i + 1) % count) for i in...  11 us
    dot_general x2, matrix products, body(): jnp.einsum('ik,jk->ij', one, partner_cols, precision=highest)  8.31 us
    dot_general x4, matrix products, exact_dot(): jnp.einsum(eq, parts, jnp.concatenate([table] * 3, axis=0), preferred_ele...  7.22 us
  transfers between devices with their start and end apart: 11, of which 7 were waited for; matrix products, arithmetic and copies ran while one was open for 16% of the time, Pallas kernels for 0%

profile of v5, /device:TPU:1, one launch (start us, length us, event | category | flops | bytes accessed | tf_op | source)
XLA Modules:
  0.0 259.8 jit_solution(11159836597661485297)
XLA Ops:
  6.5 0.0 all-gather.3.cloned.1.call-start
  6.5 1.9 fusion.118
  8.4 0.3 copy.16
  8.8 4.6 %collective-permute-start = (f32[2,1024,4]{1,2,0:T(4,128)S(1)}, f32[2,1024,4]{1,2,0:T(4,128)S(1)}, u32[]{:S(2)}, u32[]{:S(2)}) collective-permute-start(f32[2,1024,4]{1,2,0:T(4,128)S(1)} %copy.16), channel_id=1, source_target_pairs={{0,1},{1,2},{2,3},{3,4},{4,5},{5,6},{6,7},{7,8},{8,9},{9,10},{10,1... | collective-permute-start | bytes 98312 | tf_op jit(solution)/shard_map/ppermute | solution.py:33
  13.4 0.3 copy.17
  13.7 1.9 collective-permute-start.1
  15.6 3.2 %reduce-precision_convert_fusion.1 = (bf16[2,1024,512]{2,1,0:T(8,128)(2,1)S(1)}, bf16[2,1024,512]{2,1,0:T(8,128)(2,1)S(1)}, bf16[2,1024,512]{2,1,0:T(8,128)(2,1)S(1)}) fusion(f32[2,1024,512]{2,1,0:T(8,128)} %param.4), kind=kLoop, calls=%fused_computation.18 | loop fusion | flops 7340032 | bytes 10485760 | tf_op jit(solution)/shard_map/convert_element_type | solution.py:64
  18.9 0.4 fusion.84
  19.2 1.3 fusion.42
  20.5 0.1 slice.112
  20.6 0.0 collective-permute-done
  20.6 0.5 fusion.87
  21.1 0.0 collective-permute-done.1
  21.2 0.5 fusion.93
  21.6 2.3 reduce-precision_convert_fusion.5
  23.9 2.8 %fusion.59 = f32[2,520,256]{2,1,0:T(8,128)} fusion(bf16[520,1024]{1,0:T(8,128)(2,1)S(1)} %fusion.42, bf16[2,1024,256]{2,1,0:T(8,128)(2,1)S(1)} %get-tuple-element.35, bf16[2,1024,256]{2,1,0:T(8,128)(2,1)S(1)} %get-tuple-element.36, bf16[2,1024,256]{2,1,0:T(8,128)(2,1)S(1)} %get-tuple-element.34), kind=kOutput, calls=%fused_computation.89 | convolution fusion | flops 1654800384 | bytes 5275648 | tf_op jit(solution)/shard_map/ip,rpj->rij/dot_general | solution.py:74
  26.7 0.0 all-gather.3.cloned.1.call-update
  26.7 0.0 all-gather.5.cloned.1.call-start
  26.8 2.6 %fusion.119 = (f32[256,512]{1,0:T(8,128)S(1)}, f32[256,512]{1,0:T(8,128)S(1)}, f32[256,512]{1,0:T(8,128)S(1)}, f32[256,512]{1,0:T(8,128)S(1)}, f32[256,512]{1,0:...) fusion(f32[256,4096]{1,0:T(8,128)} %param.7), kind=kLoop, calls=%fused_computation.165 | loop fusion | bytes 8388608 | tf_op jit(solution)/shard_map/slice | solution.py:94
  29.4 0.3 fusion.65
  29.7 0.5 copy-done.2
  30.2 0.2 copy-done.4
  30.4 0.2 copy-done.6
  30.5 0.1 copy-done.8
  30.7 0.2 copy-done.10
  30.9 0.2 copy-done.12
  31.0 1.1 collective-permute-start.2
  32.1 46.1 %collective-permute-done.2 = f32[256,2048]{1,0:T(8,128)S(1)} collective-permute-done((f32[256,2048]{1,0:T(8,128)S(1)}, f32[256,2048]{1,0:T(8,128)S(1)}, u32[]{:S(2)}, u32[]{:S(2)}) %collective-permute-start.2) | collective-permute-done | bytes 2097184 | tf_op jit(solution)/shard_map/ppermute | solution.py:98
  78.3 2.4 all-gather.3.cloned.1.call-done
  80.6 4.2 %fusion.11 = f32[520,256]{1,0:T(8,128)S(1)} fusion(f32[256,2048]{1,0:T(8,128)S(1)} %collective-permute-done.2, f32[2,520,2048]{2,1,0:T(8,128)} %all-gather.3.cloned.1.call-done), kind=kOutput, calls=%fused_computation.22 | convolution fusion | flops 1635778560 | bytes 6889472 | tf_op jit(solution)/shard_map/ik,jk->ij/dot_general | solution.py:115
  84.9 1.5 collective-permute-start.3
  86.5 4.1 %fusion.10 = f32[520,256]{1,0:T(8,128)S(1)} fusion(f32[256,2048]{1,0:T(8,128)S(1)} %collective-permute-done.2, f32[2,520,2048]{2,1,0:T(8,128)} %all-gather.3.cloned.1.call-done), kind=kOutput, calls=%fused_computation.20 | convolution fusion | flops 1635778560 | bytes 6889472 | tf_op jit(solution)/shard_map/ik,jk->ij/dot_general | solution.py:115
  90.5 0.5 collective-permute-start.4
  91.1 7.6 %collective-permute-done.3 = f32[520,256]{1,0:T(8,128)S(1)} collective-permute-done((f32[520,256]{1,0:T(8,128)S(1)}, f32[520,256]{1,0:T(8,128)S(1)}, u32[]{:S(2)}, u32[]{:S(2)}) %collective-permute-start.3) | collective-permute-done | bytes 532512 | tf_op jit(solution)/shard_map/ppermute | solution.py:115
  98.7 11.4 %collective-permute-done.4 = f32[520,256]{1,0:T(8,128)S(1)} collective-permute-done((f32[520,256]{1,0:T(8,128)S(1)}, f32[520,256]{1,0:T(8,128)S(1)}, u32[]{:S(2)}, u32[]{:S(2)}) %collective-permute-start.4) | collective-permute-done | bytes 532512 | tf_op jit(solution)/shard_map/ppermute | solution.py:115
  110.1 0.0 copy-done.3
  110.1 4.6 %maximum_add_fusion = f32[2,520,256]{2,1,0:T(8,128)} fusion(f32[1,520,256]{2,1,0:T(8,128)S(1)} %bitcast.58, f32[1,520,256]{2,1,0:T(8,128)S(1)} %bitcast.57, f32[2,520,2048]{2,1,0:T(8,128)S(1)} %copy-done, f32[256,512]{1,0:T(8,128)S(1)} %copy-done.11, f32[256,512]{1,0:T(8,128)S(1)} %copy-done.13, f32[256,512]{1,0:T(8,128)S(1)} %get-tuple-element.21, ...), kind=kOutput, calls=%fused_computation.92 | convolution fusion | flops 3275759616 | bytes 14843905 | tf_op jit(solution)/shard_map/rik,jk->rij/dot_general | solution.py:117
  114.7 0.0 all-gather.5.cloned.1.call-update
  114.7 1.0 fusion.117
  115.7 3.2 %collective-permute-start.5 = (f32[2,4096]{1,0:T(2,128)S(1)}, f32[2,4096]{1,0:T(2,128)S(1)}, u32[]{:S(2)}, u32[]{:S(2)}) collective-permute-start(f32[2,4096]{1,0:T(2,128)S(1)} %get-tuple-element.13), channel_id=1, source_target_pairs={{0,16},{16,32},{32,48},{48,64},{64,80},{80,96},{96,112},{1,17},{17... | collective-permute-start | bytes 98312 | tf_op jit(solution)/shard_map/ppermute | solution.py:19
  118.9 1.5 collective-permute-start.6
  120.5 2.3 fusion.45
  122.7 0.0 collective-permute-done.5
  122.7 0.8 collective-permute-done.6
  123.6 11.0 %select_maximum_fusion = f32[520,4104]{1,0:T(8,128)S(1)} fusion(f32[2,4096]{1,0:T(2,128)S(1)} %collective-permute-done.6, f32[512,4096]{1,0:T(8,128)} %param.6, f32[2,4096]{1,0:T(2,128)S(1)} %collective-permute-done.5), kind=kLoop, calls=%fused_computation.2 | loop fusion | flops 27743040 | bytes 16990464 | tf_op jit(solution)/shard_map/concatenate | solution.py:17
  134.6 3.4 %fusion.116 = (f32[520,520]{1,0:T(8,128)S(1)}, f32[520,520]{1,0:T(8,128)S(1)}, f32[520,520]{1,0:T(8,128)}, f32[520,520]{1,0:T(8,128)}, f32[520,520]{1,0:T(8,128)...) fusion(f32[520,4104]{1,0:T(8,128)S(1)} %select_maximum_fusion), kind=kLoop, calls=%fused_computation.162 | loop fusion | bytes 17305600 | tf_op jit(solution)/shard_map/slice | solution.py:79
  137.9 11.7 %concatenate.62 = f32[520,4160]{1,0:T(8,128)} concatenate(f32[520,520]{1,0:T(8,128)} %get-tuple-element.12, f32[520,520]{1,0:T(8,128)} %get-tuple-element.11, f32[520,520]{1,0:T(8,128)} %get-tuple-element.10, f32[520,520]{1,0:T(8,128)} %get-tuple-element.9, f32[520,520]{1,0:T(8,128)} %get-tuple-element.8, f32[520,520]{1,0:T(8,128)} %get-tuple-element.7, ...), dimensions={1} | concatenate | bytes 17305600 | tf_op jit(solution)/shard_map/concatenate | solution.py:79
  149.6 74.0 %all-gather.5.cloned.1.call-done = f32[2,4160,256]{2,1,0:T(8,128)} async-done(((f32[2,520,256]{2,1,0:T(8,128)}), f32[2,4160,256]{2,1,0:T(8,128)}) %all-gather.5.cloned.1.call-update) | async-done | bytes 8519696 | tf_op jit(solution)/shard_map/all_gather | solution.py:120
  223.5 12.2 %fusion.62 = f32[2,520,256]{2,1,0:T(8,128)S(1)} fusion(f32[2,4160,256]{2,1,0:T(8,128)} %all-gather.5.cloned.1.call-done, f32[520,4160]{1,0:T(8,128)} %concatenate.62), kind=kOutput, calls=%fused_computation.90 | convolution fusion | flops 6645350400 | bytes 18237440 | tf_op jit(solution)/shard_map/ik,rkj->rij/dot_general | solution.py:119
  235.8 0.2 fusion.120
  236.0 0.2 copy.10
  236.2 3.2 %collective-permute-start.7 = (f32[2,520,2]{1,2,0:T(2,128)S(1)}, f32[2,520,2]{1,2,0:T(2,128)S(1)}, u32[]{:S(2)}, u32[]{:S(2)}) collective-permute-start(f32[2,520,2]{1,2,0:T(2,128)S(1)} %copy.10), channel_id=1, source_target_pairs={{0,1},{1,2},{2,3},{3,4},{4,5},{5,6},{6,7},{7,8},{8,9},{9,10},{10,1... | collective-permute-start | bytes 24968 | tf_op jit(solution)/shard_map/ppermute | solution.py:19
  239.4 0.2 copy.11
  239.6 2.2 collective-permute-start.8
  241.8 0.4 fusion.79
  242.2 0.0 collective-permute-done.7
  242.2 0.2 copy.12
  242.4 2.2 collective-permute-done.8
  244.6 0.2 copy.13
  244.8 0.7 reduce-precision_convert_fusion.7
  245.6 0.5 copy-done.14
  246.1 2.5 reduce-precision_convert_fusion.3
  248.6 0.3 copy-done.15
  248.9 4.0 %multiply_add_fusion = f32[2,1024,512]{2,1,0:T(8,128)} fusion(f32[2,1024,512]{2,1,0:T(8,128)S(1)} %copy-done.1, f32[1024,512]{1,0:T(8,128)S(1)} %copy-done.15, bf16[2,1024,260]{1,2,0:T(8,128)(2,1)S(1)} %get-tuple-element.29, bf16[2,1024,260]{1,2,0:T(8,128)(2,1)S(1)} %get-tuple-element.30, bf16[2,1024,260]{1,2,0:T(8,128)(2,1)S(1)} %get-tuple-element.28, ...), kind=kOutput, calls=%fused_computation.24 | convolution fusion | flops 1649856512 | bytes 13946880 | tf_op jit(solution)/shard_map/rpj,jq->rpq/dot_general | solution.py:72
  (31 shorter events, 0.1 us)
Async XLA Ops:
  6.5 74.1 %all-gather.3.cloned.1.call-start = ((), (), s32[]{:S(2)}) async-start(), calls=%async_computation | async-start | bytes 9584640 | tf_op jit(solution)/shard_map/all_gather | solution.py:113
  8.8 11.8 %collective-permute-start = (f32[2,1024,4]{1,2,0:T(4,128)S(1)}, f32[2,1024,4]{1,2,0:T(4,128)S(1)}, u32[]{:S(2)}, u32[]{:S(2)}) collective-permute-start(f32[2,1024,4]{1,2,0:T(4,128)S(1)} %copy.16), channel_id=1, source_target_pairs={{0,1},{1,2},{2,3},{3,4},{4,5},{5,6},{6,7},{7,8},{8,9},{9,10},{10,1... | collective-permute-start | bytes 98312 | tf_op jit(solution)/shard_map/ppermute | solution.py:33
  13.7 7.4 %collective-permute-start.1 = (f32[2,1024,4]{1,2,0:T(4,128)S(1)}, f32[2,1024,4]{1,2,0:T(4,128)S(1)}, u32[]{:S(2)}, u32[]{:S(2)}) collective-permute-start(f32[2,1024,4]{1,2,0:T(4,128)S(1)} %copy.17), channel_id=1, source_target_pairs={{1,0},{2,1},{3,2},{4,3},{5,4},{6,5},{7,6},{8,7},{9,8},{10,9},{11,1... | collective-permute-start | bytes 98312 | tf_op jit(solution)/shard_map/ppermute | solution.py:34
  26.7 196.8 %all-gather.5.cloned.1.call-start = ((), (), s32[]{:S(2)}) async-start(), calls=%async_computation.1 | async-start | bytes 9584640 | tf_op jit(solution)/shard_map/all_gather | solution.py:120
  29.4 0.8 copy-start.2
  29.4 1.0 copy-start.4
  29.4 1.1 copy-start.6
  29.4 1.3 copy-start.8
  29.4 1.4 copy-start.10
  29.4 1.6 copy-start.12
  31.0 47.2 %collective-permute-start.2 = (f32[256,2048]{1,0:T(8,128)S(1)}, f32[256,2048]{1,0:T(8,128)S(1)}, u32[]{:S(2)}, u32[]{:S(2)}) collective-permute-start(f32[256,2048]{1,0:T(8,128)S(1)} %fusion.65), channel_id=1, source_target_pairs={{0,2},{2,0},{1,3},{3,1},{4,6},{6,4},{5,7},{7,5},{8,10},{10,8},{9,1... | collective-permute-start | bytes 6291464 | tf_op jit(solution)/shard_map/ppermute | solution.py:98
  80.6 29.4 %copy-start = (f32[2,520,2048]{2,1,0:T(8,128)S(1)}, f32[2,520,2048]{2,1,0:T(8,128)}, u32[]{:S(2)}) copy-start(f32[2,520,2048]{2,1,0:T(8,128)} %all-gather.3.cloned.1.call-done) | copy-start | bytes 25559044
  84.9 25.2 %copy-start.3 = (f32[256,512]{1,0:T(8,128)S(1)}, f32[256,512]{1,0:T(8,128)}, u32[]{:S(2)}) copy-start(f32[256,512]{1,0:T(8,128)} %copy-done.2) | copy-start | bytes 1572868
  84.9 25.2 %copy-start.5 = (f32[256,512]{1,0:T(8,128)S(1)}, f32[256,512]{1,0:T(8,128)}, u32[]{:S(2)}) copy-start(f32[256,512]{1,0:T(8,128)} %copy-done.4) | copy-start | bytes 1572868
  84.9 25.2 %copy-start.7 = (f32[256,512]{1,0:T(8,128)S(1)}, f32[256,512]{1,0:T(8,128)}, u32[]{:S(2)}) copy-start(f32[256,512]{1,0:T(8,128)} %copy-done.6) | copy-start | bytes 1572868
  84.9 25.2 %copy-start.9 = (f32[256,512]{1,0:T(8,128)S(1)}, f32[256,512]{1,0:T(8,128)}, u32[]{:S(2)}) copy-start(f32[256,512]{1,0:T(8,128)} %copy-done.8) | copy-start | bytes 1572868
  84.9 25.2 %copy-start.11 = (f32[256,512]{1,0:T(8,128)S(1)}, f32[256,512]{1,0:T(8,128)}, u32[]{:S(2)}) copy-start(f32[256,512]{1,0:T(8,128)} %copy-done.10) | copy-start | bytes 1572868
  84.9 25.2 %copy-start.13 = (f32[256,512]{1,0:T(8,128)S(1)}, f32[256,512]{1,0:T(8,128)}, u32[]{:S(2)}) copy-start(f32[256,512]{1,0:T(8,128)} %copy-done.12) | copy-start | bytes 1572868
  84.9 13.7 %collective-permute-start.3 = (f32[520,256]{1,0:T(8,128)S(1)}, f32[520,256]{1,0:T(8,128)S(1)}, u32[]{:S(2)}, u32[]{:S(2)}) collective-permute-start(f32[520,256]{1,0:T(8,128)S(1)} %fusion.11), channel_id=1, source_target_pairs={{0,2},{2,0},{1,3},{3,1},{4,6},{6,4},{5,7},{7,5},{8,10},{10,8},{9,1... | collective-permute-start | bytes 1597448 | tf_op jit(solution)/shard_map/ppermute | solution.py:115
  90.5 19.5 %collective-permute-start.4 = (f32[520,256]{1,0:T(8,128)S(1)}, f32[520,256]{1,0:T(8,128)S(1)}, u32[]{:S(2)}, u32[]{:S(2)}) collective-permute-start(f32[520,256]{1,0:T(8,128)S(1)} %fusion.10), channel_id=1, source_target_pairs={{0,2},{2,0},{1,3},{3,1},{4,6},{6,4},{5,7},{7,5},{8,10},{10,8},{9,1... | collective-permute-start | bytes 1597448 | tf_op jit(solution)/shard_map/ppermute | solution.py:115
  115.7 7.0 %collective-permute-start.5 = (f32[2,4096]{1,0:T(2,128)S(1)}, f32[2,4096]{1,0:T(2,128)S(1)}, u32[]{:S(2)}, u32[]{:S(2)}) collective-permute-start(f32[2,4096]{1,0:T(2,128)S(1)} %get-tuple-element.13), channel_id=1, source_target_pairs={{0,16},{16,32},{32,48},{48,64},{64,80},{80,96},{96,112},{1,17},{17... | collective-permute-start | bytes 98312 | tf_op jit(solution)/shard_map/ppermute | solution.py:19
  118.9 4.7 %collective-permute-start.6 = (f32[2,4096]{1,0:T(2,128)S(1)}, f32[2,4096]{1,0:T(2,128)S(1)}, u32[]{:S(2)}, u32[]{:S(2)}) collective-permute-start(f32[2,4096]{1,0:T(2,128)S(1)} %get-tuple-element.14), channel_id=1, source_target_pairs={{16,0},{32,16},{48,32},{64,48},{80,64},{96,80},{112,96},{17,1},{33... | collective-permute-start | bytes 98312 | tf_op jit(solution)/shard_map/ppermute | solution.py:21
  236.2 6.0 %collective-permute-start.7 = (f32[2,520,2]{1,2,0:T(2,128)S(1)}, f32[2,520,2]{1,2,0:T(2,128)S(1)}, u32[]{:S(2)}, u32[]{:S(2)}) collective-permute-start(f32[2,520,2]{1,2,0:T(2,128)S(1)} %copy.10), channel_id=1, source_target_pairs={{0,1},{1,2},{2,3},{3,4},{4,5},{5,6},{6,7},{7,8},{8,9},{9,10},{10,1... | collective-permute-start | bytes 24968 | tf_op jit(solution)/shard_map/ppermute | solution.py:19
  239.6 5.0 %collective-permute-start.8 = (f32[2,520,2]{1,2,0:T(2,128)S(1)}, f32[2,520,2]{1,2,0:T(2,128)S(1)}, u32[]{:S(2)}, u32[]{:S(2)}) collective-permute-start(f32[2,520,2]{1,2,0:T(2,128)S(1)} %copy.11), channel_id=1, source_target_pairs={{1,0},{2,1},{3,2},{4,3},{5,4},{6,5},{7,6},{8,7},{9,8},{10,9},{11,1... | collective-permute-start | bytes 24968 | tf_op jit(solution)/shard_map/ppermute | solution.py:21
  244.8 1.2 copy-start.14
  246.1 2.5 copy-start.1
  246.1 2.9 %copy-start.15 = (f32[1024,512]{1,0:T(8,128)S(1)}, f32[1024,512]{1,0:T(8,128)}, u32[]{:S(2)}) copy-start(f32[1024,512]{1,0:T(8,128)} %param.5) | copy-start | bytes 6291460
Sparse Core Ops, SparseCore 0:
  26.8 53.7 all-gather.2
  114.8 108.6 all-gather.4

commit v6 on v2

--- a/solution.py
+++ b/solution.py
@@ -114,9 +114,12 @@
     near = jnp.einsum("rik,jk->rij", half, near_cols, precision=highest)
     for_partner = jnp.einsum("rik,jk->rij", half, partner_cols, precision=highest)
     mixed = near + lax.ppermute(for_partner, "yl", swap)
-    product = jnp.einsum(
-        "ik,rkj->rij", row_big, lax.all_gather(mixed, ("z", "yh"), axis=1, tiled=True), precision=highest
-    )
+    kernel_hi = lax.reduce_precision(row_big, exponent_bits=8, mantissa_bits=7)
+    kernel_parts = jnp.concatenate([kernel_hi, kernel_hi, row_big - kernel_hi], axis=1).astype(jnp.bfloat16)
+    column_slab = lax.all_gather(mixed, ("z", "yh"), axis=1, tiled=True)
+    slab_hi = lax.reduce_precision(column_slab, exponent_bits=8, mantissa_bits=7)
+    slab_parts = jnp.concatenate([slab_hi, column_slab - slab_hi, slab_hi], axis=1).astype(jnp.bfloat16)
+    product = jnp.einsum("ik,rkj->rij", kernel_parts, slab_parts, preferred_element_type=jnp.float32)
     coarse_ext = with_halo(product, ((cols_axis, 2),), 2)
     row_fwd = tap_table(2 * tile_rows, ext_rows, False, 2)
     col_fwd = tap_table(tile_cols + 4, 2 * tile_cols, True, 2)

time: 260 us -> 276 us (1.062)
  waiting for transfers between devices: 147 us -> 113 us
  local copies, waits for them, and re-layouts: 23.9 us -> 47.7 us
  other arithmetic: 20.6 us -> 36.7 us
  matrix products: 35.2 us -> 43 us
    all_gather x1, waiting for transfers between devices: 73.9 us -> 42.1 us  [body(): column_slab = lax.all_gather(mixed, ('z', 'yh'), axis=1, tiled=True)]
    concatenate x0 -> x1, local copies, waits for them, and re-layouts: none -> 23.9 us  [body(): jnp.concatenate([kernel_hi, kernel_hi, row_big - kernel_hi], axis=1)]
    another operation x0 -> x2, other arithmetic: none -> 16.1 us
    dot_general x1, matrix products: 12.2 us -> 20 us  [body(): jnp.einsum('ik,rkj->rij', kernel_parts, slab_parts, preferred_element_typ...]
  transfers between devices with their start and end apart: 10 -> 10, of which waited for: 6 -> 6; matrix products, arithmetic and copies ran while one was open for 16% -> 27% of each run, Pallas kernels for 0% -> 0%
where the time goes in v6:
time: 276 us; the launch traced here: 274 us
  waiting for transfers between devices  113 us (41%)
  local copies, waits for them, and re-layouts  47.7 us (17%)
  matrix products  43 us (16%)
  other arithmetic  36.7 us (13%)
  starting transfers between devices  19.9 us (7%)
  between operations  13.7 us (5%)
    ppermute x1, waiting for transfers between devices, body(): partner_cols = lax.ppermute(far_cols, 'yl', swap)  45.4 us
    all_gather x1, waiting for transfers between devices, body(): column_slab = lax.all_gather(mixed, ('z', 'yh'), axis=1, tiled=True)  42.1 us
    concatenate x1, local copies, waits for them, and re-layouts, body(): jnp.concatenate([kernel_hi, kernel_hi, row_big - kernel_hi], axis=1)  23.9 us
    ppermute x1, waiting for transfers between devices, body(): mixed = near + lax.ppermute(for_partner, 'yl', swap)  20.1 us
    dot_general x1, matrix products, body(): jnp.einsum('ik,rkj->rij', kernel_parts, slab_parts, preferred_element_typ...  20 us
    another operation x2, other arithmetic  16.1 us
    concatenate x1, local copies, waits for them, and re-layouts, row_windows(): jnp.concatenate([padded[:, block * w:block * w + width] for w in order],...  11.6 us
    concatenate x1, other arithmetic, with_halo(): jnp.concatenate([lax.ppermute(tail, axis, [(i, (i + 1) % count) for i in...  10.9 us
  transfers between devices with their start and end apart: 10, of which 6 were waited for; matrix products, arithmetic and copies ran while one was open for 27% of the time, Pallas kernels for 0%

profile of v6, /device:TPU:1, one launch (start us, length us, event | category | flops | bytes accessed | tf_op | source)
XLA Modules:
  0.0 274.2 jit_solution(13731665931565389013)
XLA Ops:
  6.5 0.0 all-gather.3.cloned.1.call-start
  6.5 1.9 fusion.127
  8.4 0.3 copy.17
  8.8 3.3 %collective-permute-start.1 = (f32[2,1024,4]{1,2,0:T(4,128)S(1)}, f32[2,1024,4]{1,2,0:T(4,128)S(1)}, u32[]{:S(2)}, u32[]{:S(2)}) collective-permute-start(f32[2,1024,4]{1,2,0:T(4,128)S(1)} %copy.17), channel_id=1, source_target_pairs={{1,0},{2,1},{3,2},{4,3},{5,4},{6,5},{7,6},{8,7},{9,8},{10,9},{11,1... | collective-permute-start | bytes 98312 | tf_op jit(solution)/shard_map/ppermute | solution.py:34
  12.1 0.3 copy.16
  12.4 3.2 %collective-permute-start = (f32[2,1024,4]{1,2,0:T(4,128)S(1)}, f32[2,1024,4]{1,2,0:T(4,128)S(1)}, u32[]{:S(2)}, u32[]{:S(2)}) collective-permute-start(f32[2,1024,4]{1,2,0:T(4,128)S(1)} %copy.16), channel_id=1, source_target_pairs={{0,1},{1,2},{2,3},{3,4},{4,5},{5,6},{6,7},{7,8},{8,9},{9,10},{10,1... | collective-permute-start | bytes 98312 | tf_op jit(solution)/shard_map/ppermute | solution.py:33
  15.6 3.2 %reduce-precision_convert_fusion.3 = (bf16[2,1024,512]{2,1,0:T(8,128)(2,1)S(1)}, bf16[2,1024,512]{2,1,0:T(8,128)(2,1)S(1)}, bf16[2,1024,512]{2,1,0:T(8,128)(2,1)S(1)}) fusion(f32[2,1024,512]{2,1,0:T(8,128)} %param.4), kind=kLoop, calls=%fused_computation.29 | loop fusion | flops 7340032 | bytes 10485760 | tf_op jit(solution)/shard_map/convert_element_type | solution.py:64
  18.9 0.4 fusion.91
  19.2 1.3 fusion.47
  20.5 0.1 slice.112
  20.6 0.0 collective-permute-done.1
  20.6 0.5 fusion.100
  21.1 0.0 collective-permute-done
  21.2 0.5 fusion.94
  21.6 2.3 reduce-precision_convert_fusion.7
  23.9 2.8 %fusion.71 = f32[2,520,256]{2,1,0:T(8,128)} fusion(bf16[520,1024]{1,0:T(8,128)(2,1)S(1)} %fusion.47, bf16[2,1024,256]{2,1,0:T(8,128)(2,1)S(1)} %get-tuple-element.39, bf16[2,1024,256]{2,1,0:T(8,128)(2,1)S(1)} %get-tuple-element.40, bf16[2,1024,256]{2,1,0:T(8,128)(2,1)S(1)} %get-tuple-element.38), kind=kOutput, calls=%fused_computation.99 | convolution fusion | flops 1654800384 | bytes 5275648 | tf_op jit(solution)/shard_map/ip,rpj->rij/dot_general | solution.py:74
  26.7 0.0 all-gather.3.cloned.1.call-update
  26.7 0.0 all-gather.5.cloned.1.call-start
  26.8 2.6 fusion.126
  29.4 0.0 copy-start.2
  29.4 0.0 copy-start.4
  29.4 0.3 fusion.74
  29.7 0.5 copy-done.2
  30.2 0.1 copy-done.4
  30.4 2.1 collective-permute-start.2
  32.4 45.4 %collective-permute-done.2 = f32[256,2048]{1,0:T(8,128)} collective-permute-done((f32[256,2048]{1,0:T(8,128)S(1)}, f32[256,2048]{1,0:T(8,128)}, u32[]{:S(2)}, u32[]{:S(2)}) %collective-permute-start.2) | collective-permute-done | bytes 2097184 | tf_op jit(solution)/shard_map/ppermute | solution.py:98
  77.8 2.1 all-gather.3.cloned.1.call-done
  80.0 7.0 %fusion.56 = f32[2,520,256]{2,1,0:T(8,128)S(1)} fusion(f32[2,520,2048]{2,1,0:T(8,128)} %all-gather.3.cloned.1.call-done, f32[256,2048]{1,0:T(8,128)} %collective-permute-done.2), kind=kOutput, calls=%fused_computation.90 | convolution fusion | flops 3271557120 | bytes 11681792 | tf_op jit(solution)/shard_map/rik,jk->rij/dot_general | solution.py:115
  86.9 1.5 collective-permute-start.3
  88.4 0.0 copy-done
  88.4 0.0 copy-done.3
  88.4 3.5 %fusion.58 = f32[2,520,256]{2,1,0:T(8,128)S(1)} fusion(f32[2,520,2048]{2,1,0:T(8,128)S(1)} %copy-done, f32[256,512]{1,0:T(8,128)S(1)} %copy-done.3, f32[256,512]{1,0:T(8,128)S(1)} %copy-done.5, f32[256,512]{1,0:T(8,128)S(1)} %get-tuple-element.20, f32[256,512]{1,0:T(8,128)S(1)} %get-tuple-element.21, f32[256,512]{1,0:T(8,128)S(1)} %get-tuple-element.22, ...), kind=kOutput, calls=%fused_computation.92 | convolution fusion | flops 3275227136 | bytes 13778945 | tf_op jit(solution)/shard_map/rik,jk->rij/dot_general | solution.py:114
  92.0 20.1 %collective-permute-done.3 = f32[2,520,256]{2,1,0:T(8,128)S(1)} collective-permute-done((f32[2,520,256]{2,1,0:T(8,128)S(1)}, f32[2,520,256]{2,1,0:T(8,128)S(1)}, u32[]{:S(2)}, u32[]{:S(2)}) %collective-permute-start.3) | collective-permute-done | bytes 1064992 | tf_op jit(solution)/shard_map/ppermute | solution.py:116
  112.0 1.1 add.216
  113.2 0.0 all-gather.5.cloned.1.call-update
  113.2 1.0 fusion.125
  114.2 3.2 %collective-permute-start.4 = (f32[2,4096]{1,0:T(2,128)S(1)}, f32[2,4096]{1,0:T(2,128)S(1)}, u32[]{:S(2)}, u32[]{:S(2)}) collective-permute-start(f32[2,4096]{1,0:T(2,128)S(1)} %get-tuple-element.17), channel_id=1, source_target_pairs={{0,16},{16,32},{32,48},{48,64},{64,80},{80,96},{96,112},{1,17},{17... | collective-permute-start | bytes 98312 | tf_op jit(solution)/shard_map/ppermute | solution.py:19
  117.4 1.3 collective-permute-start.5
  118.7 2.3 fusion.50
  121.0 0.0 collective-permute-done.4
  121.0 1.1 collective-permute-done.5
  122.1 10.9 %select_maximum_fusion = f32[520,4104]{1,0:T(8,128)S(1)} fusion(f32[2,4096]{1,0:T(2,128)S(1)} %collective-permute-done.5, f32[512,4096]{1,0:T(8,128)} %param.6, f32[2,4096]{1,0:T(2,128)S(1)} %collective-permute-done.4), kind=kLoop, calls=%fused_computation.14 | loop fusion | flops 27743040 | bytes 16990464 | tf_op jit(solution)/shard_map/concatenate | solution.py:17
  133.0 3.4 %fusion.124 = (f32[520,520]{1,0:T(8,128)S(1)}, f32[520,520]{1,0:T(8,128)S(1)}, f32[520,520]{1,0:T(8,128)}, f32[520,520]{1,0:T(8,128)}, f32[520,520]{1,0:T(8,128)...) fusion(f32[520,4104]{1,0:T(8,128)S(1)} %select_maximum_fusion), kind=kLoop, calls=%fused_computation.171 | loop fusion | bytes 17305600 | tf_op jit(solution)/shard_map/slice | solution.py:79
  136.4 11.6 %concatenate.71 = f32[520,4160]{1,0:T(8,128)} concatenate(f32[520,520]{1,0:T(8,128)} %get-tuple-element.14, f32[520,520]{1,0:T(8,128)} %get-tuple-element.13, f32[520,520]{1,0:T(8,128)} %get-tuple-element.12, f32[520,520]{1,0:T(8,128)} %get-tuple-element.11, f32[520,520]{1,0:T(8,128)} %get-tuple-element.10, f32[520,520]{1,0:T(8,128)} %get-tuple-element.9, ...), dimensions={1} | concatenate | bytes 17305600 | tf_op jit(solution)/shard_map/concatenate | solution.py:79
  148.0 8.0 %fusion.7 = (bf16[520,4160]{1,0:T(8,128)(2,1)}, bf16[520,4160]{1,0:T(8,128)(2,1)}) fusion(f32[520,4160]{1,0:T(8,128)} %concatenate.71), kind=kLoop, calls=%fused_computation.13 | loop fusion | flops 8652800 | bytes 17305600 | tf_op jit(solution)/shard_map/convert.2
  156.1 23.9 %concatenate.72 = bf16[520,12480]{1,0:T(8,128)(2,1)} concatenate(bf16[520,4160]{1,0:T(8,128)(2,1)} %get-tuple-element.6, bf16[520,4160]{1,0:T(8,128)(2,1)} %get-tuple-element.6, bf16[520,4160]{1,0:T(8,128)(2,1)} %get-tuple-element.5), dimensions={1} | concatenate | bytes 25958400 | tf_op jit(solution)/shard_map/concatenate | solution.py:118
  180.0 42.1 %all-gather.5.cloned.1.call-done = f32[2,4160,256]{2,1,0:T(8,128)} async-done(((f32[2,520,256]{2,1,0:T(8,128)}), f32[2,4160,256]{2,1,0:T(8,128)}) %all-gather.5.cloned.1.call-update) | async-done | bytes 8519696 | tf_op jit(solution)/shard_map/all_gather | solution.py:119
  222.1 8.1 %fusion.10 = (bf16[2,4160,256]{2,1,0:T(8,128)(2,1)}, bf16[2,4160,256]{2,1,0:T(8,128)(2,1)}) fusion(f32[2,4160,256]{2,1,0:T(8,128)} %all-gather.5.cloned.1.call-done), kind=kLoop, calls=%fused_computation.19 | loop fusion | flops 8519680 | bytes 17039360 | tf_op jit(solution)/shard_map/convert.4
  230.2 20.0 %fusion.66 = f32[2,520,256]{2,1,0:T(8,128)S(1)} fusion(bf16[520,12480]{1,0:T(8,128)(2,1)} %concatenate.72, bf16[2,4160,256]{2,1,0:T(8,128)(2,1)} %get-tuple-element.16, bf16[2,4160,256]{2,1,0:T(8,128)(2,1)} %get-tuple-element.15), kind=kOutput, calls=%fused_computation.98 | convolution fusion | flops 6683688960 | bytes 22563840 | tf_op jit(solution)/shard_map/ik,rkj->rij/dot_general | solution.py:122
  250.2 0.2 fusion.128
  250.4 0.2 copy.10
  250.6 3.2 %collective-permute-start.6 = (f32[2,520,2]{1,2,0:T(2,128)S(1)}, f32[2,520,2]{1,2,0:T(2,128)S(1)}, u32[]{:S(2)}, u32[]{:S(2)}) collective-permute-start(f32[2,520,2]{1,2,0:T(2,128)S(1)} %copy.10), channel_id=1, source_target_pairs={{0,1},{1,2},{2,3},{3,4},{4,5},{5,6},{6,7},{7,8},{8,9},{9,10},{10,1... | collective-permute-start | bytes 24968 | tf_op jit(solution)/shard_map/ppermute | solution.py:19
  253.8 0.2 copy.11
  254.0 2.1 collective-permute-start.7
  256.1 0.4 fusion.86
  256.5 0.0 collective-permute-done.6
  256.5 0.2 copy.12
  256.7 2.2 collective-permute-done.7
  259.0 0.2 copy.13
  259.2 0.7 reduce-precision_convert_fusion.9
  259.9 0.5 copy-done.6
  260.4 2.5 reduce-precision_convert_fusion.5
  263.0 0.3 copy-done.7
  263.3 4.0 %multiply_add_fusion = f32[2,1024,512]{2,1,0:T(8,128)} fusion(f32[2,1024,512]{2,1,0:T(8,128)S(1)} %copy-done.1, f32[1024,512]{1,0:T(8,128)S(1)} %copy-done.7, bf16[2,1024,260]{1,2,0:T(8,128)(2,1)S(1)} %get-tuple-element.33, bf16[2,1024,260]{1,2,0:T(8,128)(2,1)S(1)} %get-tuple-element.34, bf16[2,1024,260]{1,2,0:T(8,128)(2,1)S(1)} %get-tuple-element.32, ...), kind=kOutput, calls=%fused_computation.31 | convolution fusion | flops 1649856512 | bytes 13946880 | tf_op jit(solution)/shard_map/rpj,jq->rpq/dot_general | solution.py:72
  (16 shorter events, 0.1 us)
Async XLA Ops:
  6.5 73.4 %all-gather.3.cloned.1.call-start = ((), (), s32[]{:S(2)}) async-start(), calls=%async_computation | async-start | bytes 9584640 | tf_op jit(solution)/shard_map/all_gather | solution.py:113
  8.8 11.8 %collective-permute-start.1 = (f32[2,1024,4]{1,2,0:T(4,128)S(1)}, f32[2,1024,4]{1,2,0:T(4,128)S(1)}, u32[]{:S(2)}, u32[]{:S(2)}) collective-permute-start(f32[2,1024,4]{1,2,0:T(4,128)S(1)} %copy.17), channel_id=1, source_target_pairs={{1,0},{2,1},{3,2},{4,3},{5,4},{6,5},{7,6},{8,7},{9,8},{10,9},{11,1... | collective-permute-start | bytes 98312 | tf_op jit(solution)/shard_map/ppermute | solution.py:34
  12.4 8.7 %collective-permute-start = (f32[2,1024,4]{1,2,0:T(4,128)S(1)}, f32[2,1024,4]{1,2,0:T(4,128)S(1)}, u32[]{:S(2)}, u32[]{:S(2)}) collective-permute-start(f32[2,1024,4]{1,2,0:T(4,128)S(1)} %copy.16), channel_id=1, source_target_pairs={{0,1},{1,2},{2,3},{3,4},{4,5},{5,6},{6,7},{7,8},{8,9},{9,10},{10,1... | collective-permute-start | bytes 98312 | tf_op jit(solution)/shard_map/ppermute | solution.py:33
  26.7 195.4 %all-gather.5.cloned.1.call-start = ((), (), s32[]{:S(2)}) async-start(), calls=%async_computation.1 | async-start | bytes 9584640 | tf_op jit(solution)/shard_map/all_gather | solution.py:119
  29.4 0.8 copy-start.2
  29.4 1.0 copy-start.4
  30.4 47.4 %collective-permute-start.2 = (f32[256,2048]{1,0:T(8,128)S(1)}, f32[256,2048]{1,0:T(8,128)}, u32[]{:S(2)}, u32[]{:S(2)}) collective-permute-start(f32[256,2048]{1,0:T(8,128)S(1)} %fusion.74), channel_id=1, source_target_pairs={{0,2},{2,0},{1,3},{3,1},{4,6},{6,4},{5,7},{7,5},{8,10},{10,8},{9,1... | collective-permute-start | bytes 6291464 | tf_op jit(solution)/shard_map/ppermute | solution.py:98
  79.9 8.5 %copy-start = (f32[2,520,2048]{2,1,0:T(8,128)S(1)}, f32[2,520,2048]{2,1,0:T(8,128)}, u32[]{:S(2)}) copy-start(f32[2,520,2048]{2,1,0:T(8,128)} %all-gather.3.cloned.1.call-done) | copy-start | bytes 25559044
  79.9 8.5 %copy-start.3 = (f32[256,512]{1,0:T(8,128)S(1)}, f32[256,512]{1,0:T(8,128)}, u32[]{:S(2)}) copy-start(f32[256,512]{1,0:T(8,128)} %copy-done.2) | copy-start | bytes 1572868
  80.0 8.5 %copy-start.5 = (f32[256,512]{1,0:T(8,128)S(1)}, f32[256,512]{1,0:T(8,128)}, u32[]{:S(2)}) copy-start(f32[256,512]{1,0:T(8,128)} %copy-done.4) | copy-start | bytes 1572868
  86.9 25.1 %collective-permute-start.3 = (f32[2,520,256]{2,1,0:T(8,128)S(1)}, f32[2,520,256]{2,1,0:T(8,128)S(1)}, u32[]{:S(2)}, u32[]{:S(2)}) collective-permute-start(f32[2,520,256]{2,1,0:T(8,128)S(1)} %fusion.56), channel_id=1, source_target_pairs={{0,2},{2,0},{1,3},{3,1},{4,6},{6,4},{5,7},{7,5},{8,10},{10,8},{9,1... | collective-permute-start | bytes 3194888 | tf_op jit(solution)/shard_map/ppermute | solution.py:116
  114.2 6.8 %collective-permute-start.4 = (f32[2,4096]{1,0:T(2,128)S(1)}, f32[2,4096]{1,0:T(2,128)S(1)}, u32[]{:S(2)}, u32[]{:S(2)}) collective-permute-start(f32[2,4096]{1,0:T(2,128)S(1)} %get-tuple-element.17), channel_id=1, source_target_pairs={{0,16},{16,32},{32,48},{48,64},{64,80},{80,96},{96,112},{1,17},{17... | collective-permute-start | bytes 98312 | tf_op jit(solution)/shard_map/ppermute | solution.py:19
  117.4 4.7 %collective-permute-start.5 = (f32[2,4096]{1,0:T(2,128)S(1)}, f32[2,4096]{1,0:T(2,128)S(1)}, u32[]{:S(2)}, u32[]{:S(2)}) collective-permute-start(f32[2,4096]{1,0:T(2,128)S(1)} %get-tuple-element.18), channel_id=1, source_target_pairs={{16,0},{32,16},{48,32},{64,48},{80,64},{96,80},{112,96},{17,1},{33... | collective-permute-start | bytes 98312 | tf_op jit(solution)/shard_map/ppermute | solution.py:21
  250.6 5.9 %collective-permute-start.6 = (f32[2,520,2]{1,2,0:T(2,128)S(1)}, f32[2,520,2]{1,2,0:T(2,128)S(1)}, u32[]{:S(2)}, u32[]{:S(2)}) collective-permute-start(f32[2,520,2]{1,2,0:T(2,128)S(1)} %copy.10), channel_id=1, source_target_pairs={{0,1},{1,2},{2,3},{3,4},{4,5},{5,6},{6,7},{7,8},{8,9},{9,10},{10,1... | collective-permute-start | bytes 24968 | tf_op jit(solution)/shard_map/ppermute | solution.py:19
  254.0 5.0 %collective-permute-start.7 = (f32[2,520,2]{1,2,0:T(2,128)S(1)}, f32[2,520,2]{1,2,0:T(2,128)S(1)}, u32[]{:S(2)}, u32[]{:S(2)}) collective-permute-start(f32[2,520,2]{1,2,0:T(2,128)S(1)} %copy.11), channel_id=1, source_target_pairs={{1,0},{2,1},{3,2},{4,3},{5,4},{6,5},{7,6},{8,7},{9,8},{10,9},{11,1... | collective-permute-start | bytes 24968 | tf_op jit(solution)/shard_map/ppermute | solution.py:21
  259.2 1.2 copy-start.6
  260.4 2.5 copy-start.1
  260.4 2.9 %copy-start.7 = (f32[1024,512]{1,0:T(8,128)S(1)}, f32[1024,512]{1,0:T(8,128)}, u32[]{:S(2)}) copy-start(f32[1024,512]{1,0:T(8,128)} %param.5) | copy-start | bytes 6291460
Sparse Core Ops, SparseCore 0:
  26.8 53.0 all-gather.2
  113.3 108.7 all-gather.4

commit v7 on v2

--- a/solution.py
+++ b/solution.py
@@ -91,8 +91,12 @@
     side = lax.axis_index("yl")
     span = 4 * tile_cols
     quarters = range(col_kernel.shape[1] // span)
-    low = jnp.concatenate([col_kernel[:, q * span : q * span + span // 2] for q in quarters], axis=1)
-    high = jnp.concatenate([col_kernel[:, q * span + span // 2 : (q + 1) * span] for q in quarters], axis=1)
+    def half_cols(s_idx):
+        starts = [q * span + s_idx * span // 2 + c * tile_cols for c in range(2) for q in quarters]
+        return jnp.concatenate([col_kernel[:, a : a + tile_cols] for a in starts], axis=1)
+
+    low = half_cols(0)
+    high = half_cols(1)
     near_cols = jnp.where(side == 0, low, high)
     far_cols = jnp.where(side == 0, high, low)
     partner_cols = lax.ppermute(far_cols, "yl", swap)
@@ -110,7 +114,7 @@
         + exact_dot("rpq,qj->rpj", after, col_adj[-4:], True)
     )
     inducing = exact_dot("ip,rpj->rij", colsum, row_adj, False)
-    half = lax.all_gather(inducing, ("x", "core"), axis=2, tiled=True)
+    half = lax.all_gather(inducing, ("core", "x"), axis=2, tiled=True)
     near = jnp.einsum("rik,jk->rij", half, near_cols, precision=highest)
     for_partner = jnp.einsum("rik,jk->rij", half, partner_cols, precision=highest)
     mixed = near + lax.ppermute(for_partner, "yl", swap)

time: 260 us -> 261 us (level)
    unnamed x18 -> x23, local copies, waits for them, and re-layouts: 2.19 us -> 7.25 us
  transfers between devices with their start and end apart: 10 -> 10, of which waited for: 6 -> 6; matrix products, arithmetic and copies ran while one was open for 16% -> 17% of each run, Pallas kernels for 0% -> 0%
where the time goes in v7:
time: 261 us; the launch traced here: 260 us
  waiting for transfers between devices  145 us (56%)
  matrix products  35.3 us (14%)
  local copies, waits for them, and re-layouts  26.4 us (10%)
  other arithmetic  20.4 us (8%)
  starting transfers between devices  18.6 us (7%)
  between operations  13.7 us (5%)
    all_gather x1, waiting for transfers between devices, body(): lax.all_gather(mixed, ('z', 'yh'), axis=1, tiled=True)  75.3 us
    ppermute x1, waiting for transfers between devices, body(): partner_cols = lax.ppermute(far_cols, 'yl', swap)  46.1 us
    ppermute x1, waiting for transfers between devices, body(): mixed = near + lax.ppermute(for_partner, 'yl', swap)  19.8 us
    dot_general x1, matrix products, body(): jnp.einsum('ik,rkj->rij', row_big, lax.all_gather(mixed, ('z', 'yh'), axi...  12.2 us
    concatenate x1, local copies, waits for them, and re-layouts, row_windows(): jnp.concatenate([padded[:, block * w:block * w + width] for w in order],...  11.6 us
    concatenate x1, other arithmetic, with_halo(): jnp.concatenate([lax.ppermute(tail, axis, [(i, (i + 1) % count) for i in...  10.7 us
    unnamed x23, local copies, waits for them, and re-layouts  7.25 us
    dot_general x4, matrix products, exact_dot(): jnp.einsum(eq, parts, jnp.concatenate([table] * 3, axis=0), preferred_ele...  7.22 us
  transfers between devices with their start and end apart: 10, of which 6 were waited for; matrix products, arithmetic and copies ran while one was open for 17% of the time, Pallas kernels for 0%

profile of v7, /device:TPU:1, one launch (start us, length us, event | category | flops | bytes accessed | tf_op | source)
XLA Modules:
  0.0 259.6 jit_solution(685826955549442781)
XLA Ops:
  6.5 0.0 all-gather.3.cloned.1.call-start
  6.5 1.9 fusion.114
  8.4 0.3 copy.16
  8.8 4.6 %collective-permute-start = (f32[2,1024,4]{1,2,0:T(4,128)S(1)}, f32[2,1024,4]{1,2,0:T(4,128)S(1)}, u32[]{:S(2)}, u32[]{:S(2)}) collective-permute-start(f32[2,1024,4]{1,2,0:T(4,128)S(1)} %copy.16), channel_id=1, source_target_pairs={{0,1},{1,2},{2,3},{3,4},{4,5},{5,6},{6,7},{7,8},{8,9},{9,10},{10,1... | collective-permute-start | bytes 98312 | tf_op jit(solution)/shard_map/ppermute | solution.py:33
  13.4 0.3 copy.17
  13.7 1.9 collective-permute-start.1
  15.6 3.2 %reduce-precision_convert_fusion.1 = (bf16[2,1024,512]{2,1,0:T(8,128)(2,1)S(1)}, bf16[2,1024,512]{2,1,0:T(8,128)(2,1)S(1)}, bf16[2,1024,512]{2,1,0:T(8,128)(2,1)S(1)}) fusion(f32[2,1024,512]{2,1,0:T(8,128)} %param.4), kind=kLoop, calls=%fused_computation.18 | loop fusion | flops 7340032 | bytes 10485760 | tf_op jit(solution)/shard_map/convert_element_type | solution.py:64
  18.9 0.4 fusion.81
  19.2 1.3 fusion.40
  20.5 0.1 slice.144
  20.6 0.0 collective-permute-done
  20.6 0.5 fusion.84
  21.1 0.0 collective-permute-done.1
  21.2 0.5 fusion.90
  21.6 2.3 reduce-precision_convert_fusion.5
  23.9 2.8 %fusion.59 = f32[2,520,256]{2,1,0:T(8,128)} fusion(bf16[520,1024]{1,0:T(8,128)(2,1)S(1)} %fusion.40, bf16[2,1024,256]{2,1,0:T(8,128)(2,1)S(1)} %get-tuple-element.43, bf16[2,1024,256]{2,1,0:T(8,128)(2,1)S(1)} %get-tuple-element.44, bf16[2,1024,256]{2,1,0:T(8,128)(2,1)S(1)} %get-tuple-element.42), kind=kOutput, calls=%fused_computation.85 | convolution fusion | flops 1654800384 | bytes 5275648 | tf_op jit(solution)/shard_map/ip,rpj->rij/dot_general | solution.py:74
  26.7 0.0 all-gather.3.cloned.1.call-update
  26.7 0.0 all-gather.5.cloned.1.call-start
  26.8 0.0 copy-start.4
  26.8 1.2 slice_dynamic-update-slice_fusion.7
  28.0 1.3 slice_dynamic-update-slice_fusion.6
  29.3 1.1 slice_dynamic-update-slice_fusion.5
  30.4 1.1 slice_dynamic-update-slice_fusion.4
  31.4 0.0 copy-done.4
  31.6 0.0 copy-start.1
  31.6 0.3 broadcast_select_fusion
  31.9 1.0 copy-done.1
  32.9 1.1 collective-permute-start.2
  34.0 46.1 %collective-permute-done.2 = f32[256,2048]{1,0:T(8,128)} collective-permute-done((f32[256,2048]{1,0:T(8,128)S(1)}, f32[256,2048]{1,0:T(8,128)}, u32[]{:S(2)}, u32[]{:S(2)}) %collective-permute-start.2) | collective-permute-done | bytes 2097184 | tf_op jit(solution)/shard_map/ppermute | solution.py:102
  80.2 0.5 all-gather.3.cloned.1.call-done
  80.7 7.0 %fusion.49 = f32[2,520,256]{2,1,0:T(8,128)S(1)} fusion(f32[2,520,2048]{2,1,0:T(8,128)} %all-gather.3.cloned.1.call-done, f32[256,2048]{1,0:T(8,128)} %collective-permute-done.2), kind=kOutput, calls=%fused_computation.77 | convolution fusion | flops 3271557120 | bytes 11681792 | tf_op jit(solution)/shard_map/rik,jk->rij/dot_general | solution.py:119
  87.7 1.5 collective-permute-start.3
  89.2 0.0 copy-done
  89.2 0.0 copy-done.2
  89.2 3.6 %fusion.51 = f32[2,520,256]{2,1,0:T(8,128)S(1)} fusion(f32[2,520,2048]{2,1,0:T(8,128)S(1)} %copy-done, f32[256,2048]{1,0:T(8,128)S(1)} %copy-done.2, f32[256,2048]{1,0:T(8,128)S(1)} %get-tuple-element.15, pred[]{:T(512)S(6)} %eq.4), kind=kOutput, calls=%fused_computation.79 | convolution fusion | flops 3272081408 | bytes 13778945 | tf_op jit(solution)/shard_map/rik,jk->rij/dot_general | solution.py:118
  92.8 19.8 %collective-permute-done.3 = f32[2,520,256]{2,1,0:T(8,128)S(1)} collective-permute-done((f32[2,520,256]{2,1,0:T(8,128)S(1)}, f32[2,520,256]{2,1,0:T(8,128)S(1)}, u32[]{:S(2)}, u32[]{:S(2)}) %collective-permute-start.3) | collective-permute-done | bytes 1064992 | tf_op jit(solution)/shard_map/ppermute | solution.py:120
  112.6 1.1 add.216
  113.7 0.0 all-gather.5.cloned.1.call-update
  113.7 1.0 fusion.113
  114.7 2.8 %collective-permute-start.4 = (f32[2,4096]{1,0:T(2,128)S(1)}, f32[2,4096]{1,0:T(2,128)S(1)}, u32[]{:S(2)}, u32[]{:S(2)}) collective-permute-start(f32[2,4096]{1,0:T(2,128)S(1)} %get-tuple-element.13), channel_id=1, source_target_pairs={{0,16},{16,32},{32,48},{48,64},{64,80},{80,96},{96,112},{1,17},{17... | collective-permute-start | bytes 98312 | tf_op jit(solution)/shard_map/ppermute | solution.py:19
  117.5 1.3 collective-permute-start.5
  118.8 2.3 fusion.43
  121.1 0.0 collective-permute-done.4
  121.1 1.1 collective-permute-done.5
  122.2 10.7 %select_maximum_fusion = f32[520,4104]{1,0:T(8,128)S(1)} fusion(f32[2,4096]{1,0:T(2,128)S(1)} %collective-permute-done.5, f32[512,4096]{1,0:T(8,128)} %param.6, f32[2,4096]{1,0:T(2,128)S(1)} %collective-permute-done.4), kind=kLoop, calls=%fused_computation.2 | loop fusion | flops 27743040 | bytes 16990464 | tf_op jit(solution)/shard_map/concatenate | solution.py:17
  132.9 3.4 %fusion.112 = (f32[520,520]{1,0:T(8,128)S(1)}, f32[520,520]{1,0:T(8,128)S(1)}, f32[520,520]{1,0:T(8,128)}, f32[520,520]{1,0:T(8,128)}, f32[520,520]{1,0:T(8,128)...) fusion(f32[520,4104]{1,0:T(8,128)S(1)} %select_maximum_fusion), kind=kLoop, calls=%fused_computation.172 | loop fusion | bytes 17305600 | tf_op jit(solution)/shard_map/slice | solution.py:79
  136.4 11.6 %concatenate.62 = f32[520,4160]{1,0:T(8,128)} concatenate(f32[520,520]{1,0:T(8,128)} %get-tuple-element.12, f32[520,520]{1,0:T(8,128)} %get-tuple-element.11, f32[520,520]{1,0:T(8,128)} %get-tuple-element.10, f32[520,520]{1,0:T(8,128)} %get-tuple-element.9, f32[520,520]{1,0:T(8,128)} %get-tuple-element.8, f32[520,520]{1,0:T(8,128)} %get-tuple-element.7, ...), dimensions={1} | concatenate | bytes 17305600 | tf_op jit(solution)/shard_map/concatenate | solution.py:79
  148.0 75.3 %all-gather.5.cloned.1.call-done = f32[2,4160,256]{2,1,0:T(8,128)} async-done(((f32[2,520,256]{2,1,0:T(8,128)}), f32[2,4160,256]{2,1,0:T(8,128)}) %all-gather.5.cloned.1.call-update) | async-done | bytes 8519696 | tf_op jit(solution)/shard_map/all_gather | solution.py:122
  223.3 12.2 %fusion.62 = f32[2,520,256]{2,1,0:T(8,128)S(1)} fusion(f32[2,4160,256]{2,1,0:T(8,128)} %all-gather.5.cloned.1.call-done, f32[520,4160]{1,0:T(8,128)} %concatenate.62), kind=kOutput, calls=%fused_computation.86 | convolution fusion | flops 6645350400 | bytes 18237440 | tf_op jit(solution)/shard_map/ik,rkj->rij/dot_general | solution.py:121
  235.5 0.2 fusion.115
  235.8 0.2 copy.10
  236.0 3.2 %collective-permute-start.6 = (f32[2,520,2]{1,2,0:T(2,128)S(1)}, f32[2,520,2]{1,2,0:T(2,128)S(1)}, u32[]{:S(2)}, u32[]{:S(2)}) collective-permute-start(f32[2,520,2]{1,2,0:T(2,128)S(1)} %copy.10), channel_id=1, source_target_pairs={{0,1},{1,2},{2,3},{3,4},{4,5},{5,6},{6,7},{7,8},{8,9},{9,10},{10,1... | collective-permute-start | bytes 24968 | tf_op jit(solution)/shard_map/ppermute | solution.py:19
  239.2 0.2 copy.11
  239.4 2.1 collective-permute-start.7
  241.5 0.4 fusion.76
  241.9 0.0 collective-permute-done.6
  241.9 0.2 copy.12
  242.2 2.2 collective-permute-done.7
  244.4 0.2 copy.13
  244.6 0.7 reduce-precision_convert_fusion.7
  245.3 0.5 copy-done.5
  245.9 2.5 reduce-precision_convert_fusion.3
  248.4 0.3 copy-done.6
  248.7 4.0 %multiply_add_fusion = f32[2,1024,512]{2,1,0:T(8,128)} fusion(f32[2,1024,512]{2,1,0:T(8,128)S(1)} %copy-done.3, f32[1024,512]{1,0:T(8,128)S(1)} %copy-done.6, bf16[2,1024,260]{1,2,0:T(8,128)(2,1)S(1)} %get-tuple-element.37, bf16[2,1024,260]{1,2,0:T(8,128)(2,1)S(1)} %get-tuple-element.38, bf16[2,1024,260]{1,2,0:T(8,128)(2,1)S(1)} %get-tuple-element.36, ...), kind=kOutput, calls=%fused_computation.20 | convolution fusion | flops 1649856512 | bytes 13946880 | tf_op jit(solution)/shard_map/rpj,jq->rpq/dot_general | solution.py:72
  (18 shorter events, 0.3 us)
Async XLA Ops:
  6.5 74.1 %all-gather.3.cloned.1.call-start = ((), (), s32[]{:S(2)}) async-start(), calls=%async_computation | async-start | bytes 9584640 | tf_op jit(solution)/shard_map/all_gather | solution.py:117
  8.8 11.8 %collective-permute-start = (f32[2,1024,4]{1,2,0:T(4,128)S(1)}, f32[2,1024,4]{1,2,0:T(4,128)S(1)}, u32[]{:S(2)}, u32[]{:S(2)}) collective-permute-start(f32[2,1024,4]{1,2,0:T(4,128)S(1)} %copy.16), channel_id=1, source_target_pairs={{0,1},{1,2},{2,3},{3,4},{4,5},{5,6},{6,7},{7,8},{8,9},{9,10},{10,1... | collective-permute-start | bytes 98312 | tf_op jit(solution)/shard_map/ppermute | solution.py:33
  13.7 7.4 %collective-permute-start.1 = (f32[2,1024,4]{1,2,0:T(4,128)S(1)}, f32[2,1024,4]{1,2,0:T(4,128)S(1)}, u32[]{:S(2)}, u32[]{:S(2)}) collective-permute-start(f32[2,1024,4]{1,2,0:T(4,128)S(1)} %copy.17), channel_id=1, source_target_pairs={{1,0},{2,1},{3,2},{4,3},{5,4},{6,5},{7,6},{8,7},{9,8},{10,9},{11,1... | collective-permute-start | bytes 98312 | tf_op jit(solution)/shard_map/ppermute | solution.py:34
  26.7 196.6 %all-gather.5.cloned.1.call-start = ((), (), s32[]{:S(2)}) async-start(), calls=%async_computation.1 | async-start | bytes 9584640 | tf_op jit(solution)/shard_map/all_gather | solution.py:122
  26.8 4.7 %copy-start.4 = (f32[256,4096]{1,0:T(8,128)S(1)}, f32[256,4096]{1,0:T(8,128)}, u32[]{:S(2)}) copy-start(f32[256,4096]{1,0:T(8,128)} %param.7) | copy-start | bytes 12582916
  31.6 1.3 copy-start.1
  32.9 47.2 %collective-permute-start.2 = (f32[256,2048]{1,0:T(8,128)S(1)}, f32[256,2048]{1,0:T(8,128)}, u32[]{:S(2)}, u32[]{:S(2)}) collective-permute-start(f32[256,2048]{1,0:T(8,128)S(1)} %broadcast_select_fusion), channel_id=1, source_target_pairs={{0,2},{2,0},{1,3},{3,1},{4,6},{6,4},{5,7},{7,5},{8,10},{10,8},{9,1... | collective-permute-start | bytes 6291464 | tf_op jit(solution)/shard_map/ppermute | solution.py:102
  80.7 8.5 %copy-start = (f32[2,520,2048]{2,1,0:T(8,128)S(1)}, f32[2,520,2048]{2,1,0:T(8,128)}, u32[]{:S(2)}) copy-start(f32[2,520,2048]{2,1,0:T(8,128)} %all-gather.3.cloned.1.call-done) | copy-start | bytes 25559044
  80.7 8.5 %copy-start.2 = (f32[256,2048]{1,0:T(8,128)S(1)}, f32[256,2048]{1,0:T(8,128)}, u32[]{:S(2)}) copy-start(f32[256,2048]{1,0:T(8,128)} %copy-done.1) | copy-start | bytes 6291460
  87.7 24.9 %collective-permute-start.3 = (f32[2,520,256]{2,1,0:T(8,128)S(1)}, f32[2,520,256]{2,1,0:T(8,128)S(1)}, u32[]{:S(2)}, u32[]{:S(2)}) collective-permute-start(f32[2,520,256]{2,1,0:T(8,128)S(1)} %fusion.49), channel_id=1, source_target_pairs={{0,2},{2,0},{1,3},{3,1},{4,6},{6,4},{5,7},{7,5},{8,10},{10,8},{9,1... | collective-permute-start | bytes 3194888 | tf_op jit(solution)/shard_map/ppermute | solution.py:120
  114.7 6.4 %collective-permute-start.4 = (f32[2,4096]{1,0:T(2,128)S(1)}, f32[2,4096]{1,0:T(2,128)S(1)}, u32[]{:S(2)}, u32[]{:S(2)}) collective-permute-start(f32[2,4096]{1,0:T(2,128)S(1)} %get-tuple-element.13), channel_id=1, source_target_pairs={{0,16},{16,32},{32,48},{48,64},{64,80},{80,96},{96,112},{1,17},{17... | collective-permute-start | bytes 98312 | tf_op jit(solution)/shard_map/ppermute | solution.py:19
  117.5 4.7 %collective-permute-start.5 = (f32[2,4096]{1,0:T(2,128)S(1)}, f32[2,4096]{1,0:T(2,128)S(1)}, u32[]{:S(2)}, u32[]{:S(2)}) collective-permute-start(f32[2,4096]{1,0:T(2,128)S(1)} %get-tuple-element.14), channel_id=1, source_target_pairs={{16,0},{32,16},{48,32},{64,48},{80,64},{96,80},{112,96},{17,1},{33... | collective-permute-start | bytes 98312 | tf_op jit(solution)/shard_map/ppermute | solution.py:21
  236.0 5.9 %collective-permute-start.6 = (f32[2,520,2]{1,2,0:T(2,128)S(1)}, f32[2,520,2]{1,2,0:T(2,128)S(1)}, u32[]{:S(2)}, u32[]{:S(2)}) collective-permute-start(f32[2,520,2]{1,2,0:T(2,128)S(1)} %copy.10), channel_id=1, source_target_pairs={{0,1},{1,2},{2,3},{3,4},{4,5},{5,6},{6,7},{7,8},{8,9},{9,10},{10,1... | collective-permute-start | bytes 24968 | tf_op jit(solution)/shard_map/ppermute | solution.py:19
  239.4 5.0 %collective-permute-start.7 = (f32[2,520,2]{1,2,0:T(2,128)S(1)}, f32[2,520,2]{1,2,0:T(2,128)S(1)}, u32[]{:S(2)}, u32[]{:S(2)}) collective-permute-start(f32[2,520,2]{1,2,0:T(2,128)S(1)} %copy.11), channel_id=1, source_target_pairs={{1,0},{2,1},{3,2},{4,3},{5,4},{6,5},{7,6},{8,7},{9,8},{10,9},{11,1... | collective-permute-start | bytes 24968 | tf_op jit(solution)/shard_map/ppermute | solution.py:21
  244.6 1.2 copy-start.5
  245.9 2.5 copy-start.3
  245.9 2.9 %copy-start.6 = (f32[1024,512]{1,0:T(8,128)S(1)}, f32[1024,512]{1,0:T(8,128)}, u32[]{:S(2)}) copy-start(f32[1024,512]{1,0:T(8,128)} %param.5) | copy-start | bytes 6291460
Sparse Core Ops, SparseCore 0:
  26.8 53.7 all-gather.2
  113.8 109.4 all-gather.4

commit v8 on v2

--- a/solution.py
+++ b/solution.py
@@ -106,8 +106,12 @@
     row_adj = tap_table(ext_rows, 2 * tile_rows, True, 2)
     colsum = (
         exact_dot("rpq,qj->rpj", observed, col_adj[4:-4], True)
-        + exact_dot("rpq,qj->rpj", before, col_adj[:4], True)
-        + exact_dot("rpq,qj->rpj", after, col_adj[-4:], True)
+        + exact_dot(
+            "rpq,qj->rpj",
+            jnp.concatenate([before, after], axis=2),
+            jnp.concatenate([col_adj[:4], col_adj[-4:]], axis=0),
+            True,
+        )
     )
     inducing = exact_dot("ip,rpj->rij", colsum, row_adj, False)
     half = lax.all_gather(inducing, ("x", "core"), axis=2, tiled=True)

time: 260 us -> 265 us (1.019)
    convert_element_type x4 -> x3, other arithmetic: 3.94 us -> 5.97 us  [split3(): hi.astype(jnp.bfloat16)]
    dot_general x4 -> x3, matrix products: 7.21 us -> 7.72 us  [exact_dot(): jnp.einsum(eq, parts, jnp.concatenate([table] * 3, axis=0), preferred_ele...]
  transfers between devices with their start and end apart: 10 -> 10, of which waited for: 6 -> 6; matrix products, arithmetic and copies ran while one was open for 16% -> 17% of each run, Pallas kernels for 0% -> 0%
where the time goes in v8:
time: 265 us; the launch traced here: 263 us
  waiting for transfers between devices  147 us (55%)
  matrix products  35.7 us (13%)
  local copies, waits for them, and re-layouts  25.6 us (10%)
  other arithmetic  22.6 us (9%)
  starting transfers between devices  19 us (7%)
  between operations  13.7 us (5%)
    all_gather x1, waiting for transfers between devices, body(): lax.all_gather(mixed, ('z', 'yh'), axis=1, tiled=True)  73.9 us
    ppermute x1, waiting for transfers between devices, body(): partner_cols = lax.ppermute(far_cols, 'yl', swap)  46.1 us
    ppermute x1, waiting for transfers between devices, body(): mixed = near + lax.ppermute(for_partner, 'yl', swap)  20.1 us
    dot_general x1, matrix products, body(): jnp.einsum('ik,rkj->rij', row_big, lax.all_gather(mixed, ('z', 'yh'), axi...  12.2 us
    concatenate x1, local copies, waits for them, and re-layouts, row_windows(): jnp.concatenate([padded[:, block * w:block * w + width] for w in order],...  11.6 us
    concatenate x1, other arithmetic, with_halo(): jnp.concatenate([lax.ppermute(tail, axis, [(i, (i + 1) % count) for i in...  11 us
    dot_general x3, matrix products, exact_dot(): jnp.einsum(eq, parts, jnp.concatenate([table] * 3, axis=0), preferred_ele...  7.72 us
    dot_general x1, matrix products, body(): jnp.einsum('rik,jk->rij', half, partner_cols, precision=highest)  6.93 us
  transfers between devices with their start and end apart: 10, of which 6 were waited for; matrix products, arithmetic and copies ran while one was open for 17% of the time, Pallas kernels for 0%

profile of v8, /device:TPU:1, one launch (start us, length us, event | category | flops | bytes accessed | tf_op | source)
XLA Modules:
  0.0 263.1 jit_solution(3624611745446575802)
XLA Ops:
  6.5 0.0 all-gather.3.cloned.1.call-start
  6.5 1.9 fusion.103
  8.4 0.3 copy.16
  8.8 4.6 %collective-permute-start = (f32[2,1024,4]{1,2,0:T(4,128)S(1)}, f32[2,1024,4]{1,2,0:T(4,128)S(1)}, u32[]{:S(2)}, u32[]{:S(2)}) collective-permute-start(f32[2,1024,4]{1,2,0:T(4,128)S(1)} %copy.16), channel_id=1, source_target_pairs={{0,1},{1,2},{2,3},{3,4},{4,5},{5,6},{6,7},{7,8},{8,9},{9,10},{10,1... | collective-permute-start | bytes 98312 | tf_op jit(solution)/shard_map/ppermute | solution.py:33
  13.4 0.9 copy.17
  14.3 1.9 collective-permute-start.1
  16.2 5.2 %reduce-precision_convert_fusion.1 = (bf16[2,1024,512]{2,1,0:T(8,128)(2,1)S(1)}, bf16[2,1024,512]{2,1,0:T(8,128)(2,1)}, bf16[2,1024,512]{2,1,0:T(8,128)(2,1)}) fusion(f32[2,1024,512]{2,1,0:T(8,128)} %param.4), kind=kLoop, calls=%fused_computation.18 | loop fusion | flops 7340032 | bytes 10485760 | tf_op jit(solution)/shard_map/convert_element_type | solution.py:64
  21.5 0.4 fusion.83
  21.8 1.3 fusion.40
  23.1 0.1 slice.112
  23.2 0.1 concatenate.54
  23.3 0.0 collective-permute-done
  23.3 0.0 collective-permute-done.1
  23.3 0.5 fusion.86
  23.8 1.1 copy-done.6
  24.9 3.2 %reduce-precision_convert_fusion.5 = (bf16[2,1024,256]{2,1,0:T(8,128)(2,1)S(1)}, bf16[2,1024,256]{2,1,0:T(8,128)(2,1)S(1)}, bf16[2,1024,256]{2,1,0:T(8,128)(2,1)S(1)}) fusion(f32[2,1024,256]{2,1,0:T(8,128)S(1)} %fusion.86, bf16[512,256]{1,0:T(8,128)(2,1)S(1)} %slice.112, bf16[2,1024,512]{2,1,0:T(8,128)(2,1)S(1)} %copy-done.6, ...), kind=kOutput, calls=%fused_computation.53 | convolution fusion | flops 1636040704 | bytes 11796480 | tf_op jit(solution)/shard_map/rpq,qj->rpj/dot_general | solution.py:72
  28.1 2.8 %fusion.60 = f32[2,520,256]{2,1,0:T(8,128)} fusion(bf16[520,1024]{1,0:T(8,128)(2,1)S(1)} %fusion.40, bf16[2,1024,256]{2,1,0:T(8,128)(2,1)S(1)} %get-tuple-element.35, bf16[2,1024,256]{2,1,0:T(8,128)(2,1)S(1)} %get-tuple-element.36, bf16[2,1024,256]{2,1,0:T(8,128)(2,1)S(1)} %get-tuple-element.34), kind=kOutput, calls=%fused_computation.87 | convolution fusion | flops 1654800384 | bytes 5275648 | tf_op jit(solution)/shard_map/ip,rpj->rij/dot_general | solution.py:74
  30.9 0.0 all-gather.3.cloned.1.call-update
  30.9 0.0 all-gather.5.cloned.1.call-start
  31.0 2.6 fusion.102
  33.6 0.0 copy-start.2
  33.6 0.0 copy-start.4
  33.6 0.3 fusion.66
  33.9 0.5 copy-done.2
  34.4 0.1 copy-done.4
  34.6 1.1 collective-permute-start.2
  35.7 46.1 %collective-permute-done.2 = f32[256,2048]{1,0:T(8,128)} collective-permute-done((f32[256,2048]{1,0:T(8,128)S(1)}, f32[256,2048]{1,0:T(8,128)}, u32[]{:S(2)}, u32[]{:S(2)}) %collective-permute-start.2) | collective-permute-done | bytes 2097184 | tf_op jit(solution)/shard_map/ppermute | solution.py:98
  81.8 3.0 %all-gather.3.cloned.1.call-done = f32[2,520,2048]{2,1,0:T(8,128)} async-done(((f32[2,520,256]{2,1,0:T(8,128)}), f32[2,520,2048]{2,1,0:T(8,128)}) %all-gather.3.cloned.1.call-update) | async-done | bytes 8519696 | tf_op jit(solution)/shard_map/all_gather | solution.py:117
  84.9 6.9 %fusion.49 = f32[2,520,256]{2,1,0:T(8,128)S(1)} fusion(f32[2,520,2048]{2,1,0:T(8,128)} %all-gather.3.cloned.1.call-done, f32[256,2048]{1,0:T(8,128)} %collective-permute-done.2), kind=kOutput, calls=%fused_computation.79 | convolution fusion | flops 3271557120 | bytes 11681792 | tf_op jit(solution)/shard_map/rik,jk->rij/dot_general | solution.py:119
  91.8 1.5 collective-permute-start.3
  93.3 0.0 copy-done
  93.3 0.0 copy-done.3
  93.3 0.0 copy-done.5
  93.3 3.5 %fusion.51 = f32[2,520,256]{2,1,0:T(8,128)S(1)} fusion(f32[2,520,2048]{2,1,0:T(8,128)S(1)} %copy-done, f32[256,512]{1,0:T(8,128)S(1)} %copy-done.3, f32[256,512]{1,0:T(8,128)S(1)} %copy-done.5, f32[256,512]{1,0:T(8,128)S(1)} %get-tuple-element.16, f32[256,512]{1,0:T(8,128)S(1)} %get-tuple-element.17, f32[256,512]{1,0:T(8,128)S(1)} %get-tuple-element.18, ...), kind=kOutput, calls=%fused_computation.81 | convolution fusion | flops 3275227136 | bytes 13778945 | tf_op jit(solution)/shard_map/rik,jk->rij/dot_general | solution.py:118
  96.9 20.1 %collective-permute-done.3 = f32[2,520,256]{2,1,0:T(8,128)S(1)} collective-permute-done((f32[2,520,256]{2,1,0:T(8,128)S(1)}, f32[2,520,256]{2,1,0:T(8,128)S(1)}, u32[]{:S(2)}, u32[]{:S(2)}) %collective-permute-start.3) | collective-permute-done | bytes 1064992 | tf_op jit(solution)/shard_map/ppermute | solution.py:120
  116.9 1.1 add.212
  118.1 0.0 all-gather.5.cloned.1.call-update
  118.1 1.0 fusion.101
  119.1 3.2 %collective-permute-start.4 = (f32[2,4096]{1,0:T(2,128)S(1)}, f32[2,4096]{1,0:T(2,128)S(1)}, u32[]{:S(2)}, u32[]{:S(2)}) collective-permute-start(f32[2,4096]{1,0:T(2,128)S(1)} %get-tuple-element.13), channel_id=1, source_target_pairs={{0,16},{16,32},{32,48},{48,64},{64,80},{80,96},{96,112},{1,17},{17... | collective-permute-start | bytes 98312 | tf_op jit(solution)/shard_map/ppermute | solution.py:19
  122.3 1.3 collective-permute-start.5
  123.6 2.3 fusion.43
  125.9 0.0 collective-permute-done.4
  125.9 1.1 collective-permute-done.5
  127.0 11.0 %select_maximum_fusion = f32[520,4104]{1,0:T(8,128)S(1)} fusion(f32[2,4096]{1,0:T(2,128)S(1)} %collective-permute-done.5, f32[512,4096]{1,0:T(8,128)} %param.6, f32[2,4096]{1,0:T(2,128)S(1)} %collective-permute-done.4), kind=kLoop, calls=%fused_computation.2 | loop fusion | flops 27743040 | bytes 16990464 | tf_op jit(solution)/shard_map/concatenate | solution.py:17
  137.9 3.4 %fusion.100 = (f32[520,520]{1,0:T(8,128)S(1)}, f32[520,520]{1,0:T(8,128)S(1)}, f32[520,520]{1,0:T(8,128)}, f32[520,520]{1,0:T(8,128)}, f32[520,520]{1,0:T(8,128)...) fusion(f32[520,4104]{1,0:T(8,128)S(1)} %select_maximum_fusion), kind=kLoop, calls=%fused_computation.139 | loop fusion | bytes 17305600 | tf_op jit(solution)/shard_map/slice | solution.py:79
  141.3 11.6 %concatenate.60 = f32[520,4160]{1,0:T(8,128)} concatenate(f32[520,520]{1,0:T(8,128)} %get-tuple-element.12, f32[520,520]{1,0:T(8,128)} %get-tuple-element.11, f32[520,520]{1,0:T(8,128)} %get-tuple-element.10, f32[520,520]{1,0:T(8,128)} %get-tuple-element.9, f32[520,520]{1,0:T(8,128)} %get-tuple-element.8, f32[520,520]{1,0:T(8,128)} %get-tuple-element.7, ...), dimensions={1} | concatenate | bytes 17305600 | tf_op jit(solution)/shard_map/concatenate | solution.py:79
  153.0 73.9 %all-gather.5.cloned.1.call-done = f32[2,4160,256]{2,1,0:T(8,128)} async-done(((f32[2,520,256]{2,1,0:T(8,128)}), f32[2,4160,256]{2,1,0:T(8,128)}) %all-gather.5.cloned.1.call-update) | async-done | bytes 8519696 | tf_op jit(solution)/shard_map/all_gather | solution.py:122
  226.9 12.2 %fusion.63 = f32[2,520,256]{2,1,0:T(8,128)S(1)} fusion(f32[2,4160,256]{2,1,0:T(8,128)} %all-gather.5.cloned.1.call-done, f32[520,4160]{1,0:T(8,128)} %concatenate.60), kind=kOutput, calls=%fused_computation.88 | convolution fusion | flops 6645350400 | bytes 18237440 | tf_op jit(solution)/shard_map/ik,rkj->rij/dot_general | solution.py:121
  239.1 0.2 fusion.104
  239.3 0.2 copy.10
  239.6 3.2 %collective-permute-start.6 = (f32[2,520,2]{1,2,0:T(2,128)S(1)}, f32[2,520,2]{1,2,0:T(2,128)S(1)}, u32[]{:S(2)}, u32[]{:S(2)}) collective-permute-start(f32[2,520,2]{1,2,0:T(2,128)S(1)} %copy.10), channel_id=1, source_target_pairs={{0,1},{1,2},{2,3},{3,4},{4,5},{5,6},{6,7},{7,8},{8,9},{9,10},{10,1... | collective-permute-start | bytes 24968 | tf_op jit(solution)/shard_map/ppermute | solution.py:19
  242.7 0.2 copy.11
  243.0 2.1 collective-permute-start.7
  245.1 0.4 fusion.78
  245.5 0.0 collective-permute-done.6
  245.5 0.2 copy.12
  245.7 2.2 collective-permute-done.7
  248.0 0.2 copy.13
  248.2 0.7 reduce-precision_convert_fusion.7
  248.9 0.5 copy-done.7
  249.4 2.5 reduce-precision_convert_fusion.3
  252.0 0.0 copy-done.1
  252.0 0.3 copy-done.8
  252.3 4.0 %multiply_add_fusion = f32[2,1024,512]{2,1,0:T(8,128)} fusion(f32[2,1024,512]{2,1,0:T(8,128)S(1)} %copy-done.1, f32[1024,512]{1,0:T(8,128)S(1)} %copy-done.8, bf16[2,1024,260]{1,2,0:T(8,128)(2,1)S(1)} %get-tuple-element.29, bf16[2,1024,260]{1,2,0:T(8,128)(2,1)S(1)} %get-tuple-element.30, bf16[2,1024,260]{1,2,0:T(8,128)(2,1)S(1)} %get-tuple-element.28, ...), kind=kOutput, calls=%fused_computation.20 | convolution fusion | flops 1649856512 | bytes 13946880 | tf_op jit(solution)/shard_map/rpj,jq->rpq/dot_general | solution.py:72
  (14 shorter events, 0.1 us)
Async XLA Ops:
  6.5 78.3 %all-gather.3.cloned.1.call-start = ((), (), s32[]{:S(2)}) async-start(), calls=%async_computation | async-start | bytes 9584640 | tf_op jit(solution)/shard_map/all_gather | solution.py:117
  8.8 14.5 %collective-permute-start = (f32[2,1024,4]{1,2,0:T(4,128)S(1)}, f32[2,1024,4]{1,2,0:T(4,128)S(1)}, u32[]{:S(2)}, u32[]{:S(2)}) collective-permute-start(f32[2,1024,4]{1,2,0:T(4,128)S(1)} %copy.16), channel_id=1, source_target_pairs={{0,1},{1,2},{2,3},{3,4},{4,5},{5,6},{6,7},{7,8},{8,9},{9,10},{10,1... | collective-permute-start | bytes 98312 | tf_op jit(solution)/shard_map/ppermute | solution.py:33
  14.3 9.0 %collective-permute-start.1 = (f32[2,1024,4]{1,2,0:T(4,128)}, f32[2,1024,4]{1,2,0:T(4,128)S(1)}, u32[]{:S(2)}, u32[]{:S(2)}) collective-permute-start(f32[2,1024,4]{1,2,0:T(4,128)} %copy.17), channel_id=1, source_target_pairs={{1,0},{2,1},{3,2},{4,3},{5,4},{6,5},{7,6},{8,7},{9,8},{10,9},{11,1... | collective-permute-start | bytes 98312 | tf_op jit(solution)/shard_map/ppermute | solution.py:34
  23.3 1.6 copy-start.6
  30.9 196.0 %all-gather.5.cloned.1.call-start = ((), (), s32[]{:S(2)}) async-start(), calls=%async_computation.1 | async-start | bytes 9584640 | tf_op jit(solution)/shard_map/all_gather | solution.py:122
  33.6 0.8 copy-start.2
  33.6 1.0 copy-start.4
  34.6 47.2 %collective-permute-start.2 = (f32[256,2048]{1,0:T(8,128)S(1)}, f32[256,2048]{1,0:T(8,128)}, u32[]{:S(2)}, u32[]{:S(2)}) collective-permute-start(f32[256,2048]{1,0:T(8,128)S(1)} %fusion.66), channel_id=1, source_target_pairs={{0,2},{2,0},{1,3},{3,1},{4,6},{6,4},{5,7},{7,5},{8,10},{10,8},{9,1... | collective-permute-start | bytes 6291464 | tf_op jit(solution)/shard_map/ppermute | solution.py:98
  84.9 8.4 %copy-start = (f32[2,520,2048]{2,1,0:T(8,128)S(1)}, f32[2,520,2048]{2,1,0:T(8,128)}, u32[]{:S(2)}) copy-start(f32[2,520,2048]{2,1,0:T(8,128)} %all-gather.3.cloned.1.call-done) | copy-start | bytes 25559044
  84.9 8.4 %copy-start.3 = (f32[256,512]{1,0:T(8,128)S(1)}, f32[256,512]{1,0:T(8,128)}, u32[]{:S(2)}) copy-start(f32[256,512]{1,0:T(8,128)} %copy-done.2) | copy-start | bytes 1572868
  84.9 8.4 %copy-start.5 = (f32[256,512]{1,0:T(8,128)S(1)}, f32[256,512]{1,0:T(8,128)}, u32[]{:S(2)}) copy-start(f32[256,512]{1,0:T(8,128)} %copy-done.4) | copy-start | bytes 1572868
  91.8 25.1 %collective-permute-start.3 = (f32[2,520,256]{2,1,0:T(8,128)S(1)}, f32[2,520,256]{2,1,0:T(8,128)S(1)}, u32[]{:S(2)}, u32[]{:S(2)}) collective-permute-start(f32[2,520,256]{2,1,0:T(8,128)S(1)} %fusion.49), channel_id=1, source_target_pairs={{0,2},{2,0},{1,3},{3,1},{4,6},{6,4},{5,7},{7,5},{8,10},{10,8},{9,1... | collective-permute-start | bytes 3194888 | tf_op jit(solution)/shard_map/ppermute | solution.py:120
  119.1 6.8 %collective-permute-start.4 = (f32[2,4096]{1,0:T(2,128)S(1)}, f32[2,4096]{1,0:T(2,128)S(1)}, u32[]{:S(2)}, u32[]{:S(2)}) collective-permute-start(f32[2,4096]{1,0:T(2,128)S(1)} %get-tuple-element.13), channel_id=1, source_target_pairs={{0,16},{16,32},{32,48},{48,64},{64,80},{80,96},{96,112},{1,17},{17... | collective-permute-start | bytes 98312 | tf_op jit(solution)/shard_map/ppermute | solution.py:19
  122.3 4.7 %collective-permute-start.5 = (f32[2,4096]{1,0:T(2,128)S(1)}, f32[2,4096]{1,0:T(2,128)S(1)}, u32[]{:S(2)}, u32[]{:S(2)}) collective-permute-start(f32[2,4096]{1,0:T(2,128)S(1)} %get-tuple-element.14), channel_id=1, source_target_pairs={{16,0},{32,16},{48,32},{64,48},{80,64},{96,80},{112,96},{17,1},{33... | collective-permute-start | bytes 98312 | tf_op jit(solution)/shard_map/ppermute | solution.py:21
  239.6 5.9 %collective-permute-start.6 = (f32[2,520,2]{1,2,0:T(2,128)S(1)}, f32[2,520,2]{1,2,0:T(2,128)S(1)}, u32[]{:S(2)}, u32[]{:S(2)}) collective-permute-start(f32[2,520,2]{1,2,0:T(2,128)S(1)} %copy.10), channel_id=1, source_target_pairs={{0,1},{1,2},{2,3},{3,4},{4,5},{5,6},{6,7},{7,8},{8,9},{9,10},{10,1... | collective-permute-start | bytes 24968 | tf_op jit(solution)/shard_map/ppermute | solution.py:19
  243.0 5.0 %collective-permute-start.7 = (f32[2,520,2]{1,2,0:T(2,128)S(1)}, f32[2,520,2]{1,2,0:T(2,128)S(1)}, u32[]{:S(2)}, u32[]{:S(2)}) collective-permute-start(f32[2,520,2]{1,2,0:T(2,128)S(1)} %copy.11), channel_id=1, source_target_pairs={{1,0},{2,1},{3,2},{4,3},{5,4},{6,5},{7,6},{8,7},{9,8},{10,9},{11,1... | collective-permute-start | bytes 24968 | tf_op jit(solution)/shard_map/ppermute | solution.py:21
  248.2 1.2 copy-start.7
  249.4 2.5 copy-start.1
  249.4 2.9 %copy-start.8 = (f32[1024,512]{1,0:T(8,128)S(1)}, f32[1024,512]{1,0:T(8,128)}, u32[]{:S(2)}) copy-start(f32[1024,512]{1,0:T(8,128)} %param.5) | copy-start | bytes 6291460
Sparse Core Ops, SparseCore 0:
  31.1 53.7 all-gather.2
  118.2 108.6 all-gather.4

commit v9 on v2

--- a/solution.py
+++ b/solution.py
@@ -111,8 +111,9 @@
     )
     inducing = exact_dot("ip,rpj->rij", colsum, row_adj, False)
     half = lax.all_gather(inducing, ("x", "core"), axis=2, tiled=True)
-    near = jnp.einsum("rik,jk->rij", half, near_cols, precision=highest)
-    for_partner = jnp.einsum("rik,jk->rij", half, partner_cols, precision=highest)
+    both = jnp.einsum("rik,jk->rij", half, jnp.concatenate([near_cols, partner_cols], axis=0), precision=highest)
+    near = both[..., :tile_cols]
+    for_partner = both[..., tile_cols:]
     mixed = near + lax.ppermute(for_partner, "yl", swap)
     product = jnp.einsum(
         "ik,rkj->rij", row_big, lax.all_gather(mixed, ("z", "yh"), axis=1, tiled=True), precision=highest

time: 260 us -> 263 us (1.012)
  waiting for transfers between devices: 147 us -> 150 us
    ppermute x1, waiting for transfers between devices: 20.1 us -> 23.6 us  [body(): mixed = near + lax.ppermute(for_partner, 'yl', swap)]
    dot_general x2 -> x1, matrix products: 10.5 us -> 9.94 us  [body(): jnp.einsum('rik,jk->rij', half, jnp.concatenate([near_cols, partner_cols]...]
  transfers between devices with their start and end apart: 10 -> 10, of which waited for: 6 -> 6; matrix products, arithmetic and copies ran while one was open for 16% -> 15% of each run, Pallas kernels for 0% -> 0%
where the time goes in v9:
time: 263 us; the launch traced here: 262 us
  waiting for transfers between devices  150 us (57%)
  matrix products  34.7 us (13%)
  local copies, waits for them, and re-layouts  23.3 us (9%)
  other arithmetic  20.9 us (8%)
  starting transfers between devices  19.1 us (7%)
  between operations  13.7 us (5%)
    all_gather x1, waiting for transfers between devices, body(): lax.all_gather(mixed, ('z', 'yh'), axis=1, tiled=True)  73.9 us
    ppermute x1, waiting for transfers between devices, body(): partner_cols = lax.ppermute(far_cols, 'yl', swap)  46.1 us
    ppermute x1, waiting for transfers between devices, body(): mixed = near + lax.ppermute(for_partner, 'yl', swap)  23.6 us
    dot_general x1, matrix products, body(): jnp.einsum('ik,rkj->rij', row_big, lax.all_gather(mixed, ('z', 'yh'), axi...  12.2 us
    concatenate x1, local copies, waits for them, and re-layouts, row_windows(): jnp.concatenate([padded[:, block * w:block * w + width] for w in order],...  11.6 us
    concatenate x1, other arithmetic, with_halo(): jnp.concatenate([lax.ppermute(tail, axis, [(i, (i + 1) % count) for i in...  11 us
    dot_general x1, matrix products, body(): jnp.einsum('rik,jk->rij', half, jnp.concatenate([near_cols, partner_cols]...  9.94 us
    dot_general x4, matrix products, exact_dot(): jnp.einsum(eq, parts, jnp.concatenate([table] * 3, axis=0), preferred_ele...  7.21 us
  transfers between devices with their start and end apart: 10, of which 6 were waited for; matrix products, arithmetic and copies ran while one was open for 15% of the time, Pallas kernels for 0%

profile of v9, /device:TPU:1, one launch (start us, length us, event | category | flops | bytes accessed | tf_op | source)
XLA Modules:
  0.0 262.0 jit_solution(1446146630531067640)
XLA Ops:
  6.5 0.0 all-gather.3.cloned.1.call-start
  6.5 1.9 fusion.115
  8.4 0.3 copy.16
  8.8 4.6 %collective-permute-start = (f32[2,1024,4]{1,2,0:T(4,128)S(1)}, f32[2,1024,4]{1,2,0:T(4,128)S(1)}, u32[]{:S(2)}, u32[]{:S(2)}) collective-permute-start(f32[2,1024,4]{1,2,0:T(4,128)S(1)} %copy.16), channel_id=1, source_target_pairs={{0,1},{1,2},{2,3},{3,4},{4,5},{5,6},{6,7},{7,8},{8,9},{9,10},{10,1... | collective-permute-start | bytes 98312 | tf_op jit(solution)/shard_map/ppermute | solution.py:33
  13.4 0.3 copy.17
  13.7 1.9 collective-permute-start.1
  15.6 3.2 %reduce-precision_convert_fusion.1 = (bf16[2,1024,512]{2,1,0:T(8,128)(2,1)S(1)}, bf16[2,1024,512]{2,1,0:T(8,128)(2,1)S(1)}, bf16[2,1024,512]{2,1,0:T(8,128)(2,1)S(1)}) fusion(f32[2,1024,512]{2,1,0:T(8,128)} %param.4), kind=kLoop, calls=%fused_computation.18 | loop fusion | flops 7340032 | bytes 10485760 | tf_op jit(solution)/shard_map/convert_element_type | solution.py:64
  18.9 0.4 fusion.80
  19.2 1.3 fusion.43
  20.5 0.1 slice.120
  20.6 0.0 collective-permute-done
  20.6 0.5 fusion.83
  21.1 0.0 collective-permute-done.1
  21.2 0.5 fusion.89
  21.6 2.3 reduce-precision_convert_fusion.5
  23.9 2.8 %fusion.57 = f32[2,520,256]{2,1,0:T(8,128)} fusion(bf16[520,1024]{1,0:T(8,128)(2,1)S(1)} %fusion.43, bf16[2,1024,256]{2,1,0:T(8,128)(2,1)S(1)} %get-tuple-element.37, bf16[2,1024,256]{2,1,0:T(8,128)(2,1)S(1)} %get-tuple-element.38, bf16[2,1024,256]{2,1,0:T(8,128)(2,1)S(1)} %get-tuple-element.36), kind=kOutput, calls=%fused_computation.86 | convolution fusion | flops 1654800384 | bytes 5275648 | tf_op jit(solution)/shard_map/ip,rpj->rij/dot_general | solution.py:74
  26.7 0.0 all-gather.3.cloned.1.call-update
  26.7 0.0 all-gather.5.cloned.1.call-start
  26.8 2.6 fusion.114
  29.4 0.4 fusion.64
  29.8 1.4 collective-permute-start.2
  31.1 46.1 %collective-permute-done.2 = f32[256,2048]{1,0:T(8,128)} collective-permute-done((f32[256,2048]{1,0:T(8,128)S(1)}, f32[256,2048]{1,0:T(8,128)}, u32[]{:S(2)}, u32[]{:S(2)}) %collective-permute-start.2) | collective-permute-done | bytes 2097184 | tf_op jit(solution)/shard_map/ppermute | solution.py:98
  77.3 3.4 %all-gather.3.cloned.1.call-done = f32[2,520,2048]{2,1,0:T(8,128)} async-done(((f32[2,520,256]{2,1,0:T(8,128)}), f32[2,520,2048]{2,1,0:T(8,128)}) %all-gather.3.cloned.1.call-update) | async-done | bytes 8519696 | tf_op jit(solution)/shard_map/all_gather | solution.py:113
  80.6 9.9 %fusion.11 = f32[2,520,512]{2,1,0:T(8,128)S(1)} fusion(f32[2,520,2048]{2,1,0:T(8,128)} %all-gather.3.cloned.1.call-done, f32[256,2048]{1,0:T(8,128)} %collective-permute-done.2, f32[256,2048]{1,0:T(8,128)S(1)} %get-tuple-element.15), kind=kOutput, calls=%fused_computation.21 | convolution fusion | flops 6544162816 | bytes 14843904 | tf_op jit(solution)/shard_map/rik,jk->rij/dot_general | solution.py:114
  90.6 0.1 slice.124
  90.7 1.3 collective-permute-start.3
  92.0 23.6 %collective-permute-done.3 = f32[2,520,256]{2,1,0:T(8,128)S(1)} collective-permute-done((f32[2,520,256]{2,1,0:T(8,128)S(1)}, f32[2,520,256]{2,1,0:T(8,128)S(1)}, u32[]{:S(2)}, u32[]{:S(2)}) %collective-permute-start.3) | collective-permute-done | bytes 1064992 | tf_op jit(solution)/shard_map/ppermute | solution.py:117
  115.7 1.3 slice_add_fusion
  116.9 0.0 all-gather.5.cloned.1.call-update
  116.9 1.0 fusion.113
  117.9 3.2 %collective-permute-start.4 = (f32[2,4096]{1,0:T(2,128)S(1)}, f32[2,4096]{1,0:T(2,128)S(1)}, u32[]{:S(2)}, u32[]{:S(2)}) collective-permute-start(f32[2,4096]{1,0:T(2,128)S(1)} %get-tuple-element.13), channel_id=1, source_target_pairs={{0,16},{16,32},{32,48},{48,64},{64,80},{80,96},{96,112},{1,17},{17... | collective-permute-start | bytes 98312 | tf_op jit(solution)/shard_map/ppermute | solution.py:19
  121.2 1.3 collective-permute-start.5
  122.5 2.3 fusion.46
  124.7 0.0 collective-permute-done.4
  124.7 1.1 collective-permute-done.5
  125.8 11.0 %select_maximum_fusion = f32[520,4104]{1,0:T(8,128)S(1)} fusion(f32[2,4096]{1,0:T(2,128)S(1)} %collective-permute-done.5, f32[512,4096]{1,0:T(8,128)} %param.6, f32[2,4096]{1,0:T(2,128)S(1)} %collective-permute-done.4), kind=kLoop, calls=%fused_computation.2 | loop fusion | flops 27743040 | bytes 16990464 | tf_op jit(solution)/shard_map/concatenate | solution.py:17
  136.8 3.4 %fusion.112 = (f32[520,520]{1,0:T(8,128)S(1)}, f32[520,520]{1,0:T(8,128)S(1)}, f32[520,520]{1,0:T(8,128)}, f32[520,520]{1,0:T(8,128)}, f32[520,520]{1,0:T(8,128)...) fusion(f32[520,4104]{1,0:T(8,128)S(1)} %select_maximum_fusion), kind=kLoop, calls=%fused_computation.159 | loop fusion | bytes 17305600 | tf_op jit(solution)/shard_map/slice | solution.py:79
  140.2 11.6 %concatenate.66 = f32[520,4160]{1,0:T(8,128)} concatenate(f32[520,520]{1,0:T(8,128)} %get-tuple-element.12, f32[520,520]{1,0:T(8,128)} %get-tuple-element.11, f32[520,520]{1,0:T(8,128)} %get-tuple-element.10, f32[520,520]{1,0:T(8,128)} %get-tuple-element.9, f32[520,520]{1,0:T(8,128)} %get-tuple-element.8, f32[520,520]{1,0:T(8,128)} %get-tuple-element.7, ...), dimensions={1} | concatenate | bytes 17305600 | tf_op jit(solution)/shard_map/concatenate | solution.py:79
  151.8 73.9 %all-gather.5.cloned.1.call-done = f32[2,4160,256]{2,1,0:T(8,128)} async-done(((f32[2,520,256]{2,1,0:T(8,128)}), f32[2,4160,256]{2,1,0:T(8,128)}) %all-gather.5.cloned.1.call-update) | async-done | bytes 8519696 | tf_op jit(solution)/shard_map/all_gather | solution.py:119
  225.8 12.2 %fusion.60 = f32[2,520,256]{2,1,0:T(8,128)S(1)} fusion(f32[2,4160,256]{2,1,0:T(8,128)} %all-gather.5.cloned.1.call-done, f32[520,4160]{1,0:T(8,128)} %concatenate.66), kind=kOutput, calls=%fused_computation.87 | convolution fusion | flops 6645350400 | bytes 18237440 | tf_op jit(solution)/shard_map/ik,rkj->rij/dot_general | solution.py:118
  238.0 0.2 fusion.116
  238.2 0.2 copy.10
  238.4 3.2 %collective-permute-start.6 = (f32[2,520,2]{1,2,0:T(2,128)S(1)}, f32[2,520,2]{1,2,0:T(2,128)S(1)}, u32[]{:S(2)}, u32[]{:S(2)}) collective-permute-start(f32[2,520,2]{1,2,0:T(2,128)S(1)} %copy.10), channel_id=1, source_target_pairs={{0,1},{1,2},{2,3},{3,4},{4,5},{5,6},{6,7},{7,8},{8,9},{9,10},{10,1... | collective-permute-start | bytes 24968 | tf_op jit(solution)/shard_map/ppermute | solution.py:19
  241.6 0.2 copy.11
  241.8 2.1 collective-permute-start.7
  244.0 0.4 fusion.75
  244.3 0.0 collective-permute-done.6
  244.4 0.2 copy.12
  244.6 2.2 collective-permute-done.7
  246.8 0.2 copy.13
  247.0 0.0 copy-start.1
  247.0 0.7 reduce-precision_convert_fusion.7
  247.8 0.5 copy-done.1
  248.3 0.0 copy-start
  248.3 0.0 copy-start.2
  248.3 2.5 reduce-precision_convert_fusion.3
  250.8 0.0 copy-done
  250.8 0.3 copy-done.2
  251.1 4.0 %multiply_add_fusion = f32[2,1024,512]{2,1,0:T(8,128)} fusion(f32[2,1024,512]{2,1,0:T(8,128)S(1)} %copy-done, f32[1024,512]{1,0:T(8,128)S(1)} %copy-done.2, bf16[2,1024,260]{1,2,0:T(8,128)(2,1)S(1)} %get-tuple-element.31, bf16[2,1024,260]{1,2,0:T(8,128)(2,1)S(1)} %get-tuple-element.32, bf16[2,1024,260]{1,2,0:T(8,128)(2,1)S(1)} %get-tuple-element.30, ...), kind=kOutput, calls=%fused_computation.24 | convolution fusion | flops 1649856512 | bytes 13946880 | tf_op jit(solution)/shard_map/rpj,jq->rpq/dot_general | solution.py:72
  (8 shorter events, 0.1 us)
Async XLA Ops:
  6.5 74.1 %all-gather.3.cloned.1.call-start = ((), (), s32[]{:S(2)}) async-start(), calls=%async_computation | async-start | bytes 9584640 | tf_op jit(solution)/shard_map/all_gather | solution.py:113
  8.8 11.8 %collective-permute-start = (f32[2,1024,4]{1,2,0:T(4,128)S(1)}, f32[2,1024,4]{1,2,0:T(4,128)S(1)}, u32[]{:S(2)}, u32[]{:S(2)}) collective-permute-start(f32[2,1024,4]{1,2,0:T(4,128)S(1)} %copy.16), channel_id=1, source_target_pairs={{0,1},{1,2},{2,3},{3,4},{4,5},{5,6},{6,7},{7,8},{8,9},{9,10},{10,1... | collective-permute-start | bytes 98312 | tf_op jit(solution)/shard_map/ppermute | solution.py:33
  13.7 7.4 %collective-permute-start.1 = (f32[2,1024,4]{1,2,0:T(4,128)S(1)}, f32[2,1024,4]{1,2,0:T(4,128)S(1)}, u32[]{:S(2)}, u32[]{:S(2)}) collective-permute-start(f32[2,1024,4]{1,2,0:T(4,128)S(1)} %copy.17), channel_id=1, source_target_pairs={{1,0},{2,1},{3,2},{4,3},{5,4},{6,5},{7,6},{8,7},{9,8},{10,9},{11,1... | collective-permute-start | bytes 98312 | tf_op jit(solution)/shard_map/ppermute | solution.py:34
  26.7 199.0 %all-gather.5.cloned.1.call-start = ((), (), s32[]{:S(2)}) async-start(), calls=%async_computation.1 | async-start | bytes 9584640 | tf_op jit(solution)/shard_map/all_gather | solution.py:119
  29.8 47.5 %collective-permute-start.2 = (f32[256,2048]{1,0:T(8,128)S(1)}, f32[256,2048]{1,0:T(8,128)}, u32[]{:S(2)}, u32[]{:S(2)}) collective-permute-start(f32[256,2048]{1,0:T(8,128)S(1)} %get-tuple-element.16), channel_id=1, source_target_pairs={{0,2},{2,0},{1,3},{3,1},{4,6},{6,4},{5,7},{7,5},{8,10},{10,8},{9,1... | collective-permute-start | bytes 6291464 | tf_op jit(solution)/shard_map/ppermute | solution.py:98
  90.7 24.9 %collective-permute-start.3 = (f32[2,520,256]{2,1,0:T(8,128)S(1)}, f32[2,520,256]{2,1,0:T(8,128)S(1)}, u32[]{:S(2)}, u32[]{:S(2)}) collective-permute-start(f32[2,520,256]{2,1,0:T(8,128)S(1)} %slice.124), channel_id=1, source_target_pairs={{0,2},{2,0},{1,3},{3,1},{4,6},{6,4},{5,7},{7,5},{8,10},{10,8},{9,1... | collective-permute-start | bytes 3194888 | tf_op jit(solution)/shard_map/ppermute | solution.py:117
  117.9 6.8 %collective-permute-start.4 = (f32[2,4096]{1,0:T(2,128)S(1)}, f32[2,4096]{1,0:T(2,128)S(1)}, u32[]{:S(2)}, u32[]{:S(2)}) collective-permute-start(f32[2,4096]{1,0:T(2,128)S(1)} %get-tuple-element.13), channel_id=1, source_target_pairs={{0,16},{16,32},{32,48},{48,64},{64,80},{80,96},{96,112},{1,17},{17... | collective-permute-start | bytes 98312 | tf_op jit(solution)/shard_map/ppermute | solution.py:19
  121.2 4.7 %collective-permute-start.5 = (f32[2,4096]{1,0:T(2,128)S(1)}, f32[2,4096]{1,0:T(2,128)S(1)}, u32[]{:S(2)}, u32[]{:S(2)}) collective-permute-start(f32[2,4096]{1,0:T(2,128)S(1)} %get-tuple-element.14), channel_id=1, source_target_pairs={{16,0},{32,16},{48,32},{64,48},{80,64},{96,80},{112,96},{17,1},{33... | collective-permute-start | bytes 98312 | tf_op jit(solution)/shard_map/ppermute | solution.py:21
  238.4 5.9 %collective-permute-start.6 = (f32[2,520,2]{1,2,0:T(2,128)S(1)}, f32[2,520,2]{1,2,0:T(2,128)S(1)}, u32[]{:S(2)}, u32[]{:S(2)}) collective-permute-start(f32[2,520,2]{1,2,0:T(2,128)S(1)} %copy.10), channel_id=1, source_target_pairs={{0,1},{1,2},{2,3},{3,4},{4,5},{5,6},{6,7},{7,8},{8,9},{9,10},{10,1... | collective-permute-start | bytes 24968 | tf_op jit(solution)/shard_map/ppermute | solution.py:19
  241.8 5.0 %collective-permute-start.7 = (f32[2,520,2]{1,2,0:T(2,128)S(1)}, f32[2,520,2]{1,2,0:T(2,128)S(1)}, u32[]{:S(2)}, u32[]{:S(2)}) collective-permute-start(f32[2,520,2]{1,2,0:T(2,128)S(1)} %copy.11), channel_id=1, source_target_pairs={{1,0},{2,1},{3,2},{4,3},{5,4},{6,5},{7,6},{8,7},{9,8},{10,9},{11,1... | collective-permute-start | bytes 24968 | tf_op jit(solution)/shard_map/ppermute | solution.py:21
  247.0 1.2 copy-start.1
  248.3 2.5 copy-start
  248.3 2.9 %copy-start.2 = (f32[1024,512]{1,0:T(8,128)S(1)}, f32[1024,512]{1,0:T(8,128)}, u32[]{:S(2)}) copy-start(f32[1024,512]{1,0:T(8,128)} %param.5) | copy-start | bytes 6291460
Sparse Core Ops, SparseCore 0:
  26.8 53.7 all-gather.2
  117.0 108.6 all-gather.4
